TPU v7x, 32 devices: a whole 2x2x4 slice. The times are simulated.
32 devices in a mesh: expert: 4 (over y, x), dp: 8 (over z, core).
Axes of the slice: x: 2, y: 2, z: 4, core: 2. Of those that a mesh axis runs over, the one named last changes fastest.
Arguments:
- out_grad: bfloat16 [4096, 2048], P(('expert', 'dp')), may hold values from -6 to 6
- combine_weight: float32 [4096, 2], P(('expert', 'dp')), may hold values from 0.02 to 0.5
- routes: int32 [4096, 2], P(('expert', 'dp')), may hold values from 0 to 3, all different within a row; in each aligned block of 128 rows (0 to 127, 128 to 255, ...) at most 96 rows name the same one
- saved_gate: bfloat16 [4, 8, 4, 96, 768], P('expert', 'dp'), may hold values from -6 to 6
- saved_up: bfloat16 [4, 8, 4, 96, 768], P('expert', 'dp'), may hold values from -6 to 6
- w_down: bfloat16 [4, 768, 2048], P('expert'), may hold values from -0.21875 to 0.21875
Outputs:
- grad_w_down: float32 [4, 768, 2048], P('expert', 'dp')
- grad_gate: bfloat16 [4, 8, 4, 96, 768], P('expert', 'dp')
- grad_up: bfloat16 [4, 8, 4, 96, 768], P('expert', 'dp')
- grad_combine: float32 [4096, 2], P(('expert', 'dp'))
Inputs may be any that keep to these rules, and one draw needn't show every extreme that they name: The routes of a token name different experts. In the rows of one device (aligned blocks of 128 tokens) no expert is named by more than 96 routes, and every expert is named somewhere.
All inputs are finite; a program needn't handle non-finite values.
Results may differ from a plain program's by a relative error of at most 0.015.
Values may be sent and summed in bfloat16 or wider, within the bound.
No kernel may reach another device: no remote copies, remote signals or barrier semaphores. Data moves between devices by JAX's collectives and lax.ppermute only.
A program may use at most 64 MiB of HBM per device.

v0:
```python
import jax
import jax.numpy as jnp
from jax import lax
from jax.sharding import PartitionSpec as P


def flat_lanes(term):
    lanes = 128
    return term.reshape(-1, lanes)


def local(out_grad, combine_weight, routes, saved_gate, saved_up, w_down):
    experts = lax.axis_size("expert")
    data_count = lax.axis_size("dp")
    tok_rows, route_count = routes.shape
    capacity = saved_gate.shape[3]
    hidden_count = saved_gate.shape[4]
    feature_count = out_grad.shape[1]
    share_rows = hidden_count // data_count
    flat_routes = routes.reshape(-1)
    onehot = (flat_routes[:, None] == jnp.arange(experts, dtype=jnp.int32)[None, :]).astype(
        jnp.int32
    )
    before = jnp.cumsum(onehot, axis=0) - onehot
    position = flat_routes * capacity + jnp.sum(before * onehot, axis=1)
    repeated = jnp.repeat(out_grad, route_count, axis=0)
    sent_rows = (
        jnp.zeros((experts * capacity, feature_count), out_grad.dtype).at[position].set(repeated)
    )
    sent_weight = (
        jnp.zeros((experts * capacity,), jnp.float32).at[position].set(combine_weight.reshape(-1))
    )
    rows_in, weight_in = (
        lax.all_to_all(
            sent_rows.reshape(experts, capacity, feature_count),
            "expert",
            split_axis=0,
            concat_axis=0,
            tiled=True,
        ),
        lax.all_to_all(
            sent_weight.reshape(experts, capacity).astype(jnp.bfloat16),
            "expert",
            split_axis=0,
            concat_axis=0,
            tiled=True,
        ).astype(jnp.float32),
    )
    rows = rows_in.reshape(experts * capacity, feature_count)
    weights = weight_in.reshape(-1)
    gate_pre = saved_gate.reshape(-1, hidden_count).astype(jnp.float32)
    up_pre = saved_up.reshape(-1, hidden_count).astype(jnp.float32)
    sigmoid_gate = jax.nn.sigmoid(gate_pre)
    hidden = (gate_pre * sigmoid_gate * up_pre).astype(jnp.bfloat16)
    weighted = (weights[:, None] * rows.astype(jnp.float32)).astype(jnp.bfloat16)
    matrix = w_down[0]
    contract_rows = (((0,), (0,)), ((), ()))
    partial_grad = lax.dot_general(
        hidden, weighted, contract_rows, preferred_element_type=jnp.float32
    )
    summed = lax.psum_scatter(flat_lanes(partial_grad), "dp", scatter_dimension=0, tiled=True)
    grad_weight = summed.reshape(share_rows, feature_count)
    back = lax.dot_general(
        rows, matrix, (((1,), (1,)), ((), ())), preferred_element_type=jnp.float32
    )
    grad_hidden = weights[:, None] * back
    grad_gate = (
        grad_hidden * up_pre * sigmoid_gate * (1.0 + gate_pre * (1.0 - sigmoid_gate))
    ).astype(jnp.bfloat16)
    grad_up = (grad_hidden * gate_pre * sigmoid_gate).astype(jnp.bfloat16)
    expert_out = jnp.dot(hidden, matrix, preferred_element_type=jnp.float32)
    slot_grad = jnp.sum(rows.astype(jnp.float32) * expert_out, axis=1)
    returned = lax.all_to_all(
        slot_grad.reshape(experts, capacity), "expert", split_axis=0, concat_axis=0, tiled=True
    )
    grad_combine = returned.reshape(-1)[position].reshape(tok_rows, route_count)
    return (
        grad_weight[None],
        grad_gate.reshape(saved_gate.shape),
        grad_up.reshape(saved_up.shape),
        grad_combine,
    )


def solution(mesh):
    in_specs = (
        P(("expert", "dp"), None),
        P(("expert", "dp"), None),
        P(("expert", "dp"), None),
        P("expert", "dp", None, None, None),
        P("expert", "dp", None, None, None),
        P("expert", None, None),
    )
    out_specs = (
        P("expert", "dp", None),
        P("expert", "dp", None, None, None),
        P("expert", "dp", None, None, None),
        P(("expert", "dp"), None),
    )
    return jax.shard_map(local, mesh=mesh, in_specs=in_specs, out_specs=out_specs, check_vma=False)
```

profile of v0, /device:TPU:0, one launch (start us, length us, event | category | flops | bytes accessed | tf_op | source)
XLA Modules:
  0.0 144.6 jit_solution(10766795179834258448)
XLA Ops:
  7.2 0.8 broadcast_multiply_fusion
  8.0 0.9 copy.27
  8.9 0.1 eq.29
  9.1 0.1 eq.25
  9.2 0.1 copy.26
  9.3 0.1 mul.71
  9.5 1.2 reduce-window.6
  11.1 0.8 copy.31
  11.9 0.1 reshape.150
  12.0 1.4 scatter_custom_fusion
  13.5 0.7 convert_element_type.108
  14.1 5.2 %all-to-all-start = ((bf16[4,1,96]{2,1,0:T(2,128)(2,1)}), bf16[4,1,96]{2,1,0:T(2,128)(2,1)S(1)}, u32[]{:S(2)}, u32[]{:S(2)}) async-start(bf16[4,1,96]{2,1,0:T(2,128)(2,1)} %convert_element_type.108), calls=%async_computation | async-start | bytes 4096 | tf_op jit(solution)/shard_map/all_to_all | solution.py:41
  19.3 2.7 %broadcast_in_dim.15 = bf16[128,2,2048]{2,1,0:T(2,128)(2,1)} broadcast(bf16[128,2048]{1,0:T(8,128)(2,1)} %param.6), dimensions={0,2} | broadcast | bytes 1572864 | tf_op jit(solution)/shard_map/broadcast_in_dim | solution.py:26
  22.0 2.2 %reshape.158 = bf16[256,2048]{1,0:T(8,128)(2,1)} reshape(bf16[128,2,2048]{2,1,0:T(2,128)(2,1)} %broadcast_in_dim.15) | data formatting | bytes 2097152 | tf_op jit(solution)/shard_map/reshape | solution.py:26
  24.2 4.1 %scatter_custom_fusion.1 = bf16[384,2048]{1,0:T(8,128)(2,1)} fusion(s32[256]{0:T(256)S(1)} %bitcast.81, bf16[256,2048]{1,0:T(8,128)(2,1)} %reshape.158, bf16[]{:T(256)} %constant.5.clone.1), kind=kCustom, calls=%fused_computation.30 | custom fusion | bytes 1573376 | tf_op jit(solution)/shard_map/scatter | solution.py:28
  28.3 4.4 %all-to-all-start.1 = ((bf16[4,96,2048]{2,1,0:T(8,128)(2,1)}), bf16[4,96,2048]{2,1,0:T(8,128)(2,1)}, u32[]{:S(2)}, u32[]{:S(2)}) async-start(bf16[4,96,2048]{2,1,0:T(8,128)(2,1)} %bitcast.75), calls=%async_computation.1 | async-start | bytes 3145728 | tf_op jit(solution)/shard_map/all_to_all | solution.py:34
  32.7 2.4 %fusion.22 = bf16[1,1,4,96,768]{4,3,2,1,0:T(8,128)(2,1)} fusion(bf16[1,1,4,96,768]{4,3,2,1,0:T(8,128)(2,1)} %param.9, bf16[1,1,4,96,768]{4,3,2,1,0:T(8,128)(2,1)} %param.10), kind=kLoop, calls=%fused_computation.29 | loop fusion | flops 2359296 | bytes 1769472 | tf_op jit(solution)/shard_map/convert_element_type | solution.py:54
  35.2 16.8 %all-to-all-done.1 = bf16[4,96,2048]{2,1,0:T(8,128)(2,1)} async-done(((bf16[4,96,2048]{2,1,0:T(8,128)(2,1)}), bf16[4,96,2048]{2,1,0:T(8,128)(2,1)}, u32[]{:S(2)}, u32[]{:S(2)}) %all-to-all-start.1) | async-done | bytes 1572896 | tf_op jit(solution)/shard_map/all_to_all | solution.py:34
  52.0 1.8 %multiply_convert_fusion = bf16[4,96,2048]{2,1,0:T(8,128)(2,1)S(1)} fusion(bf16[4,96,2048]{2,1,0:T(8,128)(2,1)} %all-to-all-done.1, f32[4,96]{1,0:T(4,128)S(1)} %bitcast.79), kind=kLoop, calls=%fused_computation.8 | loop fusion | flops 2359296 | bytes 3147264 | tf_op jit(solution)/shard_map/convert_element_type | solution.py:55
  53.8 4.5 %fusion.30 = f32[768,2048]{1,0:T(8,128)} fusion(bf16[384,768]{1,0:T(8,128)(2,1)S(1)} %bitcast.78, bf16[384,2048]{1,0:T(8,128)(2,1)S(1)} %bitcast.76), kind=kOutput, calls=%fused_computation.45 | convolution fusion | flops 1207959552 | bytes 8454144 | tf_op jit(solution)/shard_map/dot_general | solution.py:58
  58.3 7.1 %reshape.128 = f32[12288,128]{1,0:T(8,128)} reshape(f32[768,2048]{1,0:T(8,128)} %fusion.30) | data formatting | bytes 12582912 | tf_op jit(solution)/shard_map/reshape | solution.py:9
  65.6 3.1 %multiply_reduce_fusion = f32[384]{0:T(512)S(1)} fusion(bf16[384,2048]{1,0:T(8,128)(2,1)} %bitcast.8, bf16[384,768]{1,0:T(8,128)(2,1)} %bitcast.77, bf16[1,768,2048]{2,1,0:T(8,128)(2,1)S(1)} %copy-done), kind=kOutput, calls=%fused_computation.7 | convolution fusion | flops 1210318464 | bytes 5309952 | tf_op jit(solution)/shard_map/dot_general | solution.py:71
  68.6 0.7 all_to_all.15
  69.3 3.2 %all-to-all-start.2 = ((f32[4,1,96]{2,1,0:T(1,128)}), f32[4,1,96]{2,1,0:T(1,128)S(1)}, u32[]{:S(2)}, u32[]{:S(2)}) async-start(f32[4,1,96]{2,1,0:T(1,128)} %all_to_all.15), calls=%async_computation.3 | async-start | bytes 4096 | tf_op jit(solution)/shard_map/all_to_all | solution.py:73
  72.5 4.5 %fusion.20 = (bf16[384,768]{1,0:T(8,128)(2,1)}, bf16[384,768]{1,0:T(8,128)(2,1)}) fusion(bf16[1,1,4,96,768]{4,3,2,1,0:T(8,128)(2,1)} %param.9, bf16[1,1,4,96,768]{4,3,2,1,0:T(8,128)(2,1)} %param.10, bf16[384,2048]{1,0:T(8,128)(2,1)} %bitcast.8, bf16[1,768,2048]{2,1,0:T(8,128)(2,1)S(1)} %copy-done, f32[384]{0:T(512)S(1)} %reshape.135), kind=kOutput, calls=%fused_computation.26 | convolution fusion | flops 1212678144 | bytes 7079424 | tf_op jit(solution)/shard_map/dot_general | solution.py:63
  77.1 0.5 broadcast.77
  77.6 0.7 reduce.7
  78.3 1.9 %gather_fusion = f32[256]{0:T(256)S(1)} fusion(f32[384]{0:T(512)S(1)} %reshape.132, s32[1024]{0:T(1024)S(1)} %pad_clamp_fusion), kind=kCustom, calls=%fused_computation | custom fusion | bytes 3072 | tf_op jit(solution)/shard_map/gather | solution.py:76
  80.3 0.1 reshape.133
  80.4 0.6 copy.33
  81.1 54.6 %reduce-scatter.2.cloned.1.call-done = f32[1536,128]{1,0:T(8,128)} async-done(((f32[12288,128]{1,0:T(8,128)}), f32[1536,128]{1,0:T(8,128)}) %reduce-scatter.2.cloned.1.call-update) | async-done | bytes 786448 | tf_op jit(solution)/shard_map/reduce_scatter | solution.py:61
  135.7 2.1 %broadcast_in_dim_reshape.2 = f32[1,96,2048]{2,1,0:T(8,128)} reshape(f32[1536,128]{1,0:T(8,128)} %reduce-scatter.2.cloned.1.call-done) | data formatting | bytes 1572864 | tf_op jit(solution)/shard_map/broadcast_in_dim;reshape | solution.py:78
  (23 shorter events, 0.7 us)
Async XLA Ops:
  7.2 58.4 %copy-start = (bf16[1,768,2048]{2,1,0:T(8,128)(2,1)S(1)}, bf16[1,768,2048]{2,1,0:T(8,128)(2,1)}, u32[]{:S(2)}) copy-start(bf16[1,768,2048]{2,1,0:T(8,128)(2,1)} %param.11) | copy-start | bytes 9437188
  14.1 14.2 %all-to-all-start = ((bf16[4,1,96]{2,1,0:T(2,128)(2,1)}), bf16[4,1,96]{2,1,0:T(2,128)(2,1)S(1)}, u32[]{:S(2)}, u32[]{:S(2)}) async-start(bf16[4,1,96]{2,1,0:T(2,128)(2,1)} %convert_element_type.108), calls=%async_computation | async-start | bytes 4096 | tf_op jit(solution)/shard_map/all_to_all | solution.py:41
  28.3 23.7 %all-to-all-start.1 = ((bf16[4,96,2048]{2,1,0:T(8,128)(2,1)}), bf16[4,96,2048]{2,1,0:T(8,128)(2,1)}, u32[]{:S(2)}, u32[]{:S(2)}) async-start(bf16[4,96,2048]{2,1,0:T(8,128)(2,1)} %bitcast.75), calls=%async_computation.1 | async-start | bytes 3145728 | tf_op jit(solution)/shard_map/all_to_all | solution.py:34
  32.7 103.0 %reduce-scatter.2.cloned.1.call-start = ((), (), s32[]{:S(2)}) async-start(), calls=%async_computation.4 | async-start | bytes 7077888 | tf_op jit(solution)/shard_map/reduce_scatter | solution.py:61
  52.0 1.8 %copy-start.1 = (bf16[1,1,4,96,768]{4,3,2,1,0:T(8,128)(2,1)S(1)}, bf16[1,1,4,96,768]{4,3,2,1,0:T(8,128)(2,1)}, u32[]{:S(2)}) copy-start(bf16[1,1,4,96,768]{4,3,2,1,0:T(8,128)(2,1)} %fusion.22) | copy-start | bytes 1769476
  69.3 7.8 %all-to-all-start.2 = ((f32[4,1,96]{2,1,0:T(1,128)}), f32[4,1,96]{2,1,0:T(1,128)S(1)}, u32[]{:S(2)}, u32[]{:S(2)}) async-start(f32[4,1,96]{2,1,0:T(1,128)} %all_to_all.15), calls=%async_computation.3 | async-start | bytes 4096 | tf_op jit(solution)/shard_map/all_to_all | solution.py:73
Sparse Core Ops, SparseCore 0:
  65.6 70.0 reduce-scatter.1
where the time goes:
time: 145 us
  waiting for transfers between devices  71.5 us (49%)
  local copies, waits for them, and re-layouts  27 us (19%)
  between operations  14.1 us (10%)
  starting transfers between devices  12.8 us (9%)
  matrix products  12.1 us (8%)
  other arithmetic  7.11 us (5%)
    reduce_scatter x1, waiting for transfers between devices, local(): lax.psum_scatter(flat_lanes(partial_grad), 'dp', scatter_dimension=0, til...  54.6 us
    all_to_all x1, waiting for transfers between devices, local(): lax.all_to_all(sent_rows.reshape(experts, capacity, feature_count), 'expe...  16.8 us
    reshape x1, local copies, waits for them, and re-layouts, flat_lanes(): return term.reshape(-1, lanes)  7.09 us
    all_to_all x1, starting transfers between devices, local(): lax.all_to_all(sent_weight.reshape(experts, capacity).astype(jnp.bfloat16...  5.16 us
    dot_general x1, matrix products, local(): lax.dot_general(rows, matrix, (((1,), (1,)), ((), ())), preferred_element...  4.54 us
    dot_general x1, matrix products, local(): lax.dot_general(hidden, weighted, contract_rows, preferred_element_type=j...  4.49 us
    all_to_all x1, starting transfers between devices, local(): lax.all_to_all(sent_rows.reshape(experts, capacity, feature_count), 'expe...  4.37 us
    scatter x1, local copies, waits for them, and re-layouts, local(): jnp.zeros((experts * capacity, feature_count), out_grad.dtype).at[position]  4.11 us
  transfers between devices with their start and end apart: 4, of which 2 were waited for; matrix products, arithmetic and copies ran while one was open for 16% of the time, Pallas kernels for 0%

commit v1 on v0

v1 whole, which is shorter than its diff:
```python
import jax
import jax.numpy as jnp
from jax import lax
from jax.sharding import PartitionSpec as P


def round_bf16(value):
    return lax.reduce_precision(value, exponent_bits=8, mantissa_bits=7)


def weight_pieces(weights):
    high = round_bf16(weights)
    rest = weights - high
    middle = round_bf16(rest)
    low = rest - middle
    return jnp.stack([high, middle, low], axis=-1).astype(jnp.bfloat16)


def local(out_grad, combine_weight, routes, saved_gate, saved_up, w_down):
    experts = lax.axis_size("expert")
    tok_rows, route_count = routes.shape
    capacity = saved_gate.shape[3]
    hidden_count = saved_gate.shape[4]
    feature_count = out_grad.shape[1]
    slots = experts * capacity
    lanes = 128

    flat_routes = routes.reshape(-1)
    route_total = flat_routes.shape[0]
    onehot = (flat_routes[:, None] == jnp.arange(experts, dtype=jnp.int32)[None, :]).astype(
        jnp.float32
    )
    order = jnp.arange(route_total, dtype=jnp.int32)
    earlier = (order[None, :] < order[:, None]).astype(jnp.bfloat16)
    before = jnp.dot(earlier, onehot.astype(jnp.bfloat16), preferred_element_type=jnp.float32)
    slot = jnp.sum(before * onehot, axis=1).astype(jnp.int32)
    position = flat_routes * capacity + slot

    slot_ids = jnp.arange(slots, dtype=jnp.int32)
    pick_route = position[None, :] == slot_ids[:, None]
    pick_token = pick_route.reshape(slots, tok_rows, route_count).any(axis=2)
    sent_rows = jnp.dot(
        pick_token.astype(out_grad.dtype), out_grad, preferred_element_type=jnp.float32
    ).astype(out_grad.dtype)
    pieces = weight_pieces(combine_weight.reshape(-1))
    pieces = jnp.pad(pieces, ((0, 0), (0, lanes - pieces.shape[1])))
    sent_pieces = jnp.dot(
        pick_route.astype(jnp.bfloat16), pieces, preferred_element_type=jnp.float32
    ).astype(jnp.bfloat16)
    packed = jnp.concatenate([sent_rows, sent_pieces], axis=1)
    arrived = lax.all_to_all(
        packed.reshape(experts, capacity, feature_count + lanes),
        "expert",
        split_axis=0,
        concat_axis=0,
        tiled=True,
    ).reshape(slots, feature_count + lanes)
    rows = arrived[:, :feature_count]
    got = arrived[:, feature_count:feature_count + 3].astype(jnp.float32)
    weights = (got[:, 0] + got[:, 1]) + got[:, 2]

    gate_pre = saved_gate.reshape(-1, hidden_count).astype(jnp.float32)
    up_pre = saved_up.reshape(-1, hidden_count).astype(jnp.float32)
    sigmoid_gate = jax.nn.sigmoid(gate_pre)
    hidden = (gate_pre * sigmoid_gate * up_pre).astype(jnp.bfloat16)
    weighted = (weights[:, None] * rows.astype(jnp.float32)).astype(jnp.bfloat16)
    partial_grad = lax.dot_general(
        hidden, weighted, (((0,), (0,)), ((), ())), preferred_element_type=jnp.float32
    )
    summed = lax.psum_scatter(
        partial_grad.astype(jnp.bfloat16), "dp", scatter_dimension=0, tiled=True
    )
    grad_weight = summed.astype(jnp.float32)

    matrix = w_down[0]
    back = lax.dot_general(
        rows, matrix, (((1,), (1,)), ((), ())), preferred_element_type=jnp.float32
    )
    grad_hidden = weights[:, None] * back
    grad_gate = (
        grad_hidden * up_pre * sigmoid_gate * (1.0 + gate_pre * (1.0 - sigmoid_gate))
    ).astype(jnp.bfloat16)
    grad_up = (grad_hidden * gate_pre * sigmoid_gate).astype(jnp.bfloat16)
    slot_grad = jnp.sum(hidden.astype(jnp.float32) * back, axis=1)
    returned = lax.all_to_all(
        slot_grad.reshape(experts, capacity), "expert", split_axis=0, concat_axis=0, tiled=True
    )
    grad_combine = returned.reshape(-1)[position].reshape(tok_rows, route_count)
    return (
        grad_weight[None],
        grad_gate.reshape(saved_gate.shape),
        grad_up.reshape(saved_up.shape),
        grad_combine,
    )


def solution(mesh):
    in_specs = (
        P(("expert", "dp"), None),
        P(("expert", "dp"), None),
        P(("expert", "dp"), None),
        P("expert", "dp", None, None, None),
        P("expert", "dp", None, None, None),
        P("expert", None, None),
    )
    out_specs = (
        P("expert", "dp", None),
        P("expert", "dp", None, None, None),
        P("expert", "dp", None, None, None),
        P(("expert", "dp"), None),
    )
    return jax.shard_map(local, mesh=mesh, in_specs=in_specs, out_specs=out_specs, check_vma=False)
```

time: 145 us -> 93.9 us (0.65)
  waiting for transfers between devices: 71.5 us -> 32.1 us
  blocking collectives: 0 us -> 26 us
  local copies, waits for them, and re-layouts: 27 us -> 6.32 us
  starting transfers between devices: 12.8 us -> 3.26 us
  other arithmetic: 7.11 us -> 3.13 us
  matrix products: 12.1 us -> 8.54 us
    reduce_scatter x1, waiting for transfers between devices: 54.6 us -> 27.6 us  [local(): lax.psum_scatter(partial_grad.astype(jnp.bfloat16), 'dp', scatter_dimensi...]
    all_to_all x0 -> x1, blocking collectives: none -> 26 us  [local(): lax.all_to_all(packed.reshape(experts, capacity, feature_count + lanes),...]
    all_to_all x2 -> x0, waiting for transfers between devices: 16.9 us -> none  [the longest x1 16.8 us: local(): lax.all_to_all(sent_rows.reshape(experts, capacity, feature_count), 'expe...]
    all_to_all x2 -> x0, starting transfers between devices: 9.53 us -> none  [the longest x1 5.16 us: local(): lax.all_to_all(sent_weight.reshape(experts, capacity).astype(jnp.bfloat16...]
    reshape x3 -> x1, local copies, waits for them, and re-layouts: 9.47 us -> 0.14 us  [local(): pieces = weight_pieces(combine_weight.reshape(-1))]
    scatter x2 -> x0, local copies, waits for them, and re-layouts: 5.51 us -> none  [the longest x1 4.11 us: local(): jnp.zeros((experts * capacity, feature_count), out_grad.dtype).at[position]]
    all_to_all x1, waiting for transfers between devices: 0.01 us -> 4.52 us  [local(): lax.all_to_all(slot_grad.reshape(experts, capacity), 'expert', split_axis...]
    convert_element_type x6 -> x2, other arithmetic: 4.24 us -> 0.02 us  [the longest x1 0.01 us: local(): got = arrived[:, feature_count:feature_count + 3].astype(jnp.float32)]
  transfers between devices with their start and end apart: 4 -> 2, of which waited for: 2 -> 2; matrix products, arithmetic and copies ran while one was open for 16% -> 4% of each run, Pallas kernels for 0% -> 0%
where the time goes in v1:
time: 93.9 us; the launch traced here: 93.5 us
  waiting for transfers between devices  32.1 us (34%)
  blocking collectives  26 us (28%)
  between operations  14.2 us (15%)
  matrix products  8.54 us (9%)
  local copies, waits for them, and re-layouts  6.32 us (7%)
  starting transfers between devices  3.26 us (3%)
  other arithmetic  3.13 us (3%)
    reduce_scatter x1, waiting for transfers between devices, local(): lax.psum_scatter(partial_grad.astype(jnp.bfloat16), 'dp', scatter_dimensi...  27.6 us
    all_to_all x1, blocking collectives, local(): lax.all_to_all(packed.reshape(experts, capacity, feature_count + lanes),...  26 us
    all_to_all x1, waiting for transfers between devices, local(): lax.all_to_all(slot_grad.reshape(experts, capacity), 'expert', split_axis...  4.52 us
    dot_general x1, matrix products, local(): lax.dot_general(hidden, weighted, (((0,), (0,)), ((), ())), preferred_ele...  3.57 us
    all_to_all x1, starting transfers between devices, local(): lax.all_to_all(slot_grad.reshape(experts, capacity), 'expert', split_axis...  3.22 us
    dot_general x1, matrix products, local(): lax.dot_general(rows, matrix, (((1,), (1,)), ((), ())), preferred_element...  2.98 us
    unnamed x9, local copies, waits for them, and re-layouts  2.38 us
    gather x1, local copies, waits for them, and re-layouts, local(): grad_combine = returned.reshape(-1)[position].reshape(tok_rows, route_count)  1.94 us
  transfers between devices with their start and end apart: 2, of which 2 were waited for; matrix products, arithmetic and copies ran while one was open for 4% of the time, Pallas kernels for 0%

profile of v1, /device:TPU:0, one launch (start us, length us, event | category | flops | bytes accessed | tf_op | source)
XLA Modules:
  0.0 93.5 jit_solution(6056065932511979873)
XLA Ops:
  7.2 0.0 copy-start
  7.2 0.0 reduce-scatter.2.cloned.1.call-start
  7.2 0.9 %copy.23 = s32[128,2]{1,0:T(8,128)S(1)} copy(s32[128,2]{0,1:T(2,128)} %param.8) | data formatting | bytes 2048 | tf_op args[2]
  8.2 0.1 eq.35
  8.3 0.2 fusion.15
  8.5 0.1 convert_element_type.84
  8.7 0.1 copy.25
  8.8 0.1 fusion.16
  8.8 0.8 copy.26
  9.6 0.1 reshape.130
  9.8 1.6 %convolution_convert_fusion.1 = bf16[384,2048]{1,0:T(8,128)(2,1)S(1)} fusion(pred[384,128]{1,0:T(8,128)(4,1)S(1)} %fusion.16, bf16[128,2048]{1,0:T(8,128)(2,1)} %param.6), kind=kOutput, calls=%fused_computation.5 | convolution fusion | flops 202113024 | bytes 2146304 | tf_op jit(solution)/shard_map/dot_general | solution.py:42
  11.4 0.2 convolution_convert_fusion.2
  11.6 0.1 pad_maximum_fusion
  11.7 0.0 copy-start.1
  11.7 0.0 copy-start.2
  11.8 26.0 %all_to_all.14 = bf16[4,96,2176]{2,1,0:T(8,128)(2,1)S(1)} all-to-all(bf16[4,96,2176]{2,1,0:T(8,128)(2,1)S(1)} %bitcast.28), channel_id=1, replica_groups=mesh['expert'=4,'dp'=8] {'expert'}, dimensions={0} | all-to-all | bytes 3342336 | tf_op jit(solution)/shard_map/all_to_all | solution.py:51
  37.8 0.3 fusion.17
  38.0 3.0 %multiply_reduce_fusion = (f32[384]{0:T(512)S(1)}, bf16[384,768]{1,0:T(8,128)(2,1)S(1)}, bf16[384,768]{1,0:T(8,128)(2,1)}, bf16[384,768]{1,0:T(8,128)(2,1)}) fusion(bf16[1,1,4,96,768]{4,3,2,1,0:T(8,128)(2,1)S(1)} %copy-done.1, bf16[1,1,4,96,768]{4,3,2,1,0:T(8,128)(2,1)S(1)} %copy-done.2, f32[384]{0:T(512)S(1)} %fusion.17, ...), kind=kOutput, calls=%fused_computation.26 | convolution fusion | flops 1214447232 | bytes 7671296 | tf_op jit(solution)/shard_map/dot_general | solution.py:76
  41.0 3.6 %convolution_convert_fusion = bf16[768,2048]{1,0:T(8,128)(2,1)} fusion(bf16[384,768]{1,0:T(8,128)(2,1)S(1)} %get-tuple-element.17, f32[384]{0:T(512)S(1)} %fusion.17, bf16[384,2176]{1,0:T(8,128)(2,1)S(1)} %bitcast.31), kind=kOutput, calls=%fused_computation.1 | convolution fusion | flops 1211891712 | bytes 5310464 | tf_op jit(solution)/shard_map/dot_general | solution.py:67
  44.6 0.0 reduce-scatter.2.cloned.1.call-update
  44.6 0.1 mul.92
  44.8 0.7 all_to_all.10
  45.4 3.2 %all-to-all-start.1 = ((f32[4,1,96]{2,1,0:T(1,128)}), f32[4,1,96]{2,1,0:T(1,128)S(1)}, u32[]{:S(2)}, u32[]{:S(2)}) async-start(f32[4,1,96]{2,1,0:T(1,128)} %all_to_all.10), calls=%async_computation.2 | async-start | bytes 4096 | tf_op jit(solution)/shard_map/all_to_all | solution.py:85
  48.7 4.5 %all-to-all-done.1 = f32[4,1,96]{2,1,0:T(1,128)S(1)} async-done(((f32[4,1,96]{2,1,0:T(1,128)}), f32[4,1,96]{2,1,0:T(1,128)S(1)}, u32[]{:S(2)}, u32[]{:S(2)}) %all-to-all-start.1) | async-done | bytes 1568 | tf_op jit(solution)/shard_map/all_to_all | solution.py:85
  53.2 0.5 broadcast.69
  53.7 0.7 reduce.5
  54.4 0.1 reshape.135
  54.5 1.9 %gather_fusion = f32[256]{0:T(256)S(1)} fusion(f32[384]{0:T(512)S(1)} %reshape.135, s32[1024]{0:T(1024)S(1)} %pad_clamp_fusion), kind=kCustom, calls=%fused_computation | custom fusion | bytes 3072 | tf_op jit(solution)/shard_map/gather | solution.py:88
  56.4 0.1 reshape.136
  56.6 0.6 copy.28
  57.2 27.6 %reduce-scatter.2.cloned.1.call-done = bf16[96,2048]{1,0:T(8,128)(2,1)} async-done(((bf16[768,2048]{1,0:T(8,128)(2,1)}), bf16[96,2048]{1,0:T(8,128)(2,1)}) %reduce-scatter.2.cloned.1.call-update) | async-done | bytes 393232 | tf_op jit(solution)/shard_map/reduce_scatter | solution.py:70
  84.7 1.9 %bitcast_convert_fusion = f32[1,96,2048]{2,1,0:T(8,128)} fusion(bf16[96,2048]{1,0:T(8,128)(2,1)} %reduce-scatter.2.cloned.1.call-done), kind=kLoop, calls=%fused_computation.30 | loop fusion | flops 196608 | bytes 1179648 | tf_op jit(solution)/shard_map/broadcast_in_dim | solution.py:90
  (10 shorter events, 0.1 us)
Async XLA Ops:
  7.2 30.9 %copy-start = (bf16[1,768,2048]{2,1,0:T(8,128)(2,1)S(1)}, bf16[1,768,2048]{2,1,0:T(8,128)(2,1)}, u32[]{:S(2)}) copy-start(bf16[1,768,2048]{2,1,0:T(8,128)(2,1)} %param.11) | copy-start | bytes 9437188
  7.2 77.6 %reduce-scatter.2.cloned.1.call-start = ((), (), s32[]{:S(2)}) async-start(), calls=%async_computation.3 | async-start | bytes 3538944 | tf_op jit(solution)/shard_map/reduce_scatter | solution.py:70
  11.7 26.3 %copy-start.1 = (bf16[1,1,4,96,768]{4,3,2,1,0:T(8,128)(2,1)S(1)}, bf16[1,1,4,96,768]{4,3,2,1,0:T(8,128)(2,1)}, u32[]{:S(2)}) copy-start(bf16[1,1,4,96,768]{4,3,2,1,0:T(8,128)(2,1)} %param.10) | copy-start | bytes 1769476
  11.7 26.3 %copy-start.2 = (bf16[1,1,4,96,768]{4,3,2,1,0:T(8,128)(2,1)S(1)}, bf16[1,1,4,96,768]{4,3,2,1,0:T(8,128)(2,1)}, u32[]{:S(2)}) copy-start(bf16[1,1,4,96,768]{4,3,2,1,0:T(8,128)(2,1)} %param.9) | copy-start | bytes 1769476
  45.4 7.8 %all-to-all-start.1 = ((f32[4,1,96]{2,1,0:T(1,128)}), f32[4,1,96]{2,1,0:T(1,128)S(1)}, u32[]{:S(2)}, u32[]{:S(2)}) async-start(f32[4,1,96]{2,1,0:T(1,128)} %all_to_all.10), calls=%async_computation.2 | async-start | bytes 4096 | tf_op jit(solution)/shard_map/all_to_all | solution.py:85
Sparse Core Ops, SparseCore 0:
  44.7 39.9 reduce-scatter.1

commit v2 on v1

--- a/solution.py
+++ b/solution.py
@@ -2,6 +2,9 @@
 import jax.numpy as jnp
 from jax import lax
 from jax.sharding import PartitionSpec as P
+
+
+CHUNKS = 4
 
 
 def round_bf16(value):
@@ -39,38 +42,58 @@
     slot_ids = jnp.arange(slots, dtype=jnp.int32)
     pick_route = position[None, :] == slot_ids[:, None]
     pick_token = pick_route.reshape(slots, tok_rows, route_count).any(axis=2)
-    sent_rows = jnp.dot(
-        pick_token.astype(out_grad.dtype), out_grad, preferred_element_type=jnp.float32
-    ).astype(out_grad.dtype)
     pieces = weight_pieces(combine_weight.reshape(-1))
     pieces = jnp.pad(pieces, ((0, 0), (0, lanes - pieces.shape[1])))
     sent_pieces = jnp.dot(
         pick_route.astype(jnp.bfloat16), pieces, preferred_element_type=jnp.float32
     ).astype(jnp.bfloat16)
-    packed = jnp.concatenate([sent_rows, sent_pieces], axis=1)
-    arrived = lax.all_to_all(
-        packed.reshape(experts, capacity, feature_count + lanes),
-        "expert",
-        split_axis=0,
-        concat_axis=0,
-        tiled=True,
-    ).reshape(slots, feature_count + lanes)
-    rows = arrived[:, :feature_count]
-    got = arrived[:, feature_count:feature_count + 3].astype(jnp.float32)
-    weights = (got[:, 0] + got[:, 1]) + got[:, 2]
 
     gate_pre = saved_gate.reshape(-1, hidden_count).astype(jnp.float32)
     up_pre = saved_up.reshape(-1, hidden_count).astype(jnp.float32)
     sigmoid_gate = jax.nn.sigmoid(gate_pre)
     hidden = (gate_pre * sigmoid_gate * up_pre).astype(jnp.bfloat16)
-    weighted = (weights[:, None] * rows.astype(jnp.float32)).astype(jnp.bfloat16)
-    partial_grad = lax.dot_general(
-        hidden, weighted, (((0,), (0,)), ((), ())), preferred_element_type=jnp.float32
-    )
-    summed = lax.psum_scatter(
-        partial_grad.astype(jnp.bfloat16), "dp", scatter_dimension=0, tiled=True
-    )
-    grad_weight = summed.astype(jnp.float32)
+
+    def exchange(block):
+        width = block.shape[1]
+        return lax.all_to_all(
+            block.reshape(experts, capacity, width), "expert",
+            split_axis=0, concat_axis=0, tiled=True,
+        ).reshape(slots, width)
+
+    chunks = CHUNKS if feature_count % (CHUNKS * lanes) == 0 else 1
+    width = feature_count // chunks
+    row_parts, grad_parts = [], []
+    weights = None
+    pick_rows = pick_token.astype(out_grad.dtype)
+    sends = [
+        jnp.dot(
+            pick_rows, out_grad[:, part * width:(part + 1) * width],
+            preferred_element_type=jnp.float32,
+        ).astype(out_grad.dtype)
+        for part in range(chunks)
+    ]
+    sends[0] = jnp.concatenate([sends[0], sent_pieces], axis=1)
+    for part in range(chunks):
+        arrived = exchange(sends[part])
+        if part == 0:
+            rows_part = arrived[:, :width]
+            got = arrived[:, width:width + 3].astype(jnp.float32)
+            weights = (got[:, 0] + got[:, 1]) + got[:, 2]
+        else:
+            rows_part = arrived
+        weighted = (weights[:, None] * rows_part.astype(jnp.float32)).astype(jnp.bfloat16)
+        partial_grad = lax.dot_general(
+            hidden, weighted, (((0,), (0,)), ((), ())), preferred_element_type=jnp.float32
+        ).astype(jnp.bfloat16)
+        if part + 1 < chunks:
+            partial_grad, sends[part + 1] = lax.optimization_barrier(
+                (partial_grad, sends[part + 1])
+            )
+        summed = lax.psum_scatter(partial_grad, "dp", scatter_dimension=0, tiled=True)
+        row_parts.append(rows_part)
+        grad_parts.append(summed.astype(jnp.float32))
+    rows = jnp.concatenate(row_parts, axis=1) if chunks > 1 else row_parts[0]
+    grad_weight = jnp.concatenate(grad_parts, axis=1) if chunks > 1 else grad_parts[0]
 
     matrix = w_down[0]
     back = lax.dot_general(

time: 93.9 us -> 168 us (1.79)
  waiting for transfers between devices: 32.1 us -> 85.5 us
  blocking collectives: 26 us -> 10 us
  starting transfers between devices: 3.26 us -> 16 us
  matrix products: 8.54 us -> 21.2 us
  other arithmetic: 3.13 us -> 11.7 us
  local copies, waits for them, and re-layouts: 6.32 us -> 9.03 us
    reduce_scatter x1 -> x4, waiting for transfers between devices: 27.6 us -> 71.4 us  [local(): lax.psum_scatter(partial_grad, 'dp', scatter_dimension=0, tiled=True)]
    all_to_all x1, blocking collectives: 26 us -> 10 us  [exchange(): lax.all_to_all(block.reshape(experts, capacity, width), 'expert', split_a...]
    all_to_all x0 -> x3, starting transfers between devices: none -> 12.8 us  [exchange(): lax.all_to_all(block.reshape(experts, capacity, width), 'expert', split_a...]
    all_to_all x0 -> x3, waiting for transfers between devices: none -> 9.42 us  [exchange(): lax.all_to_all(block.reshape(experts, capacity, width), 'expert', split_a...]
    convert_element_type x1 -> x6, other arithmetic: 0.01 us -> 7.19 us  [the longest x2 4.87 us: local(): hidden = (gate_pre * sigmoid_gate * up_pre).astype(jnp.bfloat16)]
    dot_general x1 -> x4, matrix products: 3.57 us -> 9.33 us  [local(): lax.dot_general(hidden, weighted, (((0,), (0,)), ((), ())), preferred_ele...]
    dot_general x1 -> x4, matrix products: 1.6 us -> 6.92 us  [local(): jnp.dot(pick_rows, out_grad[:, part * width:(part + 1) * width], preferre...]
  transfers between devices with their start and end apart: 2 -> 8, of which waited for: 2 -> 7; matrix products, arithmetic and copies ran while one was open for 4% -> 18% of each run, Pallas kernels for 0% -> 0%
where the time goes in v2:
time: 168 us; the launch traced here: 167 us
  waiting for transfers between devices  85.5 us (51%)
  matrix products  21.2 us (13%)
  starting transfers between devices  16 us (10%)
  between operations  14 us (8%)
  other arithmetic  11.7 us (7%)
  blocking collectives  10 us (6%)
  local copies, waits for them, and re-layouts  9.03 us (5%)
    reduce_scatter x4, waiting for transfers between devices, local(): lax.psum_scatter(partial_grad, 'dp', scatter_dimension=0, tiled=True)  71.4 us
    all_to_all x3, starting transfers between devices, exchange(): lax.all_to_all(block.reshape(experts, capacity, width), 'expert', split_a...  12.8 us
    all_to_all x1, blocking collectives, exchange(): lax.all_to_all(block.reshape(experts, capacity, width), 'expert', split_a...  10 us
    all_to_all x3, waiting for transfers between devices, exchange(): lax.all_to_all(block.reshape(experts, capacity, width), 'expert', split_a...  9.42 us
    dot_general x4, matrix products, local(): lax.dot_general(hidden, weighted, (((0,), (0,)), ((), ())), preferred_ele...  9.33 us
    dot_general x4, matrix products, local(): jnp.dot(pick_rows, out_grad[:, part * width:(part + 1) * width], preferre...  6.92 us
    convert_element_type x2, other arithmetic, local(): hidden = (gate_pre * sigmoid_gate * up_pre).astype(jnp.bfloat16)  4.87 us
    all_to_all x1, waiting for transfers between devices, local(): lax.all_to_all(slot_grad.reshape(experts, capacity), 'expert', split_axis...  4.6 us
  transfers between devices with their start and end apart: 8, of which 7 were waited for; matrix products, arithmetic and copies ran while one was open for 18% of the time, Pallas kernels for 0%

profile of v2, /device:TPU:0, one launch (start us, length us, event | category | flops | bytes accessed | tf_op | source)
XLA Modules:
  0.0 167.4 jit_solution(4591094652488381306)
XLA Ops:
  7.2 0.9 copy.26
  9.4 0.8 copy.29
  10.4 1.2 convolution_convert_fusion.7
  11.7 0.8 pad_maximum_fusion
  12.6 5.2 %all-to-all-start = ((bf16[4,96,640]{2,1,0:T(8,128)(2,1)}), bf16[4,96,640]{2,1,0:T(8,128)(2,1)}, u32[]{:S(2)}, u32[]{:S(2)}) async-start(bf16[4,96,640]{2,1,0:T(8,128)(2,1)} %bitcast.75), calls=%async_computation | async-start | bytes 983040 | tf_op jit(solution)/shard_map/all_to_all | solution.py:58
  17.7 1.9 %convolution_convert_fusion.6 = bf16[384,512]{1,0:T(8,128)(2,1)} fusion(pred[384,128]{1,0:T(8,128)(4,1)S(1)} %fusion.26, bf16[128,2048]{1,0:T(8,128)(2,1)} %param.6), kind=kOutput, calls=%fused_computation.16 | convolution fusion | flops 50528256 | bytes 573440 | tf_op jit(solution)/shard_map/dot_general | solution.py:69
  19.6 2.4 %fusion.10 = bf16[384,768]{1,0:T(8,128)(2,1)} fusion(bf16[1,1,4,96,768]{4,3,2,1,0:T(8,128)(2,1)} %param.10, bf16[1,1,4,96,768]{4,3,2,1,0:T(8,128)(2,1)} %param.9), kind=kLoop, calls=%fused_computation.22 | loop fusion | flops 2359296 | bytes 1769472 | tf_op jit(solution)/shard_map/convert_element_type | solution.py:54
  22.1 3.9 %all-to-all-done = bf16[4,96,640]{2,1,0:T(8,128)(2,1)} async-done(((bf16[4,96,640]{2,1,0:T(8,128)(2,1)}), bf16[4,96,640]{2,1,0:T(8,128)(2,1)}, u32[]{:S(2)}, u32[]{:S(2)}) %all-to-all-start) | async-done | bytes 491552 | tf_op jit(solution)/shard_map/all_to_all | solution.py:58
  25.9 0.9 slice_convert_fusion
  27.1 2.7 %convolution_convert_fusion.3 = bf16[768,512]{1,0:T(8,128)(2,1)} fusion(bf16[384,768]{1,0:T(8,128)(2,1)} %fusion.10, f32[384]{0:T(512)S(1)} %fusion.27, bf16[384,640]{1,0:T(8,128)(2,1)} %bitcast.3), kind=kOutput, calls=%fused_computation.13 | convolution fusion | flops 302972928 | bytes 1771008 | tf_op jit(solution)/shard_map/dot_general | solution.py:85
  29.8 3.5 %all-to-all-start.1 = ((bf16[4,96,512]{2,1,0:T(8,128)(2,1)}), bf16[4,96,512]{2,1,0:T(8,128)(2,1)S(1)}, u32[]{:S(2)}, u32[]{:S(2)}) async-start(bf16[4,96,512]{2,1,0:T(8,128)(2,1)} %bitcast.78), calls=%async_computation.2 | async-start | bytes 786432 | tf_op jit(solution)/shard_map/all_to_all | solution.py:58
  33.4 1.9 %convolution_convert_fusion.5 = bf16[384,512]{1,0:T(8,128)(2,1)} fusion(pred[384,128]{1,0:T(8,128)(4,1)} %copy-done.2, bf16[128,2048]{1,0:T(8,128)(2,1)} %param.6), kind=kOutput, calls=%fused_computation.15 | convolution fusion | flops 50528256 | bytes 573440 | tf_op jit(solution)/shard_map/dot_general | solution.py:69
  35.3 2.5 %fusion.9 = bf16[1,1,4,96,768]{4,3,2,1,0:T(8,128)(2,1)} fusion(bf16[1,1,4,96,768]{4,3,2,1,0:T(8,128)(2,1)} %param.10, bf16[1,1,4,96,768]{4,3,2,1,0:T(8,128)(2,1)} %param.9), kind=kLoop, calls=%fused_computation.21 | loop fusion | flops 2359296 | bytes 1769472 | tf_op jit(solution)/shard_map/convert_element_type | solution.py:54
  37.8 1.6 all-to-all-done.1
  39.6 2.6 %convolution_convert_fusion.2 = bf16[768,512]{1,0:T(8,128)(2,1)} fusion(bf16[384,768]{1,0:T(8,128)(2,1)} %bitcast.81, bf16[384,512]{1,0:T(8,128)(2,1)S(1)} %bitcast.85), kind=kOutput, calls=%fused_computation.12 | convolution fusion | flops 302383104 | bytes 1769472 | tf_op jit(solution)/shard_map/dot_general | solution.py:85
  42.2 4.1 %all-to-all-start.2 = ((bf16[4,96,512]{2,1,0:T(8,128)(2,1)}), bf16[4,96,512]{2,1,0:T(8,128)(2,1)}, u32[]{:S(2)}, u32[]{:S(2)}) async-start(bf16[4,96,512]{2,1,0:T(8,128)(2,1)} %bitcast.79), calls=%async_computation.4 | async-start | bytes 786432 | tf_op jit(solution)/shard_map/all_to_all | solution.py:58
  46.3 1.9 %convolution_convert_fusion.4 = bf16[384,512]{1,0:T(8,128)(2,1)} fusion(pred[384,128]{1,0:T(8,128)(4,1)} %copy-done.2, bf16[128,2048]{1,0:T(8,128)(2,1)} %param.6), kind=kOutput, calls=%fused_computation.14 | convolution fusion | flops 50528256 | bytes 573440 | tf_op jit(solution)/shard_map/dot_general | solution.py:69
  48.3 4.0 %all-to-all-done.2 = bf16[4,96,512]{2,1,0:T(8,128)(2,1)} async-done(((bf16[4,96,512]{2,1,0:T(8,128)(2,1)}), bf16[4,96,512]{2,1,0:T(8,128)(2,1)}, u32[]{:S(2)}, u32[]{:S(2)}) %all-to-all-start.2) | async-done | bytes 393248 | tf_op jit(solution)/shard_map/all_to_all | solution.py:58
  52.2 1.1 multiply_convert_fusion.1
  53.4 2.6 %convolution_convert_fusion.1 = bf16[768,512]{1,0:T(8,128)(2,1)} fusion(bf16[384,768]{1,0:T(8,128)(2,1)} %bitcast.82, bf16[384,512]{1,0:T(8,128)(2,1)S(1)} %bitcast.86), kind=kOutput, calls=%fused_computation.11 | convolution fusion | flops 302383104 | bytes 1769472 | tf_op jit(solution)/shard_map/dot_general | solution.py:85
  56.0 10.0 %all_to_all.29 = bf16[4,96,512]{2,1,0:T(8,128)(2,1)S(1)} all-to-all(bf16[4,96,512]{2,1,0:T(8,128)(2,1)} %bitcast.80), channel_id=1, replica_groups=mesh['expert'=4,'dp'=8] {'expert'}, dimensions={0} | all-to-all | bytes 786432 | tf_op jit(solution)/shard_map/all_to_all | solution.py:58
  66.9 1.5 convolution_convert_fusion
  68.4 1.0 mul.134
  69.4 1.0 slice.42
  70.4 4.6 %fusion.22 = (bf16[384,768]{1,0:T(8,128)(2,1)}, bf16[384,768]{1,0:T(8,128)(2,1)}, f32[384]{0:T(512)S(1)}) fusion(bf16[1,1,4,96,768]{4,3,2,1,0:T(8,128)(2,1)} %param.9, f32[384]{0:T(512)S(1)} %fusion.27, bf16[1,1,4,96,768]{4,3,2,1,0:T(8,128)(2,1)} %param.10, bf16[384,768]{1,0:T(8,128)(2,1)} %fusion.10, bf16[1,768,2048]{2,1,0:T(8,128)(2,1)S(1)} %copy-done, ...), kind=kOutput, calls=%fused_computation.40 | convolution fusion | flops 1219853952 | bytes 7670784 | tf_op jit(solution)/shard_map/dot_general | solution.py:99
  75.7 3.2 %all-to-all-start.4 = ((f32[4,1,96]{2,1,0:T(1,128)}), f32[4,1,96]{2,1,0:T(1,128)S(1)}, u32[]{:S(2)}, u32[]{:S(2)}) async-start(f32[4,1,96]{2,1,0:T(1,128)} %all_to_all.22), calls=%async_computation.8 | async-start | bytes 4096 | tf_op jit(solution)/shard_map/all_to_all | solution.py:108
  78.9 4.6 %all-to-all-done.4 = f32[4,1,96]{2,1,0:T(1,128)S(1)} async-done(((f32[4,1,96]{2,1,0:T(1,128)}), f32[4,1,96]{2,1,0:T(1,128)S(1)}, u32[]{:S(2)}, u32[]{:S(2)}) %all-to-all-start.4) | async-done | bytes 1568 | tf_op jit(solution)/shard_map/all_to_all | solution.py:108
  84.8 1.9 %gather_fusion = f32[256]{0:T(256)S(1)} fusion(f32[384]{0:T(512)S(1)} %reshape.180, s32[1024]{0:T(1024)S(1)} %pad_clamp_fusion), kind=kCustom, calls=%fused_computation | custom fusion | bytes 3072 | tf_op jit(solution)/shard_map/gather | solution.py:111
  87.5 6.7 %reduce-scatter.7.cloned.1.call-done = bf16[96,512]{1,0:T(8,128)(2,1)} async-done(((bf16[768,512]{1,0:T(8,128)(2,1)}), bf16[96,512]{1,0:T(8,128)(2,1)}) %reduce-scatter.7.cloned.1.call-update) | async-done | bytes 98320 | tf_op jit(solution)/shard_map/reduce_scatter | solution.py:92
  94.2 32.1 %reduce-scatter.9.cloned.1.call-done = bf16[96,512]{1,0:T(8,128)(2,1)} async-done(((bf16[768,512]{1,0:T(8,128)(2,1)}), bf16[96,512]{1,0:T(8,128)(2,1)}) %reduce-scatter.9.cloned.1.call-update) | async-done | bytes 98320 | tf_op jit(solution)/shard_map/reduce_scatter | solution.py:92
  126.3 32.6 %reduce-scatter.11.cloned.1.call-done = bf16[96,512]{1,0:T(8,128)(2,1)} async-done(((bf16[768,512]{1,0:T(8,128)(2,1)}), bf16[96,512]{1,0:T(8,128)(2,1)}) %reduce-scatter.11.cloned.1.call-update) | async-done | bytes 98320 | tf_op jit(solution)/shard_map/reduce_scatter | solution.py:92
  158.9 2.0 %fusion.24 = f32[1,96,2048]{2,1,0:T(8,128)} fusion(bf16[96,512]{1,0:T(8,128)(2,1)} %reduce-scatter.11.cloned.1.call-done, bf16[96,512]{1,0:T(8,128)(2,1)} %reduce-scatter.9.cloned.1.call-done, bf16[96,512]{1,0:T(8,128)(2,1)} %reduce-scatter.7.cloned.1.call-done, bf16[96,512]{1,0:T(8,128)(2,1)} %reduce-scatter.5.cloned.1.call-done), kind=kLoop, calls=%fused_computation.51 | loop fusion | flops 1769472 | bytes 1179648 | tf_op jit(solution)/shard_map/broadcast_in_dim | solution.py:113
  (40 shorter events, 5.9 us)
Async XLA Ops:
  7.2 63.3 %copy-start = (bf16[1,768,2048]{2,1,0:T(8,128)(2,1)S(1)}, bf16[1,768,2048]{2,1,0:T(8,128)(2,1)}, u32[]{:S(2)}) copy-start(bf16[1,768,2048]{2,1,0:T(8,128)(2,1)} %param.11) | copy-start | bytes 9437188
  9.4 8.3 %copy-start.2 = (pred[384,128]{1,0:T(8,128)(4,1)}, pred[384,128]{1,0:T(8,128)(4,1)S(1)}, u32[]{:S(2)}) copy-start(pred[384,128]{1,0:T(8,128)(4,1)S(1)} %fusion.26) | copy-start | bytes 147460
  12.6 13.4 %all-to-all-start = ((bf16[4,96,640]{2,1,0:T(8,128)(2,1)}), bf16[4,96,640]{2,1,0:T(8,128)(2,1)}, u32[]{:S(2)}, u32[]{:S(2)}) async-start(bf16[4,96,640]{2,1,0:T(8,128)(2,1)} %bitcast.75), calls=%async_computation | async-start | bytes 983040 | tf_op jit(solution)/shard_map/all_to_all | solution.py:58
  17.7 69.8 %reduce-scatter.5.cloned.1.call-start = ((), (), s32[]{:S(2)}) async-start(), calls=%async_computation.9 | async-start | bytes 884736 | tf_op jit(solution)/shard_map/reduce_scatter | solution.py:92
  29.8 9.6 %all-to-all-start.1 = ((bf16[4,96,512]{2,1,0:T(8,128)(2,1)}), bf16[4,96,512]{2,1,0:T(8,128)(2,1)S(1)}, u32[]{:S(2)}, u32[]{:S(2)}) async-start(bf16[4,96,512]{2,1,0:T(8,128)(2,1)} %bitcast.78), calls=%async_computation.2 | async-start | bytes 786432 | tf_op jit(solution)/shard_map/all_to_all | solution.py:58
  33.3 60.9 %reduce-scatter.7.cloned.1.call-start = ((), (), s32[]{:S(2)}) async-start(), calls=%async_computation.10 | async-start | bytes 884736 | tf_op jit(solution)/shard_map/reduce_scatter | solution.py:92
  42.2 10.1 %all-to-all-start.2 = ((bf16[4,96,512]{2,1,0:T(8,128)(2,1)}), bf16[4,96,512]{2,1,0:T(8,128)(2,1)}, u32[]{:S(2)}, u32[]{:S(2)}) async-start(bf16[4,96,512]{2,1,0:T(8,128)(2,1)} %bitcast.79), calls=%async_computation.4 | async-start | bytes 786432 | tf_op jit(solution)/shard_map/all_to_all | solution.py:58
  46.3 80.0 %reduce-scatter.9.cloned.1.call-start = ((), (), s32[]{:S(2)}) async-start(), calls=%async_computation.11 | async-start | bytes 884736 | tf_op jit(solution)/shard_map/reduce_scatter | solution.py:92
  56.0 102.9 %reduce-scatter.11.cloned.1.call-start = ((), (), s32[]{:S(2)}) async-start(), calls=%async_computation.12 | async-start | bytes 884736 | tf_op jit(solution)/shard_map/reduce_scatter | solution.py:92
  56.0 10.9 %copy-start.3 = (bf16[1,1,4,96,768]{4,3,2,1,0:T(8,128)(2,1)S(1)}, bf16[1,1,4,96,768]{4,3,2,1,0:T(8,128)(2,1)}, u32[]{:S(2)}) copy-start(bf16[1,1,4,96,768]{4,3,2,1,0:T(8,128)(2,1)} %fusion.9) | copy-start | bytes 1769476
  66.0 0.7 copy-start.1
  75.7 7.8 %all-to-all-start.4 = ((f32[4,1,96]{2,1,0:T(1,128)}), f32[4,1,96]{2,1,0:T(1,128)S(1)}, u32[]{:S(2)}, u32[]{:S(2)}) async-start(f32[4,1,96]{2,1,0:T(1,128)} %all_to_all.22), calls=%async_computation.8 | async-start | bytes 4096 | tf_op jit(solution)/shard_map/all_to_all | solution.py:108
Sparse Core Ops, SparseCore 0:
  29.9 32.0 reduce-scatter.4
  64.4 29.7 reduce-scatter.6
  96.5 29.7 reduce-scatter.8
  129.1 29.7 reduce-scatter.10

commit v3 on v1

--- a/solution.py
+++ b/solution.py
@@ -64,12 +64,19 @@
     sigmoid_gate = jax.nn.sigmoid(gate_pre)
     hidden = (gate_pre * sigmoid_gate * up_pre).astype(jnp.bfloat16)
     weighted = (weights[:, None] * rows.astype(jnp.float32)).astype(jnp.bfloat16)
+    chips = lax.axis_size("z")
+    cores = lax.axis_size("core")
+    share = hidden_count // (chips * cores)
+    hidden_order = (
+        hidden.reshape(-1, chips, cores, share).transpose(0, 2, 1, 3).reshape(-1, hidden_count)
+    )
     partial_grad = lax.dot_general(
-        hidden, weighted, (((0,), (0,)), ((), ())), preferred_element_type=jnp.float32
+        hidden_order, weighted, (((0,), (0,)), ((), ())), preferred_element_type=jnp.float32
     )
-    summed = lax.psum_scatter(
-        partial_grad.astype(jnp.bfloat16), "dp", scatter_dimension=0, tiled=True
+    on_chip = lax.psum_scatter(
+        partial_grad.astype(jnp.bfloat16), "core", scatter_dimension=0, tiled=True
     )
+    summed = lax.psum_scatter(on_chip, "z", scatter_dimension=0, tiled=True)
     grad_weight = summed.astype(jnp.float32)
 
     matrix = w_down[0]
@@ -95,18 +102,23 @@
 
 
 def solution(mesh):
+    experts, data = mesh.devices.shape
+    cores = 2
+    mesh = jax.sharding.Mesh(
+        mesh.devices.reshape(experts, data // cores, cores), ("expert", "z", "core")
+    )
     in_specs = (
-        P(("expert", "dp"), None),
-        P(("expert", "dp"), None),
-        P(("expert", "dp"), None),
-        P("expert", "dp", None, None, None),
-        P("expert", "dp", None, None, None),
+        P(("expert", "z", "core"), None),
+        P(("expert", "z", "core"), None),
+        P(("expert", "z", "core"), None),
+        P("expert", ("z", "core"), None, None, None),
+        P("expert", ("z", "core"), None, None, None),
         P("expert", None, None),
     )
     out_specs = (
-        P("expert", "dp", None),
-        P("expert", "dp", None, None, None),
-        P("expert", "dp", None, None, None),
-        P(("expert", "dp"), None),
+        P("expert", ("z", "core"), None),
+        P("expert", ("z", "core"), None, None, None),
+        P("expert", ("z", "core"), None, None, None),
+        P(("expert", "z", "core"), None),
     )
     return jax.shard_map(local, mesh=mesh, in_specs=in_specs, out_specs=out_specs, check_vma=False)

time: 93.9 us -> 105 us (1.12)
  blocking collectives: 26 us -> 0 us
  waiting for transfers between devices: 32.1 us -> 43.3 us
  local copies, waits for them, and re-layouts: 6.32 us -> 17.3 us
  other arithmetic: 3.13 us -> 8.99 us
  starting transfers between devices: 3.26 us -> 9.09 us
  matrix products: 8.54 us -> 11.9 us
    all_to_all x1 -> x0, blocking collectives: 26 us -> none  [local(): lax.all_to_all(packed.reshape(experts, capacity, feature_count + lanes),...]
    convert_element_type x0 -> x2, local copies, waits for them, and re-layouts: none -> 7.96 us  [the longest x1 3.99 us: local(): up_pre = saved_up.reshape(-1, hidden_count).astype(jnp.float32)]
    all_to_all x0 -> x1, waiting for transfers between devices: none -> 6.33 us  [local(): lax.all_to_all(packed.reshape(experts, capacity, feature_count + lanes),...]
    all_to_all x0 -> x1, starting transfers between devices: none -> 5.16 us  [local(): lax.all_to_all(packed.reshape(experts, capacity, feature_count + lanes),...]
    reduce_scatter x1 -> x2, waiting for transfers between devices: 27.6 us -> 32.4 us  [the longest x1 20.9 us: local(): summed = lax.psum_scatter(on_chip, 'z', scatter_dimension=0, tiled=True)]
    transpose x0 -> x1, other arithmetic: none -> 3.78 us  [local(): hidden.reshape(-1, chips, cores, share).transpose(0, 2, 1, 3)]
    transpose x0 -> x1, local copies, waits for them, and re-layouts: none -> 2.99 us  [local(): hidden.reshape(-1, chips, cores, share).transpose(0, 2, 1, 3)]
    dot_general x1, matrix products: 2.98 us -> 4.7 us  [local(): lax.dot_general(rows, matrix, (((1,), (1,)), ((), ())), preferred_element...]
  transfers between devices with their start and end apart: 2 -> 4, of which waited for: 2 -> 4; matrix products, arithmetic and copies ran while one was open for 4% -> 23% of each run, Pallas kernels for 0% -> 0%
where the time goes in v3:
time: 105 us
  waiting for transfers between devices  43.3 us (41%)
  local copies, waits for them, and re-layouts  17.3 us (16%)
  between operations  14.2 us (14%)
  matrix products  11.9 us (11%)
  starting transfers between devices  9.09 us (9%)
  other arithmetic  8.99 us (9%)
    reduce_scatter x1, waiting for transfers between devices, local(): summed = lax.psum_scatter(on_chip, 'z', scatter_dimension=0, tiled=True)  20.9 us
    reduce_scatter x1, waiting for transfers between devices, local(): lax.psum_scatter(partial_grad.astype(jnp.bfloat16), 'core', scatter_dimen...  11.5 us
    all_to_all x1, waiting for transfers between devices, local(): lax.all_to_all(packed.reshape(experts, capacity, feature_count + lanes),...  6.33 us
    all_to_all x1, starting transfers between devices, local(): lax.all_to_all(packed.reshape(experts, capacity, feature_count + lanes),...  5.16 us
    dot_general x1, matrix products, local(): lax.dot_general(hidden_order, weighted, (((0,), (0,)), ((), ())), preferr...  5.16 us
    dot_general x1, matrix products, local(): lax.dot_general(rows, matrix, (((1,), (1,)), ((), ())), preferred_element...  4.7 us
    all_to_all x1, waiting for transfers between devices, local(): lax.all_to_all(slot_grad.reshape(experts, capacity), 'expert', split_axis...  4.56 us
    convert_element_type x1, local copies, waits for them, and re-layouts, local(): up_pre = saved_up.reshape(-1, hidden_count).astype(jnp.float32)  3.99 us
  transfers between devices with their start and end apart: 4, of which 4 were waited for; matrix products, arithmetic and copies ran while one was open for 23% of the time, Pallas kernels for 0%

profile of v3, /device:TPU:0, one launch (start us, length us, event | category | flops | bytes accessed | tf_op | source)
XLA Modules:
  0.0 104.7 jit_solution(6805935843787772803)
XLA Ops:
  7.2 0.9 copy.26
  8.1 0.1 eq.35
  8.3 0.2 fusion.18
  8.5 0.8 copy.29
  9.3 0.1 reshape.141
  9.4 0.1 convert_element_type.99
  9.7 1.6 %convolution_convert_fusion.1 = bf16[384,2048]{1,0:T(8,128)(2,1)S(1)} fusion(pred[384,128]{1,0:T(8,128)(4,1)S(1)} %fusion.20, bf16[128,2048]{1,0:T(8,128)(2,1)} %param.6), kind=kOutput, calls=%fused_computation.5 | convolution fusion | flops 202113024 | bytes 2146304 | tf_op jit(solution)/shard_map/dot_general | solution.py:42
  11.3 0.2 convolution_convert_fusion.2
  11.5 1.3 %pad_maximum_fusion = bf16[384,2176]{1,0:T(8,128)(2,1)} fusion(bf16[384,128]{1,0:T(8,128)(2,1)S(1)} %convolution_convert_fusion.2, bf16[384,2048]{1,0:T(8,128)(2,1)S(1)} %convolution_convert_fusion.1), kind=kLoop, calls=%fused_computation.6 | loop fusion | flops 3342336 | bytes 3342336 | tf_op jit(solution)/shard_map/concatenate | solution.py:50
  12.9 5.2 %all-to-all-start = ((bf16[4,96,2176]{2,1,0:T(8,128)(2,1)}), bf16[4,96,2176]{2,1,0:T(8,128)(2,1)}, u32[]{:S(2)}, u32[]{:S(2)}) async-start(bf16[4,96,2176]{2,1,0:T(8,128)(2,1)} %bitcast.66), calls=%async_computation | async-start | bytes 3342336 | tf_op jit(solution)/shard_map/all_to_all | solution.py:51
  18.0 4.0 %reshape.149 = f32[384,4,2,96]{3,2,1,0:T(2,128)} reshape(bf16[1,1,4,96,768]{4,3,2,1,0:T(8,128)(2,1)} %param.10) | data formatting | bytes 1769472 | tf_op jit(solution)/shard_map/convert_element_type | solution.py:63
  22.0 4.0 %reshape.148 = f32[384,4,2,96]{3,2,1,0:T(2,128)} reshape(bf16[1,1,4,96,768]{4,3,2,1,0:T(8,128)(2,1)} %param.9) | data formatting | bytes 1769472 | tf_op jit(solution)/shard_map/convert_element_type | solution.py:62
  26.0 3.8 %fusion.19 = bf16[384,2,4,96]{3,1,2,0:T(2,128)(2,1)} fusion(f32[384,4,2,96]{3,2,1,0:T(2,128)} %reshape.149, f32[384,4,2,96]{3,2,1,0:T(2,128)} %reshape.148), kind=kLoop, calls=%fused_computation.33 | loop fusion | flops 1769472 | bytes 2949120 | tf_op jit(solution)/shard_map/transpose | solution.py:71
  29.8 3.0 %copy.25 = bf16[384,2,4,96]{0,3,2,1:T(8,128)(2,1)} copy(bf16[384,2,4,96]{3,1,2,0:T(2,128)(2,1)} %fusion.19) | data formatting | bytes 1179648 | tf_op jit(solution)/shard_map/transpose | solution.py:71
  32.8 6.3 %all-to-all-done = bf16[4,96,2176]{2,1,0:T(8,128)(2,1)} async-done(((bf16[4,96,2176]{2,1,0:T(8,128)(2,1)}), bf16[4,96,2176]{2,1,0:T(8,128)(2,1)}, u32[]{:S(2)}, u32[]{:S(2)}) %all-to-all-start) | async-done | bytes 1671200 | tf_op jit(solution)/shard_map/all_to_all | solution.py:51
  39.1 0.9 slice_convert_fusion
  40.0 0.3 fusion.21
  40.3 5.2 %convolution_convert_fusion = bf16[768,2048]{1,0:T(8,128)(2,1)} fusion(bf16[384,768]{0,1:T(8,128)(2,1)} %bitcast.67, f32[384]{0:T(512)S(1)} %fusion.21, bf16[384,2176]{1,0:T(8,128)(2,1)} %bitcast.3), kind=kOutput, calls=%fused_computation.1 | convolution fusion | flops 1211891712 | bytes 5309952 | tf_op jit(solution)/shard_map/dot_general | solution.py:73
  45.5 11.5 %reduce-scatter.3.cloned.1.call-done = bf16[384,2048]{1,0:T(8,128)(2,1)} async-done(((bf16[768,2048]{1,0:T(8,128)(2,1)}), bf16[384,2048]{1,0:T(8,128)(2,1)}) %reduce-scatter.3.cloned.1.call-update) | async-done | bytes 1572880 | tf_op jit(solution)/shard_map/reduce_scatter | solution.py:76
  57.0 0.1 mul.100
  57.2 4.7 %multiply_reduce_fusion = (f32[384]{0:T(512)S(1)}, bf16[384,768]{1,0:T(8,128)(2,1)}, bf16[384,768]{1,0:T(8,128)(2,1)}) fusion(bf16[1,1,4,96,768]{4,3,2,1,0:T(8,128)(2,1)} %param.10, bf16[1,1,4,96,768]{4,3,2,1,0:T(8,128)(2,1)} %param.9, f32[384]{0:T(512)S(1)} %fusion.21, bf16[1,768,2048]{2,1,0:T(8,128)(2,1)S(1)} %copy-done, bf16[384,2176]{1,0:T(8,128)(2,1)} %bitcast.3), kind=kOutput, calls=%fused_computation.29 | convolution fusion | flops 1214447232 | bytes 7080960 | tf_op jit(solution)/shard_map/dot_general | solution.py:83
  61.9 0.7 all_to_all.10
  62.6 3.9 %all-to-all-start.1 = ((f32[4,1,96]{2,1,0:T(1,128)}), f32[4,1,96]{2,1,0:T(1,128)S(1)}, u32[]{:S(2)}, u32[]{:S(2)}) async-start(f32[4,1,96]{2,1,0:T(1,128)} %all_to_all.10), calls=%async_computation.3 | async-start | bytes 4096 | tf_op jit(solution)/shard_map/all_to_all | solution.py:92
  66.5 4.6 %all-to-all-done.1 = f32[4,1,96]{2,1,0:T(1,128)S(1)} async-done(((f32[4,1,96]{2,1,0:T(1,128)}), f32[4,1,96]{2,1,0:T(1,128)S(1)}, u32[]{:S(2)}, u32[]{:S(2)}) %all-to-all-start.1) | async-done | bytes 1568 | tf_op jit(solution)/shard_map/all_to_all | solution.py:92
  71.0 0.5 broadcast.77
  71.5 0.7 reduce.5
  72.2 0.1 reshape.146
  72.3 1.9 %gather_fusion = f32[256]{0:T(256)S(1)} fusion(f32[384]{0:T(512)S(1)} %reshape.146, s32[1024]{0:T(1024)S(1)} %pad_clamp_fusion), kind=kCustom, calls=%fused_computation | custom fusion | bytes 3072 | tf_op jit(solution)/shard_map/gather | solution.py:95
  74.2 0.1 reshape.147
  74.4 0.6 copy.31
  75.0 20.9 %reduce-scatter.5.cloned.1.call-done = bf16[96,2048]{1,0:T(8,128)(2,1)} async-done(((bf16[384,2048]{1,0:T(8,128)(2,1)}), bf16[96,2048]{1,0:T(8,128)(2,1)}) %reduce-scatter.5.cloned.1.call-update) | async-done | bytes 393232 | tf_op jit(solution)/shard_map/reduce_scatter | solution.py:79
  95.9 1.9 %bitcast_convert_fusion = f32[1,96,2048]{2,1,0:T(8,128)} fusion(bf16[96,2048]{1,0:T(8,128)(2,1)} %reduce-scatter.5.cloned.1.call-done), kind=kLoop, calls=%fused_computation.34 | loop fusion | flops 196608 | bytes 1179648 | tf_op jit(solution)/shard_map/broadcast_in_dim | solution.py:97
  (14 shorter events, 0.3 us)
Async XLA Ops:
  7.2 50.0 %copy-start = (bf16[1,768,2048]{2,1,0:T(8,128)(2,1)S(1)}, bf16[1,768,2048]{2,1,0:T(8,128)(2,1)}, u32[]{:S(2)}) copy-start(bf16[1,768,2048]{2,1,0:T(8,128)(2,1)} %param.11) | copy-start | bytes 9437188
  12.9 26.2 %all-to-all-start = ((bf16[4,96,2176]{2,1,0:T(8,128)(2,1)}), bf16[4,96,2176]{2,1,0:T(8,128)(2,1)}, u32[]{:S(2)}, u32[]{:S(2)}) async-start(bf16[4,96,2176]{2,1,0:T(8,128)(2,1)} %bitcast.66), calls=%async_computation | async-start | bytes 3342336 | tf_op jit(solution)/shard_map/all_to_all | solution.py:51
  18.0 39.0 %reduce-scatter.3.cloned.1.call-start = ((), (), s32[]{:S(2)}) async-start(), calls=%async_computation.4 | async-start | bytes 4718592 | tf_op jit(solution)/shard_map/reduce_scatter | solution.py:76
  45.5 50.4 %reduce-scatter.5.cloned.1.call-start = ((), (), s32[]{:S(2)}) async-start(), calls=%async_computation.5 | async-start | bytes 1966080 | tf_op jit(solution)/shard_map/reduce_scatter | solution.py:79
  62.6 8.5 %all-to-all-start.1 = ((f32[4,1,96]{2,1,0:T(1,128)}), f32[4,1,96]{2,1,0:T(1,128)S(1)}, u32[]{:S(2)}, u32[]{:S(2)}) async-start(f32[4,1,96]{2,1,0:T(1,128)} %all_to_all.10), calls=%async_computation.3 | async-start | bytes 4096 | tf_op jit(solution)/shard_map/all_to_all | solution.py:92
Sparse Core Ops, SparseCore 0:
  45.6 11.3 reduce-scatter.2
  59.4 36.4 reduce-scatter.4

commit v4 on v3

--- a/solution.py
+++ b/solution.py
@@ -14,6 +14,42 @@
     middle = round_bf16(rest)
     low = rest - middle
     return jnp.stack([high, middle, low], axis=-1).astype(jnp.bfloat16)
+
+
+def pick(blocks, index):
+    return lax.dynamic_index_in_dim(blocks, index, axis=0, keepdims=False)
+
+
+def line_scatter(partial):
+    chips = lax.axis_size("z")
+    cores = lax.axis_size("core")
+    features = partial.shape[1]
+    share = partial.shape[0] // (chips * cores)
+    if chips > 4 or cores != 2:
+        summed = lax.psum_scatter(
+            partial.astype(jnp.bfloat16), ("z", "core"), scatter_dimension=0, tiled=True
+        )
+        return summed.astype(jnp.float32)
+    blocks = jnp.swapaxes(partial.reshape(chips, cores, share, features), 0, 1)
+    core = lax.axis_index("core")
+    outgoing = pick(blocks, 1 - core).astype(jnp.bfloat16)
+    incoming = lax.ppermute(outgoing, "core", perm=[(0, 1), (1, 0)])
+    mine = pick(blocks, core) + incoming.astype(jnp.float32)
+    chip = lax.axis_index("z")
+    right = jnp.zeros((share, features), jnp.bfloat16)
+    left = jnp.zeros((share, features), jnp.bfloat16)
+    for step in range(1, chips):
+        send_right = pick(mine, chip + chips - step) + right.astype(jnp.float32)
+        send_left = pick(mine, chip - chips + step) + left.astype(jnp.float32)
+        right = lax.ppermute(
+            send_right.astype(jnp.bfloat16), "z",
+            perm=[(k, k + 1) for k in range(step) if k + 1 < chips],
+        )
+        left = lax.ppermute(
+            send_left.astype(jnp.bfloat16), "z",
+            perm=[(chips - 1 - k, chips - 2 - k) for k in range(step) if chips - 2 - k >= 0],
+        )
+    return pick(mine, chip) + right.astype(jnp.float32) + left.astype(jnp.float32)
 
 
 def local(out_grad, combine_weight, routes, saved_gate, saved_up, w_down):
@@ -64,20 +100,10 @@
     sigmoid_gate = jax.nn.sigmoid(gate_pre)
     hidden = (gate_pre * sigmoid_gate * up_pre).astype(jnp.bfloat16)
     weighted = (weights[:, None] * rows.astype(jnp.float32)).astype(jnp.bfloat16)
-    chips = lax.axis_size("z")
-    cores = lax.axis_size("core")
-    share = hidden_count // (chips * cores)
-    hidden_order = (
-        hidden.reshape(-1, chips, cores, share).transpose(0, 2, 1, 3).reshape(-1, hidden_count)
+    partial_grad = lax.dot_general(
+        hidden, weighted, (((0,), (0,)), ((), ())), preferred_element_type=jnp.float32
     )
-    partial_grad = lax.dot_general(
-        hidden_order, weighted, (((0,), (0,)), ((), ())), preferred_element_type=jnp.float32
-    )
-    on_chip = lax.psum_scatter(
-        partial_grad.astype(jnp.bfloat16), "core", scatter_dimension=0, tiled=True
-    )
-    summed = lax.psum_scatter(on_chip, "z", scatter_dimension=0, tiled=True)
-    grad_weight = summed.astype(jnp.float32)
+    grad_weight = line_scatter(partial_grad)
 
     matrix = w_down[0]
     back = lax.dot_general(

time: 105 us -> 121 us (1.15)
  the two profiles are of different devices: /device:TPU:0 before, /device:TPU:16 now
where the time goes in v4:
time: 121 us
  waiting for transfers between devices  54.8 us (45%)
  starting transfers between devices  21.4 us (18%)
  local copies, waits for them, and re-layouts  17.3 us (14%)
  other arithmetic  15.8 us (13%)
  matrix products  10.4 us (9%)
    all_to_all x1, waiting for transfers between devices, local(): lax.all_to_all(packed.reshape(experts, capacity, feature_count + lanes),...  20.6 us
    ppermute x3, waiting for transfers between devices, line_scatter(): lax.ppermute(send_left.astype(jnp.bfloat16), 'z', perm=[(chips - 1 - k, c...  13.8 us
    ppermute x3, waiting for transfers between devices, line_scatter(): lax.ppermute(send_right.astype(jnp.bfloat16), 'z', perm=[(k, k + 1) for k...  12.1 us
    ppermute x3, starting transfers between devices, line_scatter(): lax.ppermute(send_left.astype(jnp.bfloat16), 'z', perm=[(chips - 1 - k, c...  8.25 us
    unnamed x9, local copies, waits for them, and re-layouts  7.49 us
    ppermute x3, starting transfers between devices, line_scatter(): lax.ppermute(send_right.astype(jnp.bfloat16), 'z', perm=[(k, k + 1) for k...  5.59 us
    dot_general x1, matrix products, local(): lax.dot_general(rows, matrix, (((1,), (1,)), ((), ())), preferred_element...  4.91 us
    convert_element_type x2, other arithmetic, line_scatter(): send_right.astype(jnp.bfloat16)  4.73 us
  transfers between devices with their start and end apart: 9, of which 6 were waited for; matrix products, arithmetic and copies ran while one was open for 9% of the time, Pallas kernels for 0%

profile of v4, /device:TPU:16, one launch (start us, length us, event | category | flops | bytes accessed | tf_op | source)
XLA Modules:
  0.0 120.6 jit_solution(17668868130810687991)
XLA Ops:
  0.6 0.9 copy.28
  3.8 1.6 %convolution_convert_fusion = bf16[384,2048]{1,0:T(8,128)(2,1)S(1)} fusion(pred[384,128]{1,0:T(8,128)(4,1)S(1)} %fusion.28, bf16[128,2048]{1,0:T(8,128)(2,1)} %param.6), kind=kOutput, calls=%fused_computation.6 | convolution fusion | flops 202113024 | bytes 2146304 | tf_op jit(solution)/shard_map/dot_general | solution.py:78
  5.6 1.3 %pad_maximum_fusion = bf16[384,2176]{1,0:T(8,128)(2,1)} fusion(bf16[384,128]{1,0:T(8,128)(2,1)S(1)} %convolution_convert_fusion.1, bf16[384,2048]{1,0:T(8,128)(2,1)S(1)} %convolution_convert_fusion), kind=kLoop, calls=%fused_computation.11 | loop fusion | flops 3342336 | bytes 3342336 | tf_op jit(solution)/shard_map/concatenate | solution.py:86
  6.9 4.4 %all-to-all-start = ((bf16[4,96,2176]{2,1,0:T(8,128)(2,1)}), bf16[4,96,2176]{2,1,0:T(8,128)(2,1)}, u32[]{:S(2)}, u32[]{:S(2)}) async-start(bf16[4,96,2176]{2,1,0:T(8,128)(2,1)} %bitcast.64), calls=%async_computation | async-start | bytes 3342336 | tf_op jit(solution)/shard_map/all_to_all | solution.py:87
  11.3 20.6 %all-to-all-done = bf16[4,96,2176]{2,1,0:T(8,128)(2,1)} async-done(((bf16[4,96,2176]{2,1,0:T(8,128)(2,1)}), bf16[4,96,2176]{2,1,0:T(8,128)(2,1)}, u32[]{:S(2)}, u32[]{:S(2)}) %all-to-all-start) | async-done | bytes 1671200 | tf_op jit(solution)/shard_map/all_to_all | solution.py:87
  32.0 0.9 slice_convert_fusion
  33.1 4.9 %multiply_reduce_fusion = (f32[384]{0:T(512)S(1)}, bf16[384,768]{1,0:T(8,128)(2,1)}, bf16[384,768]{1,0:T(8,128)(2,1)}, bf16[384,768]{1,0:T(8,128)(2,1)}) fusion(bf16[1,1,4,96,768]{4,3,2,1,0:T(8,128)(2,1)} %param.10, bf16[1,1,4,96,768]{4,3,2,1,0:T(8,128)(2,1)} %param.9, f32[384]{0:T(512)S(1)} %fusion.29, bf16[1,768,2048]{2,1,0:T(8,128)(2,1)S(1)} %copy-done, ...), kind=kOutput, calls=%fused_computation.30 | convolution fusion | flops 1214447232 | bytes 7670784 | tf_op jit(solution)/shard_map/dot_general | solution.py:109
  38.0 2.1 %copy.27 = bf16[768,384]{1,0:T(8,128)(2,1)} copy(bf16[768,384]{0,1:T(8,128)(2,1)} %bitcast.66) | data formatting | bytes 1179648 | tf_op jit(solution)/shard_map/dot_general | solution.py:103
  40.2 3.5 %fusion.3 = f32[4,2,96,2048]{3,2,1,0:T(8,128)S(1)} fusion(bf16[4,2,96,384]{3,2,1,0:T(8,128)(2,1)} %bitcast.65, f32[384]{0:T(512)S(1)} %fusion.29, bf16[384,2176]{1,0:T(8,128)(2,1)} %bitcast.6), kind=kOutput, calls=%fused_computation.13 | convolution fusion | flops 1210318848 | bytes 8455680 | tf_op jit(solution)/shard_map/dot_general | solution.py:103
  43.7 2.6 %copy-done.2 = f32[4,2,96,2048]{3,2,1,0:T(8,128)} copy-done((f32[4,2,96,2048]{3,2,1,0:T(8,128)}, f32[4,2,96,2048]{3,2,1,0:T(8,128)S(1)}, u32[]{:S(2)}) %copy-start.2) | copy-done | bytes 6291480
  46.3 1.4 %fusion.5 = bf16[4,96,2048]{2,1,0:T(8,128)(2,1)} fusion(f32[4,2,96,2048]{3,2,1,0:T(8,128)S(1)} %fusion.3, s32[]{:T(128)S(6)} %select_n.40), kind=kLoop, calls=%fused_computation.14 | loop fusion | bytes 3145732 | tf_op jit(solution)/shard_map/convert_element_type | solution.py:35
  47.8 3.7 %collective-permute-done = bf16[4,96,2048]{2,1,0:T(8,128)(2,1)} collective-permute-done((bf16[4,96,2048]{2,1,0:T(8,128)(2,1)}, bf16[4,96,2048]{2,1,0:T(8,128)(2,1)}, u32[]{:S(2)}, u32[]{:S(2)}) %collective-permute-start) | collective-permute-done | bytes 1572896 | tf_op jit(solution)/shard_map/ppermute | solution.py:36
  51.5 2.9 %bitcast_add_fusion = f32[4,96,2048]{2,1,0:T(8,128)S(1)} fusion(bf16[4,96,2048]{2,1,0:T(8,128)(2,1)} %collective-permute-done, f32[4,2,96,2048]{3,2,1,0:T(8,128)} %copy-done.2, s32[]{:T(128)S(6)} %select_n.39), kind=kLoop, calls=%fused_computation.3 | loop fusion | flops 1572864 | bytes 7864324 | tf_op jit(solution)/shard_map/add | solution.py:37
  54.4 1.6 %copy-done.1 = f32[4,96,2048]{2,1,0:T(8,128)} copy-done((f32[4,96,2048]{2,1,0:T(8,128)}, f32[4,96,2048]{2,1,0:T(8,128)S(1)}, u32[]{:S(2)}) %copy-start.1) | copy-done | bytes 3145752
  56.9 1.4 %collective-permute-start.1 = (bf16[96,2048]{1,0:T(8,128)(2,1)}, bf16[96,2048]{1,0:T(8,128)(2,1)}, u32[]{:S(2)}, u32[]{:S(2)}) collective-permute-start(bf16[96,2048]{1,0:T(8,128)(2,1)} %get-tuple-element.20), channel_id=1, source_target_pairs={{0,2},{1,3},{8,10},{9,11},{16,18},{17,19},{24,26},{25,27}} | collective-permute-start | bytes 1179656 | tf_op jit(solution)/shard_map/ppermute | solution.py:44
  58.3 1.3 %collective-permute-start.4 = (bf16[96,2048]{1,0:T(8,128)(2,1)S(1)}, bf16[96,2048]{1,0:T(8,128)(2,1)}, u32[]{:S(2)}, u32[]{:S(2)}) collective-permute-start(bf16[96,2048]{1,0:T(8,128)(2,1)S(1)} %get-tuple-element.21), channel_id=1, source_target_pairs={{6,4},{7,5},{14,12},{15,13},{22,20},{23,21},{30,28},{31,29}} | collective-permute-start | bytes 1179656 | tf_op jit(solution)/shard_map/ppermute | solution.py:48
  59.6 2.1 %fusion.22 = bf16[96,2048]{1,0:T(8,128)(2,1)} fusion(bf16[96,2048]{1,0:T(8,128)(2,1)} %collective-permute-done.1, f32[4,96,2048]{2,1,0:T(8,128)} %copy-done.1, s32[]{:T(128)S(6)} %select_n.43), kind=kLoop, calls=%fused_computation.39 | loop fusion | flops 589824 | bytes 1572868 | tf_op jit(solution)/shard_map/convert_element_type | solution.py:45
  61.6 1.3 %collective-permute-start.2 = (bf16[96,2048]{1,0:T(8,128)(2,1)}, bf16[96,2048]{1,0:T(8,128)(2,1)}, u32[]{:S(2)}, u32[]{:S(2)}) collective-permute-start(bf16[96,2048]{1,0:T(8,128)(2,1)} %fusion.22), channel_id=1, source_target_pairs={{0,2},{2,4},{1,3},{3,5},{8,10},{10,12},{9,11},{11,13},{16,18},{18,... | collective-permute-start | bytes 1179656 | tf_op jit(solution)/shard_map/ppermute | solution.py:44
  62.9 8.5 %collective-permute-done.4 = bf16[96,2048]{1,0:T(8,128)(2,1)} collective-permute-done((bf16[96,2048]{1,0:T(8,128)(2,1)S(1)}, bf16[96,2048]{1,0:T(8,128)(2,1)}, u32[]{:S(2)}, u32[]{:S(2)}) %collective-permute-start.4) | collective-permute-done | bytes 393248 | tf_op jit(solution)/shard_map/ppermute | solution.py:48
  71.4 12.1 %collective-permute-done.2 = bf16[96,2048]{1,0:T(8,128)(2,1)} collective-permute-done((bf16[96,2048]{1,0:T(8,128)(2,1)}, bf16[96,2048]{1,0:T(8,128)(2,1)}, u32[]{:S(2)}, u32[]{:S(2)}) %collective-permute-start.2) | collective-permute-done | bytes 393248 | tf_op jit(solution)/shard_map/ppermute | solution.py:44
  83.5 2.6 %fusion.23 = (bf16[96,2048]{1,0:T(8,128)(2,1)}, bf16[96,2048]{1,0:T(8,128)(2,1)}) fusion(bf16[96,2048]{1,0:T(8,128)(2,1)} %collective-permute-done.2, f32[4,96,2048]{2,1,0:T(8,128)} %copy-done.1, s32[]{:T(128)S(6)} %select_n.42, bf16[96,2048]{1,0:T(8,128)(2,1)} %collective-permute-done.4, s32[]{:T(128)S(6)} %select_n.46), kind=kLoop, calls=%fused_computation.41 | loop fusion | flops 1179648 | bytes 3145736 | tf_op jit(solution)/shard_map/convert_element_type | solution.py:45
  86.2 3.6 %collective-permute-start.5 = (bf16[96,2048]{1,0:T(8,128)(2,1)}, bf16[96,2048]{1,0:T(8,128)(2,1)}, u32[]{:S(2)}, u32[]{:S(2)}) collective-permute-start(bf16[96,2048]{1,0:T(8,128)(2,1)} %get-tuple-element.19), channel_id=1, source_target_pairs={{6,4},{4,2},{7,5},{5,3},{14,12},{12,10},{15,13},{13,11},{22,20},{2... | collective-permute-start | bytes 1179656 | tf_op jit(solution)/shard_map/ppermute | solution.py:48
  89.8 2.9 %collective-permute-start.3 = (bf16[96,2048]{1,0:T(8,128)(2,1)}, bf16[96,2048]{1,0:T(8,128)(2,1)S(1)}, u32[]{:S(2)}, u32[]{:S(2)}) collective-permute-start(bf16[96,2048]{1,0:T(8,128)(2,1)} %get-tuple-element.18), channel_id=1, source_target_pairs={{0,2},{2,4},{4,6},{1,3},{3,5},{5,7},{8,10},{10,12},{12,14},{9,11},... | collective-permute-start | bytes 1179656 | tf_op jit(solution)/shard_map/ppermute | solution.py:44
  92.8 5.3 %collective-permute-done.5 = bf16[96,2048]{1,0:T(8,128)(2,1)} collective-permute-done((bf16[96,2048]{1,0:T(8,128)(2,1)}, bf16[96,2048]{1,0:T(8,128)(2,1)}, u32[]{:S(2)}, u32[]{:S(2)}) %collective-permute-start.5) | collective-permute-done | bytes 393248 | tf_op jit(solution)/shard_map/ppermute | solution.py:48
  98.1 2.1 %fusion.21 = bf16[96,2048]{1,0:T(8,128)(2,1)} fusion(bf16[96,2048]{1,0:T(8,128)(2,1)} %collective-permute-done.5, f32[4,96,2048]{2,1,0:T(8,128)} %copy-done.1, s32[]{:T(128)S(6)} %select_n.45), kind=kLoop, calls=%fused_computation.37 | loop fusion | flops 589824 | bytes 1572868 | tf_op jit(solution)/shard_map/convert_element_type | solution.py:49
  100.2 3.3 %collective-permute-start.6 = (bf16[96,2048]{1,0:T(8,128)(2,1)}, bf16[96,2048]{1,0:T(8,128)(2,1)}, u32[]{:S(2)}, u32[]{:S(2)}) collective-permute-start(bf16[96,2048]{1,0:T(8,128)(2,1)} %fusion.21), channel_id=1, source_target_pairs={{6,4},{4,2},{2,0},{7,5},{5,3},{3,1},{14,12},{12,10},{10,8},{15,13}... | collective-permute-start | bytes 1179656 | tf_op jit(solution)/shard_map/ppermute | solution.py:48
  103.5 1.0 mul.92
  105.2 3.2 %all-to-all-start.1 = ((f32[4,1,96]{2,1,0:T(1,128)}), f32[4,1,96]{2,1,0:T(1,128)S(1)}, u32[]{:S(2)}, u32[]{:S(2)}) async-start(f32[4,1,96]{2,1,0:T(1,128)} %all_to_all.10), calls=%async_computation.1 | async-start | bytes 4096 | tf_op jit(solution)/shard_map/all_to_all | solution.py:118
  108.4 4.4 %all-to-all-done.1 = f32[4,1,96]{2,1,0:T(1,128)S(1)} async-done(((f32[4,1,96]{2,1,0:T(1,128)}), f32[4,1,96]{2,1,0:T(1,128)S(1)}, u32[]{:S(2)}, u32[]{:S(2)}) %all-to-all-start.1) | async-done | bytes 1568 | tf_op jit(solution)/shard_map/all_to_all | solution.py:118
  114.1 1.9 %gather_fusion = f32[256]{0:T(256)S(1)} fusion(f32[384]{0:T(512)S(1)} %reshape.144, s32[1024]{0:T(1024)S(1)} %pad_clamp_fusion), kind=kCustom, calls=%fused_computation | custom fusion | bytes 3072 | tf_op jit(solution)/shard_map/gather | solution.py:121
  116.8 1.5 %copy.33 = f32[128,2]{0,1:T(2,128)} copy(f32[128,2]{1,0:T(8,128)} %reshape.145) | data formatting | bytes 2048
  118.3 2.3 %fusion.25 = f32[1,96,2048]{2,1,0:T(8,128)} fusion(bf16[96,2048]{1,0:T(8,128)(2,1)} %collective-permute-done.6, bf16[96,2048]{1,0:T(8,128)(2,1)S(1)} %collective-permute-done.3, f32[4,96,2048]{2,1,0:T(8,128)} %copy-done.1, s32[]{:T(128)S(6)} %select_n.41), kind=kLoop, calls=%fused_computation.44 | loop fusion | flops 786432 | bytes 2359300 | tf_op jit(solution)/shard_map/broadcast_in_dim | solution.py:123
  (29 shorter events, 6.2 us)
Async XLA Ops:
  0.6 32.5 %copy-start = (bf16[1,768,2048]{2,1,0:T(8,128)(2,1)S(1)}, bf16[1,768,2048]{2,1,0:T(8,128)(2,1)}, u32[]{:S(2)}) copy-start(bf16[1,768,2048]{2,1,0:T(8,128)(2,1)} %param.11) | copy-start | bytes 9437188
  6.9 25.0 %all-to-all-start = ((bf16[4,96,2176]{2,1,0:T(8,128)(2,1)}), bf16[4,96,2176]{2,1,0:T(8,128)(2,1)}, u32[]{:S(2)}, u32[]{:S(2)}) async-start(bf16[4,96,2176]{2,1,0:T(8,128)(2,1)} %bitcast.64), calls=%async_computation | async-start | bytes 3342336 | tf_op jit(solution)/shard_map/all_to_all | solution.py:87
  43.6 2.7 %copy-start.2 = (f32[4,2,96,2048]{3,2,1,0:T(8,128)}, f32[4,2,96,2048]{3,2,1,0:T(8,128)S(1)}, u32[]{:S(2)}) copy-start(f32[4,2,96,2048]{3,2,1,0:T(8,128)S(1)} %fusion.3) | copy-start | bytes 18874372
  47.8 3.8 %collective-permute-start = (bf16[4,96,2048]{2,1,0:T(8,128)(2,1)}, bf16[4,96,2048]{2,1,0:T(8,128)(2,1)}, u32[]{:S(2)}, u32[]{:S(2)}) collective-permute-start(bf16[4,96,2048]{2,1,0:T(8,128)(2,1)} %fusion.5), channel_id=1, source_target_pairs={{0,1},{1,0},{2,3},{3,2},{4,5},{5,4},{6,7},{7,6},{8,9},{9,8},{10,11... | collective-permute-start | bytes 4718600 | tf_op jit(solution)/shard_map/ppermute | solution.py:36
  54.4 1.6 %copy-start.1 = (f32[4,96,2048]{2,1,0:T(8,128)}, f32[4,96,2048]{2,1,0:T(8,128)S(1)}, u32[]{:S(2)}) copy-start(f32[4,96,2048]{2,1,0:T(8,128)S(1)} %bitcast_add_fusion) | copy-start | bytes 9437188
  56.9 2.7 %collective-permute-start.1 = (bf16[96,2048]{1,0:T(8,128)(2,1)}, bf16[96,2048]{1,0:T(8,128)(2,1)}, u32[]{:S(2)}, u32[]{:S(2)}) collective-permute-start(bf16[96,2048]{1,0:T(8,128)(2,1)} %get-tuple-element.20), channel_id=1, source_target_pairs={{0,2},{1,3},{8,10},{9,11},{16,18},{17,19},{24,26},{25,27}} | collective-permute-start | bytes 1179656 | tf_op jit(solution)/shard_map/ppermute | solution.py:44
  58.3 13.1 %collective-permute-start.4 = (bf16[96,2048]{1,0:T(8,128)(2,1)S(1)}, bf16[96,2048]{1,0:T(8,128)(2,1)}, u32[]{:S(2)}, u32[]{:S(2)}) collective-permute-start(bf16[96,2048]{1,0:T(8,128)(2,1)S(1)} %get-tuple-element.21), channel_id=1, source_target_pairs={{6,4},{7,5},{14,12},{15,13},{22,20},{23,21},{30,28},{31,29}} | collective-permute-start | bytes 1179656 | tf_op jit(solution)/shard_map/ppermute | solution.py:48
  61.6 21.9 %collective-permute-start.2 = (bf16[96,2048]{1,0:T(8,128)(2,1)}, bf16[96,2048]{1,0:T(8,128)(2,1)}, u32[]{:S(2)}, u32[]{:S(2)}) collective-permute-start(bf16[96,2048]{1,0:T(8,128)(2,1)} %fusion.22), channel_id=1, source_target_pairs={{0,2},{2,4},{1,3},{3,5},{8,10},{10,12},{9,11},{11,13},{16,18},{18,... | collective-permute-start | bytes 1179656 | tf_op jit(solution)/shard_map/ppermute | solution.py:44
  86.2 11.9 %collective-permute-start.5 = (bf16[96,2048]{1,0:T(8,128)(2,1)}, bf16[96,2048]{1,0:T(8,128)(2,1)}, u32[]{:S(2)}, u32[]{:S(2)}) collective-permute-start(bf16[96,2048]{1,0:T(8,128)(2,1)} %get-tuple-element.19), channel_id=1, source_target_pairs={{6,4},{4,2},{7,5},{5,3},{14,12},{12,10},{15,13},{13,11},{22,20},{2... | collective-permute-start | bytes 1179656 | tf_op jit(solution)/shard_map/ppermute | solution.py:48
  89.8 28.5 %collective-permute-start.3 = (bf16[96,2048]{1,0:T(8,128)(2,1)}, bf16[96,2048]{1,0:T(8,128)(2,1)S(1)}, u32[]{:S(2)}, u32[]{:S(2)}) collective-permute-start(bf16[96,2048]{1,0:T(8,128)(2,1)} %get-tuple-element.18), channel_id=1, source_target_pairs={{0,2},{2,4},{4,6},{1,3},{3,5},{5,7},{8,10},{10,12},{12,14},{9,11},... | collective-permute-start | bytes 1179656 | tf_op jit(solution)/shard_map/ppermute | solution.py:44
  100.2 18.2 %collective-permute-start.6 = (bf16[96,2048]{1,0:T(8,128)(2,1)}, bf16[96,2048]{1,0:T(8,128)(2,1)}, u32[]{:S(2)}, u32[]{:S(2)}) collective-permute-start(bf16[96,2048]{1,0:T(8,128)(2,1)} %fusion.21), channel_id=1, source_target_pairs={{6,4},{4,2},{2,0},{7,5},{5,3},{3,1},{14,12},{12,10},{10,8},{15,13}... | collective-permute-start | bytes 1179656 | tf_op jit(solution)/shard_map/ppermute | solution.py:48
  105.2 7.7 %all-to-all-start.1 = ((f32[4,1,96]{2,1,0:T(1,128)}), f32[4,1,96]{2,1,0:T(1,128)S(1)}, u32[]{:S(2)}, u32[]{:S(2)}) async-start(f32[4,1,96]{2,1,0:T(1,128)} %all_to_all.10), calls=%async_computation.1 | async-start | bytes 4096 | tf_op jit(solution)/shard_map/all_to_all | solution.py:118

commit v5 on v1

--- a/solution.py
+++ b/solution.py
@@ -67,9 +67,8 @@
     partial_grad = lax.dot_general(
         hidden, weighted, (((0,), (0,)), ((), ())), preferred_element_type=jnp.float32
     )
-    summed = lax.psum_scatter(
-        partial_grad.astype(jnp.bfloat16), "dp", scatter_dimension=0, tiled=True
-    )
+    partial_grad, rows = lax.optimization_barrier((partial_grad.astype(jnp.bfloat16), rows))
+    summed = lax.psum_scatter(partial_grad, "dp", scatter_dimension=0, tiled=True)
     grad_weight = summed.astype(jnp.float32)
 
     matrix = w_down[0]

time: 93.9 us -> 98.4 us (1.048)
  blocking collectives: 26 us -> 0 us
  waiting for transfers between devices: 32.1 us -> 46.8 us
  starting transfers between devices: 3.26 us -> 8.39 us
  other arithmetic: 3.13 us -> 7.64 us
  matrix products: 8.54 us -> 11.8 us
  local copies, waits for them, and re-layouts: 6.32 us -> 9.13 us
    all_to_all x1 -> x0, blocking collectives: 26 us -> none  [local(): lax.all_to_all(packed.reshape(experts, capacity, feature_count + lanes),...]
    all_to_all x0 -> x1, waiting for transfers between devices: none -> 18.6 us  [local(): lax.all_to_all(packed.reshape(experts, capacity, feature_count + lanes),...]
    all_to_all x0 -> x1, starting transfers between devices: none -> 5.16 us  [local(): lax.all_to_all(packed.reshape(experts, capacity, feature_count + lanes),...]
    reduce_scatter x1, waiting for transfers between devices: 27.6 us -> 23.6 us  [local(): lax.psum_scatter(partial_grad, 'dp', scatter_dimension=0, tiled=True)]
    slice x0 -> x1, local copies, waits for them, and re-layouts: none -> 2.81 us  [local(): rows = arrived[:, :feature_count]]
    convert_element_type x0 -> x1, other arithmetic: none -> 2.42 us  [local(): hidden = (gate_pre * sigmoid_gate * up_pre).astype(jnp.bfloat16)]
    dot_general x1, matrix products: 2.98 us -> 4.82 us  [local(): lax.dot_general(rows, matrix, (((1,), (1,)), ((), ())), preferred_element...]
    dot_general x1, matrix products: 3.57 us -> 4.98 us  [local(): lax.dot_general(hidden, weighted, (((0,), (0,)), ((), ())), preferred_ele...]
  transfers between devices with their start and end apart: 2 -> 3, of which waited for: 2 -> 3; matrix products, arithmetic and copies ran while one was open for 4% -> 12% of each run, Pallas kernels for 0% -> 0%
where the time goes in v5:
time: 98.4 us; the launch traced here: 97.9 us
  waiting for transfers between devices  46.8 us (48%)
  between operations  14.2 us (14%)
  matrix products  11.8 us (12%)
  local copies, waits for them, and re-layouts  9.13 us (9%)
  starting transfers between devices  8.39 us (9%)
  other arithmetic  7.64 us (8%)
    reduce_scatter x1, waiting for transfers between devices, local(): lax.psum_scatter(partial_grad, 'dp', scatter_dimension=0, tiled=True)  23.6 us
    all_to_all x1, waiting for transfers between devices, local(): lax.all_to_all(packed.reshape(experts, capacity, feature_count + lanes),...  18.6 us
    all_to_all x1, starting transfers between devices, local(): lax.all_to_all(packed.reshape(experts, capacity, feature_count + lanes),...  5.16 us
    dot_general x1, matrix products, local(): lax.dot_general(hidden, weighted, (((0,), (0,)), ((), ())), preferred_ele...  4.98 us
    dot_general x1, matrix products, local(): lax.dot_general(rows, matrix, (((1,), (1,)), ((), ())), preferred_element...  4.82 us
    all_to_all x1, waiting for transfers between devices, local(): lax.all_to_all(slot_grad.reshape(experts, capacity), 'expert', split_axis...  4.52 us
    all_to_all x1, starting transfers between devices, local(): lax.all_to_all(slot_grad.reshape(experts, capacity), 'expert', split_axis...  3.22 us
    slice x1, local copies, waits for them, and re-layouts, local(): rows = arrived[:, :feature_count]  2.81 us
  transfers between devices with their start and end apart: 3, of which 3 were waited for; matrix products, arithmetic and copies ran while one was open for 12% of the time, Pallas kernels for 0%

profile of v5, /device:TPU:0, one launch (start us, length us, event | category | flops | bytes accessed | tf_op | source)
XLA Modules:
  0.0 97.9 jit_solution(7624141560803327072)
XLA Ops:
  7.2 0.9 copy.23
  8.1 0.1 eq.35
  8.3 0.2 fusion.13
  8.5 0.1 convert_element_type.84
  8.7 0.1 copy.25
  8.7 0.1 fusion.14
  8.8 0.8 copy.26
  9.6 0.1 reshape.130
  9.7 1.6 %convolution_convert_fusion.1 = bf16[384,2048]{1,0:T(8,128)(2,1)S(1)} fusion(pred[384,128]{1,0:T(8,128)(4,1)S(1)} %fusion.14, bf16[128,2048]{1,0:T(8,128)(2,1)} %param.6), kind=kOutput, calls=%fused_computation.5 | convolution fusion | flops 202113024 | bytes 2146304 | tf_op jit(solution)/shard_map/dot_general | solution.py:42
  11.3 0.2 convolution_convert_fusion.2
  11.5 1.3 %pad_maximum_fusion = bf16[384,2176]{1,0:T(8,128)(2,1)} fusion(bf16[384,128]{1,0:T(8,128)(2,1)S(1)} %convolution_convert_fusion.2, bf16[384,2048]{1,0:T(8,128)(2,1)S(1)} %convolution_convert_fusion.1), kind=kLoop, calls=%fused_computation.10 | loop fusion | flops 3342336 | bytes 3342336 | tf_op jit(solution)/shard_map/concatenate | solution.py:50
  12.9 5.2 %all-to-all-start = ((bf16[4,96,2176]{2,1,0:T(8,128)(2,1)}), bf16[4,96,2176]{2,1,0:T(8,128)(2,1)}, u32[]{:S(2)}, u32[]{:S(2)}) async-start(bf16[4,96,2176]{2,1,0:T(8,128)(2,1)} %bitcast.27), calls=%async_computation | async-start | bytes 3342336 | tf_op jit(solution)/shard_map/all_to_all | solution.py:51
  18.0 2.4 %fusion.3 = bf16[384,768]{1,0:T(8,128)(2,1)} fusion(bf16[1,1,4,96,768]{4,3,2,1,0:T(8,128)(2,1)} %param.10, bf16[1,1,4,96,768]{4,3,2,1,0:T(8,128)(2,1)} %param.9), kind=kLoop, calls=%fused_computation.14 | loop fusion | flops 2359296 | bytes 1769472 | tf_op jit(solution)/shard_map/convert_element_type | solution.py:65
  20.5 18.6 %all-to-all-done = bf16[4,96,2176]{2,1,0:T(8,128)(2,1)} async-done(((bf16[4,96,2176]{2,1,0:T(8,128)(2,1)}), bf16[4,96,2176]{2,1,0:T(8,128)(2,1)}, u32[]{:S(2)}, u32[]{:S(2)}) %all-to-all-start) | async-done | bytes 1671200 | tf_op jit(solution)/shard_map/all_to_all | solution.py:51
  39.1 0.9 slice_convert_fusion
  40.0 2.8 %slice.26 = bf16[384,2048]{1,0:T(8,128)(2,1)} slice(bf16[384,2176]{1,0:T(8,128)(2,1)} %bitcast.4), slice={[0:384], [0:2048]} | slice | bytes 3145728 | tf_op jit(solution)/shard_map/slice | solution.py:58
  42.8 0.3 fusion.15
  43.1 5.0 %convolution_convert_fusion = bf16[768,2048]{1,0:T(8,128)(2,1)} fusion(bf16[384,768]{1,0:T(8,128)(2,1)S(1)} %copy-done.1, f32[384]{0:T(512)S(1)} %fusion.15, bf16[384,2176]{1,0:T(8,128)(2,1)} %bitcast.4), kind=kOutput, calls=%fused_computation.1 | convolution fusion | flops 1211891712 | bytes 5309952 | tf_op jit(solution)/shard_map/dot_general | solution.py:67
  48.1 0.0 reduce-scatter.2.cloned.1.call-update
  48.1 0.1 mul.92
  48.3 4.8 %fusion.12 = (bf16[384,768]{1,0:T(8,128)(2,1)}, bf16[384,768]{1,0:T(8,128)(2,1)}, f32[384]{0:T(512)S(1)}) fusion(bf16[1,1,4,96,768]{4,3,2,1,0:T(8,128)(2,1)} %param.9, f32[384]{0:T(512)S(1)} %fusion.15, bf16[1,1,4,96,768]{4,3,2,1,0:T(8,128)(2,1)} %param.10, bf16[384,768]{1,0:T(8,128)(2,1)} %fusion.3, bf16[384,2048]{1,0:T(8,128)(2,1)} %slice.26, ...), kind=kOutput, calls=%fused_computation.23 | convolution fusion | flops 1213562496 | bytes 7670784 | tf_op jit(solution)/shard_map/dot_general | solution.py:75
  53.1 0.7 all_to_all.10
  53.8 3.2 %all-to-all-start.1 = ((f32[4,1,96]{2,1,0:T(1,128)}), f32[4,1,96]{2,1,0:T(1,128)S(1)}, u32[]{:S(2)}, u32[]{:S(2)}) async-start(f32[4,1,96]{2,1,0:T(1,128)} %all_to_all.10), calls=%async_computation.2 | async-start | bytes 4096 | tf_op jit(solution)/shard_map/all_to_all | solution.py:84
  57.0 4.5 %all-to-all-done.1 = f32[4,1,96]{2,1,0:T(1,128)S(1)} async-done(((f32[4,1,96]{2,1,0:T(1,128)}), f32[4,1,96]{2,1,0:T(1,128)S(1)}, u32[]{:S(2)}, u32[]{:S(2)}) %all-to-all-start.1) | async-done | bytes 1568 | tf_op jit(solution)/shard_map/all_to_all | solution.py:84
  61.5 0.5 broadcast.69
  62.0 0.7 reduce.5
  62.7 0.1 reshape.135
  62.8 1.9 %gather_fusion = f32[256]{0:T(256)S(1)} fusion(f32[384]{0:T(512)S(1)} %reshape.135, s32[1024]{0:T(1024)S(1)} %pad_clamp_fusion), kind=kCustom, calls=%fused_computation | custom fusion | bytes 3072 | tf_op jit(solution)/shard_map/gather | solution.py:87
  64.7 0.1 reshape.136
  64.9 0.6 copy.28
  65.5 23.6 %reduce-scatter.2.cloned.1.call-done = bf16[96,2048]{1,0:T(8,128)(2,1)} async-done(((bf16[768,2048]{1,0:T(8,128)(2,1)}), bf16[96,2048]{1,0:T(8,128)(2,1)}) %reduce-scatter.2.cloned.1.call-update) | async-done | bytes 393232 | tf_op jit(solution)/shard_map/reduce_scatter | solution.py:71
  89.1 1.9 %bitcast_convert_fusion = f32[1,96,2048]{2,1,0:T(8,128)} fusion(bf16[96,2048]{1,0:T(8,128)(2,1)} %reduce-scatter.2.cloned.1.call-done), kind=kLoop, calls=%fused_computation.28 | loop fusion | flops 196608 | bytes 1179648 | tf_op jit(solution)/shard_map/broadcast_in_dim | solution.py:89
  (11 shorter events, 0.1 us)
Async XLA Ops:
  7.2 41.1 %copy-start = (bf16[1,768,2048]{2,1,0:T(8,128)(2,1)S(1)}, bf16[1,768,2048]{2,1,0:T(8,128)(2,1)}, u32[]{:S(2)}) copy-start(bf16[1,768,2048]{2,1,0:T(8,128)(2,1)} %param.11) | copy-start | bytes 9437188
  12.9 26.2 %all-to-all-start = ((bf16[4,96,2176]{2,1,0:T(8,128)(2,1)}), bf16[4,96,2176]{2,1,0:T(8,128)(2,1)}, u32[]{:S(2)}, u32[]{:S(2)}) async-start(bf16[4,96,2176]{2,1,0:T(8,128)(2,1)} %bitcast.27), calls=%async_computation | async-start | bytes 3342336 | tf_op jit(solution)/shard_map/all_to_all | solution.py:51
  18.0 71.1 %reduce-scatter.2.cloned.1.call-start = ((), (), s32[]{:S(2)}) async-start(), calls=%async_computation.3 | async-start | bytes 3538944 | tf_op jit(solution)/shard_map/reduce_scatter | solution.py:71
  40.0 3.1 %copy-start.1 = (bf16[384,768]{1,0:T(8,128)(2,1)S(1)}, bf16[384,768]{1,0:T(8,128)(2,1)}, u32[]{:S(2)}) copy-start(bf16[384,768]{1,0:T(8,128)(2,1)} %fusion.3) | copy-start | bytes 1769476
  53.8 7.8 %all-to-all-start.1 = ((f32[4,1,96]{2,1,0:T(1,128)}), f32[4,1,96]{2,1,0:T(1,128)S(1)}, u32[]{:S(2)}, u32[]{:S(2)}) async-start(f32[4,1,96]{2,1,0:T(1,128)} %all_to_all.10), calls=%async_computation.2 | async-start | bytes 4096 | tf_op jit(solution)/shard_map/all_to_all | solution.py:84
Sparse Core Ops, SparseCore 0:
  48.2 40.8 reduce-scatter.1

commit v6 on v5

--- a/solution.py
+++ b/solution.py
@@ -67,7 +67,10 @@
     partial_grad = lax.dot_general(
         hidden, weighted, (((0,), (0,)), ((), ())), preferred_element_type=jnp.float32
     )
-    partial_grad, rows = lax.optimization_barrier((partial_grad.astype(jnp.bfloat16), rows))
+    partial_grad, arrived = lax.optimization_barrier(
+        (partial_grad.astype(jnp.bfloat16), arrived)
+    )
+    rows = arrived[:, :feature_count]
     summed = lax.psum_scatter(partial_grad, "dp", scatter_dimension=0, tiled=True)
     grad_weight = summed.astype(jnp.float32)
 

time: 98.4 us -> 95.7 us (0.973)
  local copies, waits for them, and re-layouts: 9.13 us -> 6.31 us
    slice x1 -> x0, local copies, waits for them, and re-layouts: 2.81 us -> none  [local(): rows = arrived[:, :feature_count]]
    unnamed x7 -> x5, local copies, waits for them, and re-layouts: 2.38 us -> 2.37 us
where the time goes in v6:
time: 95.7 us; the launch traced here: 95.3 us
  waiting for transfers between devices  46.7 us (49%)
  between operations  14.2 us (15%)
  matrix products  12 us (13%)
  starting transfers between devices  8.39 us (9%)
  other arithmetic  7.64 us (8%)
  local copies, waits for them, and re-layouts  6.31 us (7%)
    reduce_scatter x1, waiting for transfers between devices, local(): lax.psum_scatter(partial_grad, 'dp', scatter_dimension=0, tiled=True)  23.5 us
    all_to_all x1, waiting for transfers between devices, local(): lax.all_to_all(packed.reshape(experts, capacity, feature_count + lanes),...  18.6 us
    dot_general x1, matrix products, local(): lax.dot_general(hidden, weighted, (((0,), (0,)), ((), ())), preferred_ele...  5.17 us
    all_to_all x1, starting transfers between devices, local(): lax.all_to_all(packed.reshape(experts, capacity, feature_count + lanes),...  5.16 us
    dot_general x1, matrix products, local(): lax.dot_general(rows, matrix, (((1,), (1,)), ((), ())), preferred_element...  4.86 us
    all_to_all x1, waiting for transfers between devices, local(): lax.all_to_all(slot_grad.reshape(experts, capacity), 'expert', split_axis...  4.52 us
    all_to_all x1, starting transfers between devices, local(): lax.all_to_all(slot_grad.reshape(experts, capacity), 'expert', split_axis...  3.22 us
    convert_element_type x1, other arithmetic, local(): hidden = (gate_pre * sigmoid_gate * up_pre).astype(jnp.bfloat16)  2.42 us
  transfers between devices with their start and end apart: 3, of which 3 were waited for; matrix products, arithmetic and copies ran while one was open for 12% of the time, Pallas kernels for 0%

profile of v6, /device:TPU:0, one launch (start us, length us, event | category | flops | bytes accessed | tf_op | source)
XLA Modules:
  0.0 95.3 jit_solution(3559584656054569072)
XLA Ops:
  7.2 0.0 copy-start
  7.2 0.9 copy.23
  8.1 0.1 eq.35
  8.3 0.2 fusion.15
  8.5 0.1 convert_element_type.84
  8.7 0.1 copy.25
  8.7 0.1 fusion.16
  8.8 0.8 copy.26
  9.6 0.1 reshape.130
  9.7 1.6 %convolution_convert_fusion.1 = bf16[384,2048]{1,0:T(8,128)(2,1)S(1)} fusion(pred[384,128]{1,0:T(8,128)(4,1)S(1)} %fusion.16, bf16[128,2048]{1,0:T(8,128)(2,1)} %param.6), kind=kOutput, calls=%fused_computation.5 | convolution fusion | flops 202113024 | bytes 2146304 | tf_op jit(solution)/shard_map/dot_general | solution.py:42
  11.3 0.2 convolution_convert_fusion.2
  11.5 1.3 %pad_maximum_fusion = bf16[384,2176]{1,0:T(8,128)(2,1)} fusion(bf16[384,128]{1,0:T(8,128)(2,1)S(1)} %convolution_convert_fusion.2, bf16[384,2048]{1,0:T(8,128)(2,1)S(1)} %convolution_convert_fusion.1), kind=kLoop, calls=%fused_computation.10 | loop fusion | flops 3342336 | bytes 3342336 | tf_op jit(solution)/shard_map/concatenate | solution.py:50
  12.9 5.2 %all-to-all-start = ((bf16[4,96,2176]{2,1,0:T(8,128)(2,1)}), bf16[4,96,2176]{2,1,0:T(8,128)(2,1)}, u32[]{:S(2)}, u32[]{:S(2)}) async-start(bf16[4,96,2176]{2,1,0:T(8,128)(2,1)} %bitcast.26), calls=%async_computation | async-start | bytes 3342336 | tf_op jit(solution)/shard_map/all_to_all | solution.py:51
  18.0 2.4 %fusion.5 = bf16[384,768]{1,0:T(8,128)(2,1)} fusion(bf16[1,1,4,96,768]{4,3,2,1,0:T(8,128)(2,1)} %param.10, bf16[1,1,4,96,768]{4,3,2,1,0:T(8,128)(2,1)} %param.9), kind=kLoop, calls=%fused_computation.16 | loop fusion | flops 2359296 | bytes 1769472 | tf_op jit(solution)/shard_map/convert_element_type | solution.py:65
  20.5 18.6 %all-to-all-done = bf16[4,96,2176]{2,1,0:T(8,128)(2,1)} async-done(((bf16[4,96,2176]{2,1,0:T(8,128)(2,1)}), bf16[4,96,2176]{2,1,0:T(8,128)(2,1)}, u32[]{:S(2)}, u32[]{:S(2)}) %all-to-all-start) | async-done | bytes 1671200 | tf_op jit(solution)/shard_map/all_to_all | solution.py:51
  39.1 0.9 slice_convert_fusion
  40.0 0.3 fusion.17
  40.3 5.2 %convolution_convert_fusion = bf16[768,2048]{1,0:T(8,128)(2,1)} fusion(bf16[384,768]{1,0:T(8,128)(2,1)} %fusion.5, bf16[384,2176]{1,0:T(8,128)(2,1)} %bitcast.4, f32[384]{0:T(512)S(1)} %fusion.17), kind=kOutput, calls=%fused_computation.1 | convolution fusion | flops 1211891712 | bytes 5309952 | tf_op jit(solution)/shard_map/dot_general | solution.py:67
  45.4 0.0 reduce-scatter.2.cloned.1.call-update
  45.5 0.1 mul.92
  45.6 4.9 %fusion.14 = (bf16[384,768]{1,0:T(8,128)(2,1)}, bf16[384,768]{1,0:T(8,128)(2,1)}, f32[384]{0:T(512)S(1)}) fusion(bf16[1,1,4,96,768]{4,3,2,1,0:T(8,128)(2,1)} %param.9, f32[384]{0:T(512)S(1)} %fusion.17, bf16[1,1,4,96,768]{4,3,2,1,0:T(8,128)(2,1)} %param.10, bf16[384,768]{1,0:T(8,128)(2,1)} %fusion.5, bf16[1,768,2048]{2,1,0:T(8,128)(2,1)S(1)} %copy-done, ...), kind=kOutput, calls=%fused_computation.25 | convolution fusion | flops 1213562496 | bytes 7670784 | tf_op jit(solution)/shard_map/dot_general | solution.py:78
  50.5 0.7 all_to_all.10
  51.2 3.2 %all-to-all-start.1 = ((f32[4,1,96]{2,1,0:T(1,128)}), f32[4,1,96]{2,1,0:T(1,128)S(1)}, u32[]{:S(2)}, u32[]{:S(2)}) async-start(f32[4,1,96]{2,1,0:T(1,128)} %all_to_all.10), calls=%async_computation.2 | async-start | bytes 4096 | tf_op jit(solution)/shard_map/all_to_all | solution.py:87
  54.4 4.5 %all-to-all-done.1 = f32[4,1,96]{2,1,0:T(1,128)S(1)} async-done(((f32[4,1,96]{2,1,0:T(1,128)}), f32[4,1,96]{2,1,0:T(1,128)S(1)}, u32[]{:S(2)}, u32[]{:S(2)}) %all-to-all-start.1) | async-done | bytes 1568 | tf_op jit(solution)/shard_map/all_to_all | solution.py:87
  58.9 0.5 broadcast.69
  59.4 0.7 reduce.5
  60.1 0.1 reshape.135
  60.2 1.9 %gather_fusion = f32[256]{0:T(256)S(1)} fusion(f32[384]{0:T(512)S(1)} %reshape.135, s32[1024]{0:T(1024)S(1)} %pad_clamp_fusion), kind=kCustom, calls=%fused_computation | custom fusion | bytes 3072 | tf_op jit(solution)/shard_map/gather | solution.py:90
  62.1 0.1 reshape.136
  62.3 0.6 copy.28
  62.9 23.5 %reduce-scatter.2.cloned.1.call-done = bf16[96,2048]{1,0:T(8,128)(2,1)} async-done(((bf16[768,2048]{1,0:T(8,128)(2,1)}), bf16[96,2048]{1,0:T(8,128)(2,1)}) %reduce-scatter.2.cloned.1.call-update) | async-done | bytes 393232 | tf_op jit(solution)/shard_map/reduce_scatter | solution.py:74
  86.5 1.9 %bitcast_convert_fusion = f32[1,96,2048]{2,1,0:T(8,128)} fusion(bf16[96,2048]{1,0:T(8,128)(2,1)} %reduce-scatter.2.cloned.1.call-done), kind=kLoop, calls=%fused_computation.30 | loop fusion | flops 196608 | bytes 1179648 | tf_op jit(solution)/shard_map/broadcast_in_dim | solution.py:92
  (8 shorter events, 0.0 us)
Async XLA Ops:
  7.2 38.5 %copy-start = (bf16[1,768,2048]{2,1,0:T(8,128)(2,1)S(1)}, bf16[1,768,2048]{2,1,0:T(8,128)(2,1)}, u32[]{:S(2)}) copy-start(bf16[1,768,2048]{2,1,0:T(8,128)(2,1)} %param.11) | copy-start | bytes 9437188
  12.9 26.2 %all-to-all-start = ((bf16[4,96,2176]{2,1,0:T(8,128)(2,1)}), bf16[4,96,2176]{2,1,0:T(8,128)(2,1)}, u32[]{:S(2)}, u32[]{:S(2)}) async-start(bf16[4,96,2176]{2,1,0:T(8,128)(2,1)} %bitcast.26), calls=%async_computation | async-start | bytes 3342336 | tf_op jit(solution)/shard_map/all_to_all | solution.py:51
  18.0 68.4 %reduce-scatter.2.cloned.1.call-start = ((), (), s32[]{:S(2)}) async-start(), calls=%async_computation.3 | async-start | bytes 3538944 | tf_op jit(solution)/shard_map/reduce_scatter | solution.py:74
  51.2 7.8 %all-to-all-start.1 = ((f32[4,1,96]{2,1,0:T(1,128)}), f32[4,1,96]{2,1,0:T(1,128)S(1)}, u32[]{:S(2)}, u32[]{:S(2)}) async-start(f32[4,1,96]{2,1,0:T(1,128)} %all_to_all.10), calls=%async_computation.2 | async-start | bytes 4096 | tf_op jit(solution)/shard_map/all_to_all | solution.py:87
Sparse Core Ops, SparseCore 0:
  45.6 40.8 reduce-scatter.1

commit v7 on v5

--- a/solution.py
+++ b/solution.py
@@ -2,6 +2,8 @@
 import jax.numpy as jnp
 from jax import lax
 from jax.sharding import PartitionSpec as P
+from jax.experimental import pallas as pl
+from jax.experimental.pallas import tpu as pltpu
 
 
 def round_bf16(value):
@@ -14,6 +16,43 @@
     middle = round_bf16(rest)
     low = rest - middle
     return jnp.stack([high, middle, low], axis=-1).astype(jnp.bfloat16)
+
+
+def partial_kernel(arrived_ref, gate_ref, up_ref, partial_ref, hidden_ref):
+    features = partial_ref.shape[1]
+    gate = gate_ref[...].astype(jnp.float32)
+    sigmoid_gate = 1.0 / (1.0 + jnp.exp(-gate))
+    hidden = (gate * sigmoid_gate * up_ref[...].astype(jnp.float32)).astype(jnp.bfloat16)
+    hidden_ref[...] = hidden
+    hidden_t = jnp.transpose(hidden.astype(jnp.float32)).astype(jnp.bfloat16)
+    got = arrived_ref[:, features:features + 128].astype(jnp.float32)
+    weights = (got[:, 0:1] + got[:, 1:2]) + got[:, 2:3]
+    tile = 512 if features % 512 == 0 else features
+    for start in range(0, features, tile):
+        rows = arrived_ref[:, start:start + tile].astype(jnp.float32)
+        weighted = (weights * rows).astype(jnp.bfloat16)
+        partial_ref[:, start:start + tile] = jnp.dot(
+            hidden_t, weighted, preferred_element_type=jnp.float32
+        ).astype(jnp.bfloat16)
+
+
+def weighted_partial(arrived, gate, up, features):
+    slots, hidden_count = gate.shape
+    vmem = pl.BlockSpec(memory_space=pltpu.VMEM)
+    flops = 2 * slots * hidden_count * features
+    moved = 2 * (arrived.size + 2 * gate.size + hidden_count * features + gate.size)
+    return pl.pallas_call(
+        partial_kernel,
+        out_shape=(
+            jax.ShapeDtypeStruct((hidden_count, features), jnp.bfloat16),
+            jax.ShapeDtypeStruct((slots, hidden_count), jnp.bfloat16),
+        ),
+        in_specs=[vmem, vmem, vmem],
+        out_specs=(vmem, vmem),
+        cost_estimate=pl.CostEstimate(
+            flops=flops, bytes_accessed=moved, transcendentals=gate.size
+        ),
+    )(arrived, gate, up)
 
 
 def local(out_grad, combine_weight, routes, saved_gate, saved_up, w_down):
@@ -59,16 +98,13 @@
     got = arrived[:, feature_count:feature_count + 3].astype(jnp.float32)
     weights = (got[:, 0] + got[:, 1]) + got[:, 2]
 
-    gate_pre = saved_gate.reshape(-1, hidden_count).astype(jnp.float32)
-    up_pre = saved_up.reshape(-1, hidden_count).astype(jnp.float32)
+    gate_bf = saved_gate.reshape(-1, hidden_count)
+    up_bf = saved_up.reshape(-1, hidden_count)
+    partial_grad, hidden = weighted_partial(arrived, gate_bf, up_bf, feature_count)
+    summed = lax.psum_scatter(partial_grad, "dp", scatter_dimension=0, tiled=True)
+    gate_pre = gate_bf.astype(jnp.float32)
+    up_pre = up_bf.astype(jnp.float32)
     sigmoid_gate = jax.nn.sigmoid(gate_pre)
-    hidden = (gate_pre * sigmoid_gate * up_pre).astype(jnp.bfloat16)
-    weighted = (weights[:, None] * rows.astype(jnp.float32)).astype(jnp.bfloat16)
-    partial_grad = lax.dot_general(
-        hidden, weighted, (((0,), (0,)), ((), ())), preferred_element_type=jnp.float32
-    )
-    partial_grad, rows = lax.optimization_barrier((partial_grad.astype(jnp.bfloat16), rows))
-    summed = lax.psum_scatter(partial_grad, "dp", scatter_dimension=0, tiled=True)
     grad_weight = summed.astype(jnp.float32)
 
     matrix = w_down[0]

time: 98.4 us -> 92.7 us (0.942)
  blocking collectives: 0 us -> 26 us
  waiting for transfers between devices: 46.8 us -> 26.1 us
  Pallas kernels: 0 us -> 5.63 us
  starting transfers between devices: 8.39 us -> 3.26 us
  matrix products: 11.8 us -> 6.85 us
  other arithmetic: 7.64 us -> 4.03 us
  local copies, waits for them, and re-layouts: 9.13 us -> 6.32 us
    all_to_all x0 -> x1, blocking collectives: none -> 26 us  [local(): lax.all_to_all(packed.reshape(experts, capacity, feature_count + lanes),...]
    all_to_all x1 -> x0, waiting for transfers between devices: 18.6 us -> none  [local(): lax.all_to_all(packed.reshape(experts, capacity, feature_count + lanes),...]
    pallas_call x0 -> x1, Pallas kernels: none -> 5.63 us  [weighted_partial(): pl.pallas_call(partial_kernel, out_shape=(jax.ShapeDtypeStruct((hidden_co...]
    all_to_all x1 -> x0, starting transfers between devices: 5.16 us -> none  [local(): lax.all_to_all(packed.reshape(experts, capacity, feature_count + lanes),...]
    dot_general x1 -> x0, matrix products: 4.98 us -> none  [local(): lax.dot_general(hidden, weighted, (((0,), (0,)), ((), ())), preferred_ele...]
    slice x1 -> x0, local copies, waits for them, and re-layouts: 2.81 us -> none  [local(): rows = arrived[:, :feature_count]]
    convert_element_type x1 -> x0, other arithmetic: 2.42 us -> none  [local(): hidden = (gate_pre * sigmoid_gate * up_pre).astype(jnp.bfloat16)]
    reduce_scatter x1, waiting for transfers between devices: 23.6 us -> 21.5 us  [local(): lax.psum_scatter(partial_grad, 'dp', scatter_dimension=0, tiled=True)]
  transfers between devices with their start and end apart: 3 -> 2, of which waited for: 3 -> 2; matrix products, arithmetic and copies ran while one was open for 12% -> 11% of each run, Pallas kernels for 0% -> 0%
where the time goes in v7:
time: 92.7 us; the launch traced here: 92.3 us
  waiting for transfers between devices  26.1 us (28%)
  blocking collectives  26 us (28%)
  between operations  14.2 us (15%)
  matrix products  6.85 us (7%)
  local copies, waits for them, and re-layouts  6.32 us (7%)
  Pallas kernels  5.63 us (6%)
  other arithmetic  4.03 us (4%)
  starting transfers between devices  3.26 us (4%)
    all_to_all x1, blocking collectives, local(): lax.all_to_all(packed.reshape(experts, capacity, feature_count + lanes),...  26 us
    reduce_scatter x1, waiting for transfers between devices, local(): lax.psum_scatter(partial_grad, 'dp', scatter_dimension=0, tiled=True)  21.5 us
    pallas_call x1, Pallas kernels, weighted_partial(): pl.pallas_call(partial_kernel, out_shape=(jax.ShapeDtypeStruct((hidden_co...  5.63 us
    dot_general x1, matrix products, local(): lax.dot_general(rows, matrix, (((1,), (1,)), ((), ())), preferred_element...  4.86 us
    all_to_all x1, waiting for transfers between devices, local(): lax.all_to_all(slot_grad.reshape(experts, capacity), 'expert', split_axis...  4.52 us
    all_to_all x1, starting transfers between devices, local(): lax.all_to_all(slot_grad.reshape(experts, capacity), 'expert', split_axis...  3.22 us
    unnamed x5, local copies, waits for them, and re-layouts  2.37 us
    gather x1, local copies, waits for them, and re-layouts, local(): grad_combine = returned.reshape(-1)[position].reshape(tok_rows, route_count)  1.95 us
  transfers between devices with their start and end apart: 2, of which 2 were waited for; matrix products, arithmetic and copies ran while one was open for 11% of the time, Pallas kernels for 0%

profile of v7, /device:TPU:0, one launch (start us, length us, event | category | flops | bytes accessed | tf_op | source)
XLA Modules:
  0.0 92.3 jit_solution(14032224288375417921)
XLA Ops:
  7.2 0.0 copy-start
  7.2 0.0 reduce-scatter.2.cloned.1.call-start
  7.2 0.9 %copy.17 = s32[128,2]{1,0:T(8,128)S(1)} copy(s32[128,2]{0,1:T(2,128)} %param.8) | data formatting | bytes 2048 | tf_op args[2]
  8.2 0.1 eq.35
  8.3 0.2 fusion.11
  8.5 0.8 copy.20
  9.3 0.1 reshape.130
  9.5 0.1 convert_element_type.61
  9.6 0.1 copy.19
  9.7 0.1 fusion.12
  9.8 1.6 %convolution_convert_fusion = bf16[384,2048]{1,0:T(8,128)(2,1)S(1)} fusion(pred[384,128]{1,0:T(8,128)(4,1)S(1)} %fusion.12, bf16[128,2048]{1,0:T(8,128)(2,1)} %param.6), kind=kOutput, calls=%fused_computation.3 | convolution fusion | flops 202113024 | bytes 2146304 | tf_op jit(solution)/shard_map/dot_general | solution.py:81
  11.4 0.2 convolution_convert_fusion.1
  11.6 0.1 pad_maximum_fusion
  11.7 26.0 %all_to_all.14 = bf16[4,96,2176]{2,1,0:T(8,128)(2,1)} all-to-all(bf16[4,96,2176]{2,1,0:T(8,128)(2,1)S(1)} %bitcast.21), channel_id=1, replica_groups=mesh['expert'=4,'dp'=8] {'expert'}, dimensions={0} | all-to-all | bytes 3342336 | tf_op jit(solution)/shard_map/all_to_all | solution.py:90
  37.7 5.6 %shard_map.93 = (bf16[768,2048]{1,0:T(8,128)(2,1)}, bf16[384,768]{1,0:T(8,128)(2,1)}) custom-call(bf16[384,2176]{1,0:T(8,128)(2,1)} %bitcast.22, bf16[384,768]{1,0:T(8,128)(2,1)} %bitcast.27, bf16[384,768]{1,0:T(8,128)(2,1)} %bitcast.28), custom_call_target="tpu_custom_call" | custom-call | flops 1207959552 | bytes 6586368 | tf_op jit(solution)/shard_map/pallas_call | solution.py:44
  43.3 0.0 reduce-scatter.2.cloned.1.call-update
  43.4 0.1 mul.74
  43.5 0.9 slice_convert_fusion
  44.4 0.3 fusion.13
  44.7 0.0 copy-done
  44.7 4.9 %fusion.10 = (bf16[384,768]{1,0:T(8,128)(2,1)}, bf16[384,768]{1,0:T(8,128)(2,1)}, f32[384]{0:T(512)S(1)}) fusion(f32[384]{0:T(512)S(1)} %fusion.13, bf16[1,1,4,96,768]{4,3,2,1,0:T(8,128)(2,1)} %param.9, bf16[1,1,4,96,768]{4,3,2,1,0:T(8,128)(2,1)} %param.10, bf16[384,768]{1,0:T(8,128)(2,1)} %get-tuple-element.7, bf16[1,768,2048]{2,1,0:T(8,128)(2,1)S(1)} %copy-done, ...), kind=kOutput, calls=%fused_computation.16 | convolution fusion | flops 1213562496 | bytes 7670784 | tf_op jit(solution)/shard_map/dot_general | solution.py:111
  49.5 0.7 all_to_all.10
  50.2 3.2 %all-to-all-start.1 = ((f32[4,1,96]{2,1,0:T(1,128)}), f32[4,1,96]{2,1,0:T(1,128)S(1)}, u32[]{:S(2)}, u32[]{:S(2)}) async-start(f32[4,1,96]{2,1,0:T(1,128)} %all_to_all.10), calls=%async_computation.2 | async-start | bytes 4096 | tf_op jit(solution)/shard_map/all_to_all | solution.py:120
  53.4 4.5 %all-to-all-done.1 = f32[4,1,96]{2,1,0:T(1,128)S(1)} async-done(((f32[4,1,96]{2,1,0:T(1,128)}), f32[4,1,96]{2,1,0:T(1,128)S(1)}, u32[]{:S(2)}, u32[]{:S(2)}) %all-to-all-start.1) | async-done | bytes 1568 | tf_op jit(solution)/shard_map/all_to_all | solution.py:120
  58.0 0.5 broadcast.68
  58.5 0.7 reduce.5
  59.1 0.1 reshape.137
  59.2 1.9 %gather_fusion = f32[256]{0:T(256)S(1)} fusion(f32[384]{0:T(512)S(1)} %reshape.137, s32[1024]{0:T(1024)S(1)} %pad_clamp_fusion), kind=kCustom, calls=%fused_computation | custom fusion | bytes 3072 | tf_op jit(solution)/shard_map/gather | solution.py:123
  61.2 0.1 reshape.138
  61.3 0.6 copy.22
  62.0 21.5 %reduce-scatter.2.cloned.1.call-done = bf16[96,2048]{1,0:T(8,128)(2,1)} async-done(((bf16[768,2048]{1,0:T(8,128)(2,1)}), bf16[96,2048]{1,0:T(8,128)(2,1)}) %reduce-scatter.2.cloned.1.call-update) | async-done | bytes 393232 | tf_op jit(solution)/shard_map/reduce_scatter | solution.py:104
  83.5 1.9 %bitcast_convert_fusion = f32[1,96,2048]{2,1,0:T(8,128)} fusion(bf16[96,2048]{1,0:T(8,128)(2,1)} %reduce-scatter.2.cloned.1.call-done), kind=kLoop, calls=%fused_computation.21 | loop fusion | flops 196608 | bytes 1179648 | tf_op jit(solution)/shard_map/broadcast_in_dim | solution.py:125
  (6 shorter events, 0.0 us)
Async XLA Ops:
  7.2 37.5 %copy-start = (bf16[1,768,2048]{2,1,0:T(8,128)(2,1)S(1)}, bf16[1,768,2048]{2,1,0:T(8,128)(2,1)}, u32[]{:S(2)}) copy-start(bf16[1,768,2048]{2,1,0:T(8,128)(2,1)} %param.11) | copy-start | bytes 9437188
  7.2 76.3 %reduce-scatter.2.cloned.1.call-start = ((), (), s32[]{:S(2)}) async-start(), calls=%async_computation.3 | async-start | bytes 3538944 | tf_op jit(solution)/shard_map/reduce_scatter | solution.py:104
  50.2 7.8 %all-to-all-start.1 = ((f32[4,1,96]{2,1,0:T(1,128)}), f32[4,1,96]{2,1,0:T(1,128)S(1)}, u32[]{:S(2)}, u32[]{:S(2)}) async-start(f32[4,1,96]{2,1,0:T(1,128)} %all_to_all.10), calls=%async_computation.2 | async-start | bytes 4096 | tf_op jit(solution)/shard_map/all_to_all | solution.py:120
Sparse Core Ops, SparseCore 0:
  43.5 39.9 reduce-scatter.1

commit v8 on v7

--- a/solution.py
+++ b/solution.py
@@ -18,41 +18,52 @@
     return jnp.stack([high, middle, low], axis=-1).astype(jnp.bfloat16)
 
 
-def partial_kernel(arrived_ref, gate_ref, up_ref, partial_ref, hidden_ref):
-    features = partial_ref.shape[1]
-    gate = gate_ref[...].astype(jnp.float32)
-    sigmoid_gate = 1.0 / (1.0 + jnp.exp(-gate))
-    hidden = (gate * sigmoid_gate * up_ref[...].astype(jnp.float32)).astype(jnp.bfloat16)
-    hidden_ref[...] = hidden
-    hidden_t = jnp.transpose(hidden.astype(jnp.float32)).astype(jnp.bfloat16)
-    got = arrived_ref[:, features:features + 128].astype(jnp.float32)
+def partial_kernel(rows_ref, pieces_ref, gate_ref, up_ref, partial_ref, hidden_ref, hidden_t_ref):
+    @pl.when(pl.program_id(0) == 0)
+    def _():
+        gate = gate_ref[...].astype(jnp.float32)
+        sigmoid_gate = 1.0 / (1.0 + jnp.exp(-gate))
+        hidden = (gate * sigmoid_gate * up_ref[...].astype(jnp.float32)).astype(jnp.bfloat16)
+        hidden_ref[...] = hidden
+        hidden_t_ref[...] = jnp.transpose(hidden.astype(jnp.float32)).astype(jnp.bfloat16)
+
+    got = pieces_ref[...].astype(jnp.float32)
     weights = (got[:, 0:1] + got[:, 1:2]) + got[:, 2:3]
-    tile = 512 if features % 512 == 0 else features
-    for start in range(0, features, tile):
-        rows = arrived_ref[:, start:start + tile].astype(jnp.float32)
-        weighted = (weights * rows).astype(jnp.bfloat16)
-        partial_ref[:, start:start + tile] = jnp.dot(
-            hidden_t, weighted, preferred_element_type=jnp.float32
-        ).astype(jnp.bfloat16)
+    weighted = (weights * rows_ref[...].astype(jnp.float32)).astype(jnp.bfloat16)
+    partial_ref[...] = jnp.dot(
+        hidden_t_ref[...], weighted, preferred_element_type=jnp.float32
+    ).astype(jnp.bfloat16)
 
 
 def weighted_partial(arrived, gate, up, features):
     slots, hidden_count = gate.shape
-    vmem = pl.BlockSpec(memory_space=pltpu.VMEM)
+    lanes = arrived.shape[1] - features
+    tile = 512 if features % 512 == 0 else features
     flops = 2 * slots * hidden_count * features
     moved = 2 * (arrived.size + 2 * gate.size + hidden_count * features + gate.size)
     return pl.pallas_call(
         partial_kernel,
+        grid=(features // tile,),
         out_shape=(
             jax.ShapeDtypeStruct((hidden_count, features), jnp.bfloat16),
             jax.ShapeDtypeStruct((slots, hidden_count), jnp.bfloat16),
         ),
-        in_specs=[vmem, vmem, vmem],
-        out_specs=(vmem, vmem),
+        in_specs=[
+            pl.BlockSpec((slots, tile), lambda j: (0, j)),
+            pl.BlockSpec((slots, lanes), lambda j: (0, features // lanes)),
+            pl.BlockSpec((slots, hidden_count), lambda j: (0, 0)),
+            pl.BlockSpec((slots, hidden_count), lambda j: (0, 0)),
+        ],
+        out_specs=(
+            pl.BlockSpec((hidden_count, tile), lambda j: (0, j)),
+            pl.BlockSpec((slots, hidden_count), lambda j: (0, 0)),
+        ),
+        scratch_shapes=[pltpu.VMEM((hidden_count, slots), jnp.bfloat16)],
+        compiler_params=pltpu.CompilerParams(dimension_semantics=("arbitrary",)),
         cost_estimate=pl.CostEstimate(
             flops=flops, bytes_accessed=moved, transcendentals=gate.size
         ),
-    )(arrived, gate, up)
+    )(arrived, arrived, gate, up)
 
 
 def local(out_grad, combine_weight, routes, saved_gate, saved_up, w_down):

time: 92.7 us -> 93.5 us (level)
  no operation moved by 1% of the time
where the time goes in v8:
time: 93.5 us; the launch traced here: 93 us
  waiting for transfers between devices  26.1 us (28%)
  blocking collectives  26 us (28%)
  between operations  14.2 us (15%)
  matrix products  6.85 us (7%)
  Pallas kernels  6.41 us (7%)
  local copies, waits for them, and re-layouts  6.31 us (7%)
  other arithmetic  4.03 us (4%)
  starting transfers between devices  3.26 us (3%)
    all_to_all x1, blocking collectives, local(): lax.all_to_all(packed.reshape(experts, capacity, feature_count + lanes),...  26 us
    reduce_scatter x1, waiting for transfers between devices, local(): lax.psum_scatter(partial_grad, 'dp', scatter_dimension=0, tiled=True)  21.5 us
    pallas_call x1, Pallas kernels, weighted_partial(): pl.pallas_call(partial_kernel, grid=(features // tile,), out_shape=(jax.S...  6.41 us
    dot_general x1, matrix products, local(): lax.dot_general(rows, matrix, (((1,), (1,)), ((), ())), preferred_element...  4.85 us
    all_to_all x1, waiting for transfers between devices, local(): lax.all_to_all(slot_grad.reshape(experts, capacity), 'expert', split_axis...  4.52 us
    all_to_all x1, starting transfers between devices, local(): lax.all_to_all(slot_grad.reshape(experts, capacity), 'expert', split_axis...  3.22 us
    unnamed x5, local copies, waits for them, and re-layouts  2.37 us
    gather x1, local copies, waits for them, and re-layouts, local(): grad_combine = returned.reshape(-1)[position].reshape(tok_rows, route_count)  1.94 us
  transfers between devices with their start and end apart: 2, of which 2 were waited for; matrix products, arithmetic and copies ran while one was open for 11% of the time, Pallas kernels for 0%

profile of v8, /device:TPU:0, one launch (start us, length us, event | category | flops | bytes accessed | tf_op | source)
XLA Modules:
  0.0 93.0 jit_solution(7021662180544825535)
XLA Ops:
  7.2 0.0 copy-start
  7.2 0.0 reduce-scatter.2.cloned.1.call-start
  7.2 0.9 %copy.17 = s32[128,2]{1,0:T(8,128)S(1)} copy(s32[128,2]{0,1:T(2,128)} %param.8) | data formatting | bytes 2048 | tf_op args[2]
  8.2 0.1 eq.35
  8.3 0.2 fusion.11
  8.5 0.8 copy.20
  9.3 0.1 reshape.130
  9.5 0.1 convert_element_type.61
  9.6 0.1 copy.19
  9.7 0.1 fusion.12
  9.8 1.6 %convolution_convert_fusion = bf16[384,2048]{1,0:T(8,128)(2,1)S(1)} fusion(pred[384,128]{1,0:T(8,128)(4,1)S(1)} %fusion.12, bf16[128,2048]{1,0:T(8,128)(2,1)} %param.6), kind=kOutput, calls=%fused_computation.3 | convolution fusion | flops 202113024 | bytes 2146304 | tf_op jit(solution)/shard_map/dot_general | solution.py:92
  11.4 0.2 convolution_convert_fusion.1
  11.6 0.1 pad_maximum_fusion
  11.7 26.0 %all_to_all.14 = bf16[4,96,2176]{2,1,0:T(8,128)(2,1)} all-to-all(bf16[4,96,2176]{2,1,0:T(8,128)(2,1)S(1)} %bitcast.25), channel_id=1, replica_groups=mesh['expert'=4,'dp'=8] {'expert'}, dimensions={0} | all-to-all | bytes 3342336 | tf_op jit(solution)/shard_map/all_to_all | solution.py:101
  37.7 6.4 %shard_map.93 = (bf16[768,2048]{1,0:T(8,128)(2,1)}, bf16[384,768]{1,0:T(8,128)(2,1)}) custom-call(bf16[384,2176]{1,0:T(8,128)(2,1)} %bitcast.21, bf16[384,2176]{1,0:T(8,128)(2,1)} %bitcast.22, bf16[384,768]{1,0:T(8,128)(2,1)} %bitcast.26, bf16[384,768]{1,0:T(8,128)(2,1)} %bitcast.27), custom_call_target="tpu_custom_call" | custom-call | flops 1207959552 | bytes 6586368 | tf_op jit(solution)/shard_map/pallas_call | solution.py:44
  44.1 0.0 reduce-scatter.2.cloned.1.call-update
  44.1 0.1 mul.74
  44.3 0.9 slice_convert_fusion
  45.2 0.3 fusion.13
  45.5 0.0 copy-done
  45.5 4.9 %fusion.10 = (bf16[384,768]{1,0:T(8,128)(2,1)}, bf16[384,768]{1,0:T(8,128)(2,1)}, f32[384]{0:T(512)S(1)}) fusion(f32[384]{0:T(512)S(1)} %fusion.13, bf16[1,1,4,96,768]{4,3,2,1,0:T(8,128)(2,1)} %param.9, bf16[1,1,4,96,768]{4,3,2,1,0:T(8,128)(2,1)} %param.10, bf16[384,768]{1,0:T(8,128)(2,1)} %get-tuple-element.7, bf16[1,768,2048]{2,1,0:T(8,128)(2,1)S(1)} %copy-done, ...), kind=kOutput, calls=%fused_computation.16 | convolution fusion | flops 1213562496 | bytes 7670784 | tf_op jit(solution)/shard_map/dot_general | solution.py:122
  50.3 0.7 all_to_all.10
  51.0 3.2 %all-to-all-start.1 = ((f32[4,1,96]{2,1,0:T(1,128)}), f32[4,1,96]{2,1,0:T(1,128)S(1)}, u32[]{:S(2)}, u32[]{:S(2)}) async-start(f32[4,1,96]{2,1,0:T(1,128)} %all_to_all.10), calls=%async_computation.2 | async-start | bytes 4096 | tf_op jit(solution)/shard_map/all_to_all | solution.py:131
  54.2 4.5 %all-to-all-done.1 = f32[4,1,96]{2,1,0:T(1,128)S(1)} async-done(((f32[4,1,96]{2,1,0:T(1,128)}), f32[4,1,96]{2,1,0:T(1,128)S(1)}, u32[]{:S(2)}, u32[]{:S(2)}) %all-to-all-start.1) | async-done | bytes 1568 | tf_op jit(solution)/shard_map/all_to_all | solution.py:131
  58.7 0.5 broadcast.68
  59.3 0.7 reduce.5
  59.9 0.1 reshape.137
  60.0 1.9 %gather_fusion = f32[256]{0:T(256)S(1)} fusion(f32[384]{0:T(512)S(1)} %reshape.137, s32[1024]{0:T(1024)S(1)} %pad_clamp_fusion), kind=kCustom, calls=%fused_computation | custom fusion | bytes 3072 | tf_op jit(solution)/shard_map/gather | solution.py:134
  62.0 0.1 reshape.138
  62.1 0.6 copy.22
  62.7 21.5 %reduce-scatter.2.cloned.1.call-done = bf16[96,2048]{1,0:T(8,128)(2,1)} async-done(((bf16[768,2048]{1,0:T(8,128)(2,1)}), bf16[96,2048]{1,0:T(8,128)(2,1)}) %reduce-scatter.2.cloned.1.call-update) | async-done | bytes 393232 | tf_op jit(solution)/shard_map/reduce_scatter | solution.py:115
  84.3 1.9 %bitcast_convert_fusion = f32[1,96,2048]{2,1,0:T(8,128)} fusion(bf16[96,2048]{1,0:T(8,128)(2,1)} %reduce-scatter.2.cloned.1.call-done), kind=kLoop, calls=%fused_computation.21 | loop fusion | flops 196608 | bytes 1179648 | tf_op jit(solution)/shard_map/broadcast_in_dim | solution.py:136
  (6 shorter events, 0.0 us)
Async XLA Ops:
  7.2 38.3 %copy-start = (bf16[1,768,2048]{2,1,0:T(8,128)(2,1)S(1)}, bf16[1,768,2048]{2,1,0:T(8,128)(2,1)}, u32[]{:S(2)}) copy-start(bf16[1,768,2048]{2,1,0:T(8,128)(2,1)} %param.11) | copy-start | bytes 9437188
  7.2 77.1 %reduce-scatter.2.cloned.1.call-start = ((), (), s32[]{:S(2)}) async-start(), calls=%async_computation.3 | async-start | bytes 3538944 | tf_op jit(solution)/shard_map/reduce_scatter | solution.py:115
  51.0 7.8 %all-to-all-start.1 = ((f32[4,1,96]{2,1,0:T(1,128)}), f32[4,1,96]{2,1,0:T(1,128)S(1)}, u32[]{:S(2)}, u32[]{:S(2)}) async-start(f32[4,1,96]{2,1,0:T(1,128)} %all_to_all.10), calls=%async_computation.2 | async-start | bytes 4096 | tf_op jit(solution)/shard_map/all_to_all | solution.py:131
Sparse Core Ops, SparseCore 0:
  44.3 39.9 reduce-scatter.1

commit v9 on v7

--- a/solution.py
+++ b/solution.py
@@ -21,18 +21,17 @@
 def partial_kernel(arrived_ref, gate_ref, up_ref, partial_ref, hidden_ref):
     features = partial_ref.shape[1]
     gate = gate_ref[...].astype(jnp.float32)
-    sigmoid_gate = 1.0 / (1.0 + jnp.exp(-gate))
+    sigmoid_gate = jax.nn.sigmoid(gate)
     hidden = (gate * sigmoid_gate * up_ref[...].astype(jnp.float32)).astype(jnp.bfloat16)
     hidden_ref[...] = hidden
-    hidden_t = jnp.transpose(hidden.astype(jnp.float32)).astype(jnp.bfloat16)
     got = arrived_ref[:, features:features + 128].astype(jnp.float32)
     weights = (got[:, 0:1] + got[:, 1:2]) + got[:, 2:3]
     tile = 512 if features % 512 == 0 else features
     for start in range(0, features, tile):
         rows = arrived_ref[:, start:start + tile].astype(jnp.float32)
         weighted = (weights * rows).astype(jnp.bfloat16)
-        partial_ref[:, start:start + tile] = jnp.dot(
-            hidden_t, weighted, preferred_element_type=jnp.float32
+        partial_ref[:, start:start + tile] = lax.dot_general(
+            hidden, weighted, (((0,), (0,)), ((), ())), preferred_element_type=jnp.float32
         ).astype(jnp.bfloat16)
 
 

time: 92.7 us -> 92.5 us (level)
  no operation moved by 1% of the time
where the time goes in v9:
time: 92.5 us; the launch traced here: 92.1 us
  blocking collectives  26 us (28%)
  waiting for transfers between devices  26 us (28%)
  between operations  14.2 us (15%)
  matrix products  6.86 us (7%)
  local copies, waits for them, and re-layouts  6.32 us (7%)
  Pallas kernels  5.5 us (6%)
  other arithmetic  4.03 us (4%)
  starting transfers between devices  3.26 us (4%)
    all_to_all x1, blocking collectives, local(): lax.all_to_all(packed.reshape(experts, capacity, feature_count + lanes),...  26 us
    reduce_scatter x1, waiting for transfers between devices, local(): lax.psum_scatter(partial_grad, 'dp', scatter_dimension=0, tiled=True)  21.5 us
    pallas_call x1, Pallas kernels, weighted_partial(): pl.pallas_call(partial_kernel, out_shape=(jax.ShapeDtypeStruct((hidden_co...  5.5 us
    dot_general x1, matrix products, local(): lax.dot_general(rows, matrix, (((1,), (1,)), ((), ())), preferred_element...  4.86 us
    all_to_all x1, waiting for transfers between devices, local(): lax.all_to_all(slot_grad.reshape(experts, capacity), 'expert', split_axis...  4.52 us
    all_to_all x1, starting transfers between devices, local(): lax.all_to_all(slot_grad.reshape(experts, capacity), 'expert', split_axis...  3.22 us
    unnamed x5, local copies, waits for them, and re-layouts  2.37 us
    gather x1, local copies, waits for them, and re-layouts, local(): grad_combine = returned.reshape(-1)[position].reshape(tok_rows, route_count)  1.95 us
  transfers between devices with their start and end apart: 2, of which 2 were waited for; matrix products, arithmetic and copies ran while one was open for 11% of the time, Pallas kernels for 0%

profile of v9, /device:TPU:0, one launch (start us, length us, event | category | flops | bytes accessed | tf_op | source)
XLA Modules:
  0.0 92.1 jit_solution(5001575785164164065)
XLA Ops:
  7.2 0.0 copy-start
  7.2 0.0 reduce-scatter.2.cloned.1.call-start
  7.2 0.9 %copy.17 = s32[128,2]{1,0:T(8,128)S(1)} copy(s32[128,2]{0,1:T(2,128)} %param.8) | data formatting | bytes 2048 | tf_op args[2]
  8.2 0.1 eq.35
  8.3 0.2 fusion.11
  8.5 0.8 copy.20
  9.3 0.1 reshape.130
  9.5 0.1 convert_element_type.61
  9.6 0.1 copy.19
  9.7 0.1 fusion.12
  9.8 1.6 %convolution_convert_fusion = bf16[384,2048]{1,0:T(8,128)(2,1)S(1)} fusion(pred[384,128]{1,0:T(8,128)(4,1)S(1)} %fusion.12, bf16[128,2048]{1,0:T(8,128)(2,1)} %param.6), kind=kOutput, calls=%fused_computation.3 | convolution fusion | flops 202113024 | bytes 2146304 | tf_op jit(solution)/shard_map/dot_general | solution.py:80
  11.4 0.2 convolution_convert_fusion.1
  11.6 0.1 pad_maximum_fusion
  11.7 26.0 %all_to_all.14 = bf16[4,96,2176]{2,1,0:T(8,128)(2,1)} all-to-all(bf16[4,96,2176]{2,1,0:T(8,128)(2,1)S(1)} %bitcast.21), channel_id=1, replica_groups=mesh['expert'=4,'dp'=8] {'expert'}, dimensions={0} | all-to-all | bytes 3342336 | tf_op jit(solution)/shard_map/all_to_all | solution.py:89
  37.7 5.5 %shard_map.93 = (bf16[768,2048]{1,0:T(8,128)(2,1)}, bf16[384,768]{1,0:T(8,128)(2,1)}) custom-call(bf16[384,2176]{1,0:T(8,128)(2,1)} %bitcast.22, bf16[384,768]{1,0:T(8,128)(2,1)} %bitcast.27, bf16[384,768]{1,0:T(8,128)(2,1)} %bitcast.28), custom_call_target="tpu_custom_call" | custom-call | flops 1207959552 | bytes 6586368 | tf_op jit(solution)/shard_map/pallas_call | solution.py:43
  43.2 0.0 reduce-scatter.2.cloned.1.call-update
  43.2 0.1 mul.74
  43.4 0.9 slice_convert_fusion
  44.3 0.3 fusion.13
  44.6 0.0 copy-done
  44.6 4.9 %fusion.10 = (bf16[384,768]{1,0:T(8,128)(2,1)}, bf16[384,768]{1,0:T(8,128)(2,1)}, f32[384]{0:T(512)S(1)}) fusion(f32[384]{0:T(512)S(1)} %fusion.13, bf16[1,1,4,96,768]{4,3,2,1,0:T(8,128)(2,1)} %param.9, bf16[1,1,4,96,768]{4,3,2,1,0:T(8,128)(2,1)} %param.10, bf16[384,768]{1,0:T(8,128)(2,1)} %get-tuple-element.7, bf16[1,768,2048]{2,1,0:T(8,128)(2,1)S(1)} %copy-done, ...), kind=kOutput, calls=%fused_computation.16 | convolution fusion | flops 1213562496 | bytes 7670784 | tf_op jit(solution)/shard_map/dot_general | solution.py:110
  49.4 0.7 all_to_all.10
  50.1 3.2 %all-to-all-start.1 = ((f32[4,1,96]{2,1,0:T(1,128)}), f32[4,1,96]{2,1,0:T(1,128)S(1)}, u32[]{:S(2)}, u32[]{:S(2)}) async-start(f32[4,1,96]{2,1,0:T(1,128)} %all_to_all.10), calls=%async_computation.2 | async-start | bytes 4096 | tf_op jit(solution)/shard_map/all_to_all | solution.py:119
  53.3 4.5 %all-to-all-done.1 = f32[4,1,96]{2,1,0:T(1,128)S(1)} async-done(((f32[4,1,96]{2,1,0:T(1,128)}), f32[4,1,96]{2,1,0:T(1,128)S(1)}, u32[]{:S(2)}, u32[]{:S(2)}) %all-to-all-start.1) | async-done | bytes 1568 | tf_op jit(solution)/shard_map/all_to_all | solution.py:119
  57.9 0.5 broadcast.68
  58.4 0.7 reduce.5
  59.0 0.1 reshape.137
  59.1 1.9 %gather_fusion = f32[256]{0:T(256)S(1)} fusion(f32[384]{0:T(512)S(1)} %reshape.137, s32[1024]{0:T(1024)S(1)} %pad_clamp_fusion), kind=kCustom, calls=%fused_computation | custom fusion | bytes 3072 | tf_op jit(solution)/shard_map/gather | solution.py:122
  61.1 0.1 reshape.138
  61.2 0.6 copy.22
  61.9 21.5 %reduce-scatter.2.cloned.1.call-done = bf16[96,2048]{1,0:T(8,128)(2,1)} async-done(((bf16[768,2048]{1,0:T(8,128)(2,1)}), bf16[96,2048]{1,0:T(8,128)(2,1)}) %reduce-scatter.2.cloned.1.call-update) | async-done | bytes 393232 | tf_op jit(solution)/shard_map/reduce_scatter | solution.py:103
  83.4 1.9 %bitcast_convert_fusion = f32[1,96,2048]{2,1,0:T(8,128)} fusion(bf16[96,2048]{1,0:T(8,128)(2,1)} %reduce-scatter.2.cloned.1.call-done), kind=kLoop, calls=%fused_computation.21 | loop fusion | flops 196608 | bytes 1179648 | tf_op jit(solution)/shard_map/broadcast_in_dim | solution.py:124
  (6 shorter events, 0.0 us)
Async XLA Ops:
  7.2 37.4 %copy-start = (bf16[1,768,2048]{2,1,0:T(8,128)(2,1)S(1)}, bf16[1,768,2048]{2,1,0:T(8,128)(2,1)}, u32[]{:S(2)}) copy-start(bf16[1,768,2048]{2,1,0:T(8,128)(2,1)} %param.11) | copy-start | bytes 9437188
  7.2 76.2 %reduce-scatter.2.cloned.1.call-start = ((), (), s32[]{:S(2)}) async-start(), calls=%async_computation.3 | async-start | bytes 3538944 | tf_op jit(solution)/shard_map/reduce_scatter | solution.py:103
  50.1 7.8 %all-to-all-start.1 = ((f32[4,1,96]{2,1,0:T(1,128)}), f32[4,1,96]{2,1,0:T(1,128)S(1)}, u32[]{:S(2)}, u32[]{:S(2)}) async-start(f32[4,1,96]{2,1,0:T(1,128)} %all_to_all.10), calls=%async_computation.2 | async-start | bytes 4096 | tf_op jit(solution)/shard_map/all_to_all | solution.py:119
Sparse Core Ops, SparseCore 0:
  43.3 39.9 reduce-scatter.1

commit v10 on v7

--- a/solution.py
+++ b/solution.py
@@ -64,24 +64,27 @@
     slots = experts * capacity
     lanes = 128
 
-    flat_routes = routes.reshape(-1)
-    route_total = flat_routes.shape[0]
-    onehot = (flat_routes[:, None] == jnp.arange(experts, dtype=jnp.int32)[None, :]).astype(
-        jnp.float32
+    by_route = routes.T
+    expert_ids = jnp.arange(experts, dtype=jnp.int32)
+    named = (by_route[:, None, :] == expert_ids[None, :, None]).astype(jnp.float32)
+    per_token = jnp.sum(named, axis=0)
+    token_ids = jnp.arange(tok_rows, dtype=jnp.int32)
+    earlier = (token_ids[:, None] < token_ids[None, :]).astype(jnp.bfloat16)
+    before = jnp.dot(
+        per_token.astype(jnp.bfloat16), earlier, preferred_element_type=jnp.float32
     )
-    order = jnp.arange(route_total, dtype=jnp.int32)
-    earlier = (order[None, :] < order[:, None]).astype(jnp.bfloat16)
-    before = jnp.dot(earlier, onehot.astype(jnp.bfloat16), preferred_element_type=jnp.float32)
-    slot = jnp.sum(before * onehot, axis=1).astype(jnp.int32)
-    position = flat_routes * capacity + slot
+    slot = jnp.sum(named * before[None], axis=1).astype(jnp.int32)
+    position = by_route * capacity + slot
 
     slot_ids = jnp.arange(slots, dtype=jnp.int32)
-    pick_route = position[None, :] == slot_ids[:, None]
-    pick_token = pick_route.reshape(slots, tok_rows, route_count).any(axis=2)
+    pick_route = position.reshape(-1)[None, :] == slot_ids[:, None]
+    pick_token = (position[0][None, :] == slot_ids[:, None]) | (
+        position[1:][:, None, :] == slot_ids[None, :, None]
+    ).any(axis=0)
     sent_rows = jnp.dot(
         pick_token.astype(out_grad.dtype), out_grad, preferred_element_type=jnp.float32
     ).astype(out_grad.dtype)
-    pieces = weight_pieces(combine_weight.reshape(-1))
+    pieces = weight_pieces(combine_weight.T.reshape(-1))
     pieces = jnp.pad(pieces, ((0, 0), (0, lanes - pieces.shape[1])))
     sent_pieces = jnp.dot(
         pick_route.astype(jnp.bfloat16), pieces, preferred_element_type=jnp.float32
@@ -120,7 +123,7 @@
     returned = lax.all_to_all(
         slot_grad.reshape(experts, capacity), "expert", split_axis=0, concat_axis=0, tiled=True
     )
-    grad_combine = returned.reshape(-1)[position].reshape(tok_rows, route_count)
+    grad_combine = returned.reshape(-1)[position].T
     return (
         grad_weight[None],
         grad_gate.reshape(saved_gate.shape),

time: 92.7 us -> 93.2 us (level)
  other arithmetic: 4.03 us -> 6.84 us
  local copies, waits for them, and re-layouts: 6.32 us -> 3.78 us
    unnamed x5 -> x2, local copies, waits for them, and re-layouts: 2.37 us -> 0.01 us
    reduce_sum x0 -> x2, other arithmetic: none -> 1.55 us  [the longest x1 0.84 us: local(): per_token = jnp.sum(named, axis=0)]
where the time goes in v10:
time: 93.2 us; the launch traced here: 92.8 us
  waiting for transfers between devices  26.4 us (28%)
  blocking collectives  26 us (28%)
  between operations  14.1 us (15%)
  other arithmetic  6.84 us (7%)
  matrix products  6.78 us (7%)
  Pallas kernels  5.63 us (6%)
  local copies, waits for them, and re-layouts  3.78 us (4%)
  starting transfers between devices  3.26 us (3%)
    all_to_all x1, blocking collectives, local(): lax.all_to_all(packed.reshape(experts, capacity, feature_count + lanes),...  26 us
    reduce_scatter x1, waiting for transfers between devices, local(): lax.psum_scatter(partial_grad, 'dp', scatter_dimension=0, tiled=True)  21.9 us
    pallas_call x1, Pallas kernels, weighted_partial(): pl.pallas_call(partial_kernel, out_shape=(jax.ShapeDtypeStruct((hidden_co...  5.63 us
    dot_general x1, matrix products, local(): lax.dot_general(rows, matrix, (((1,), (1,)), ((), ())), preferred_element...  4.86 us
    all_to_all x1, waiting for transfers between devices, local(): lax.all_to_all(slot_grad.reshape(experts, capacity), 'expert', split_axis...  4.52 us
    all_to_all x1, starting transfers between devices, local(): lax.all_to_all(slot_grad.reshape(experts, capacity), 'expert', split_axis...  3.22 us
    gather x1, local copies, waits for them, and re-layouts, local(): grad_combine = returned.reshape(-1)[position].T  2.51 us
    broadcast_in_dim x1, other arithmetic, local(): grad_weight[None]  1.94 us
  transfers between devices with their start and end apart: 2, of which 2 were waited for; matrix products, arithmetic and copies ran while one was open for 11% of the time, Pallas kernels for 0%

profile of v10, /device:TPU:0, one launch (start us, length us, event | category | flops | bytes accessed | tf_op | source)
XLA Modules:
  0.0 92.8 jit_solution(2833234228445646342)
XLA Ops:
  7.2 0.0 copy-start
  7.2 0.0 reduce-scatter.2.cloned.1.call-start
  7.2 0.8 convert_reduce_fusion
  8.1 0.1 fusion.29
  8.2 0.7 select_reduce_fusion
  8.9 0.7 fusion.32
  9.6 0.7 reduce-precision_convert_fusion.1
  10.3 1.6 %convolution_convert_fusion = bf16[384,2048]{1,0:T(8,128)(2,1)S(1)} fusion(bf16[128,2048]{1,0:T(8,128)(2,1)} %param.6, s32[128]{0:T(128)S(1)} %get-tuple-element.14, s32[128]{0:T(128)S(1)} %get-tuple-element.13), kind=kOutput, calls=%fused_computation.3 | convolution fusion | flops 202260480 | bytes 2098176 | tf_op jit(solution)/shard_map/dot_general | solution.py:84
  11.9 0.2 convolution_convert_fusion.1
  12.1 0.1 pad_maximum_fusion
  12.2 26.0 %all_to_all.14 = bf16[4,96,2176]{2,1,0:T(8,128)(2,1)} all-to-all(bf16[4,96,2176]{2,1,0:T(8,128)(2,1)S(1)} %bitcast.35), channel_id=1, replica_groups=mesh['expert'=4,'dp'=8] {'expert'}, dimensions={0} | all-to-all | bytes 3342336 | tf_op jit(solution)/shard_map/all_to_all | solution.py:93
  38.2 5.6 %shard_map.93 = (bf16[768,2048]{1,0:T(8,128)(2,1)}, bf16[384,768]{1,0:T(8,128)(2,1)}) custom-call(bf16[384,2176]{1,0:T(8,128)(2,1)} %bitcast.36, bf16[384,768]{1,0:T(8,128)(2,1)} %bitcast.44, bf16[384,768]{1,0:T(8,128)(2,1)} %bitcast.45), custom_call_target="tpu_custom_call" | custom-call | flops 1207959552 | bytes 6586368 | tf_op jit(solution)/shard_map/pallas_call | solution.py:44
  43.8 0.0 reduce-scatter.2.cloned.1.call-update
  43.9 0.9 slice_convert_fusion
  44.8 0.3 fusion.11
  45.0 0.0 copy-done
  45.0 4.9 %fusion.10 = (bf16[384,768]{1,0:T(8,128)(2,1)}, bf16[384,768]{1,0:T(8,128)(2,1)}, f32[384]{0:T(512)S(1)}) fusion(f32[384]{0:T(512)S(1)} %fusion.11, bf16[1,1,4,96,768]{4,3,2,1,0:T(8,128)(2,1)} %param.9, bf16[1,1,4,96,768]{4,3,2,1,0:T(8,128)(2,1)} %param.10, bf16[384,768]{1,0:T(8,128)(2,1)} %get-tuple-element.7, bf16[1,768,2048]{2,1,0:T(8,128)(2,1)S(1)} %copy-done, ...), kind=kOutput, calls=%fused_computation.16 | convolution fusion | flops 1213562496 | bytes 7670784 | tf_op jit(solution)/shard_map/dot_general | solution.py:114
  49.9 0.7 all_to_all.10
  50.6 3.2 %all-to-all-start.1 = ((f32[4,1,96]{2,1,0:T(1,128)}), f32[4,1,96]{2,1,0:T(1,128)S(1)}, u32[]{:S(2)}, u32[]{:S(2)}) async-start(f32[4,1,96]{2,1,0:T(1,128)} %all_to_all.10), calls=%async_computation.2 | async-start | bytes 4096 | tf_op jit(solution)/shard_map/all_to_all | solution.py:123
  53.8 4.5 %all-to-all-done.1 = f32[4,1,96]{2,1,0:T(1,128)S(1)} async-done(((f32[4,1,96]{2,1,0:T(1,128)}), f32[4,1,96]{2,1,0:T(1,128)S(1)}, u32[]{:S(2)}, u32[]{:S(2)}) %all-to-all-start.1) | async-done | bytes 1568 | tf_op jit(solution)/shard_map/all_to_all | solution.py:123
  58.3 0.5 broadcast.50
  58.8 0.7 reduce.5
  59.5 0.1 reshape.103
  59.6 2.5 %gather_fusion = f32[256]{0:T(256)} fusion(f32[384]{0:T(512)S(1)} %reshape.103, s32[1024]{0:T(1024)S(1)} %pad_clamp_fusion), kind=kCustom, calls=%fused_computation | custom fusion | bytes 3072 | tf_op jit(solution)/shard_map/gather | solution.py:126
  62.1 21.9 %reduce-scatter.2.cloned.1.call-done = bf16[96,2048]{1,0:T(8,128)(2,1)} async-done(((bf16[768,2048]{1,0:T(8,128)(2,1)}), bf16[96,2048]{1,0:T(8,128)(2,1)}) %reduce-scatter.2.cloned.1.call-update) | async-done | bytes 393232 | tf_op jit(solution)/shard_map/reduce_scatter | solution.py:107
  84.0 1.9 %bitcast_convert_fusion = f32[1,96,2048]{2,1,0:T(8,128)} fusion(bf16[96,2048]{1,0:T(8,128)(2,1)} %reduce-scatter.2.cloned.1.call-done), kind=kLoop, calls=%fused_computation.19 | loop fusion | flops 196608 | bytes 1179648 | tf_op jit(solution)/shard_map/broadcast_in_dim | solution.py:128
  (2 shorter events, 0.0 us)
Async XLA Ops:
  7.2 37.9 %copy-start = (bf16[1,768,2048]{2,1,0:T(8,128)(2,1)S(1)}, bf16[1,768,2048]{2,1,0:T(8,128)(2,1)}, u32[]{:S(2)}) copy-start(bf16[1,768,2048]{2,1,0:T(8,128)(2,1)} %param.11) | copy-start | bytes 9437188
  7.2 76.8 %reduce-scatter.2.cloned.1.call-start = ((), (), s32[]{:S(2)}) async-start(), calls=%async_computation.3 | async-start | bytes 3538944 | tf_op jit(solution)/shard_map/reduce_scatter | solution.py:107
  50.6 7.8 %all-to-all-start.1 = ((f32[4,1,96]{2,1,0:T(1,128)}), f32[4,1,96]{2,1,0:T(1,128)S(1)}, u32[]{:S(2)}, u32[]{:S(2)}) async-start(f32[4,1,96]{2,1,0:T(1,128)} %all_to_all.10), calls=%async_computation.2 | async-start | bytes 4096 | tf_op jit(solution)/shard_map/all_to_all | solution.py:123
Sparse Core Ops, SparseCore 0:
  44.0 39.9 reduce-scatter.1

commit v11 on v7

--- a/solution.py
+++ b/solution.py
@@ -1,3 +1,5 @@
+import functools
+
 import jax
 import jax.numpy as jnp
 from jax import lax
@@ -16,6 +18,69 @@
     middle = round_bf16(rest)
     low = rest - middle
     return jnp.stack([high, middle, low], axis=-1).astype(jnp.bfloat16)
+
+
+def front_kernel(routes_ref, weights_ref, rows_ref, packed_ref, position_ref, *, experts, capacity):
+    route_count, tokens = routes_ref.shape
+    slots, width = packed_ref.shape
+    features = rows_ref.shape[1]
+    padded = -(-experts // 8) * 8
+    routes = routes_ref[...]
+    expert_col = lax.broadcasted_iota(jnp.int32, (padded, tokens), 0)
+    per_token = jnp.zeros((padded, tokens), jnp.float32)
+    for k in range(route_count):
+        per_token = per_token + jnp.where(routes[k:k + 1, :] == expert_col, 1.0, 0.0)
+    earlier = jnp.where(
+        lax.broadcasted_iota(jnp.int32, (tokens, tokens), 0)
+        < lax.broadcasted_iota(jnp.int32, (tokens, tokens), 1), 1.0, 0.0
+    ).astype(jnp.bfloat16)
+    before = jnp.dot(per_token.astype(jnp.bfloat16), earlier, preferred_element_type=jnp.float32)
+    slot_row = lax.broadcasted_iota(jnp.int32, (slots, tokens), 0)
+    pick = jnp.zeros((slots, tokens), jnp.float32)
+    weight = jnp.zeros((slots, 1), jnp.float32)
+    for k in range(route_count):
+        mine = routes[k:k + 1, :] == expert_col
+        slot = jnp.sum(jnp.where(mine, before, 0.0), axis=0, keepdims=True).astype(jnp.int32)
+        place = routes[k:k + 1, :] * capacity + slot
+        position_ref[k:k + 1, :] = place
+        chosen = slot_row == place
+        pick = pick + jnp.where(chosen, 1.0, 0.0)
+        weight = weight + jnp.sum(
+            jnp.where(chosen, weights_ref[k:k + 1, :], 0.0), axis=1, keepdims=True
+        )
+    pick = pick.astype(jnp.bfloat16)
+    tile = 512 if features % 512 == 0 else features
+    for start in range(0, features, tile):
+        packed_ref[:, start:start + tile] = jnp.dot(
+            pick, rows_ref[:, start:start + tile], preferred_element_type=jnp.float32
+        ).astype(jnp.bfloat16)
+    high = weight.astype(jnp.bfloat16).astype(jnp.float32)
+    rest = weight - high
+    middle = rest.astype(jnp.bfloat16).astype(jnp.float32)
+    low = rest - middle
+    column = lax.broadcasted_iota(jnp.int32, (slots, width - features), 1)
+    pieces = jnp.where(column == 0, high, jnp.where(column == 1, middle, jnp.where(column == 2, low, 0.0)))
+    packed_ref[:, features:] = pieces.astype(jnp.bfloat16)
+
+
+def pack_slots(routes_t, weights_t, rows, experts, capacity):
+    route_count, tokens = routes_t.shape
+    features = rows.shape[1]
+    slots = experts * capacity
+    vmem = pl.BlockSpec(memory_space=pltpu.VMEM)
+    return pl.pallas_call(
+        functools.partial(front_kernel, experts=experts, capacity=capacity),
+        out_shape=(
+            jax.ShapeDtypeStruct((slots, features + 128), jnp.bfloat16),
+            jax.ShapeDtypeStruct((route_count, tokens), jnp.int32),
+        ),
+        in_specs=[vmem, vmem, vmem],
+        out_specs=(vmem, vmem),
+        cost_estimate=pl.CostEstimate(
+            flops=2 * slots * tokens * features, bytes_accessed=2 * (rows.size + slots * features),
+            transcendentals=0,
+        ),
+    )(routes_t, weights_t, rows)
 
 
 def partial_kernel(arrived_ref, gate_ref, up_ref, partial_ref, hidden_ref):
@@ -64,29 +129,7 @@
     slots = experts * capacity
     lanes = 128
 
-    flat_routes = routes.reshape(-1)
-    route_total = flat_routes.shape[0]
-    onehot = (flat_routes[:, None] == jnp.arange(experts, dtype=jnp.int32)[None, :]).astype(
-        jnp.float32
-    )
-    order = jnp.arange(route_total, dtype=jnp.int32)
-    earlier = (order[None, :] < order[:, None]).astype(jnp.bfloat16)
-    before = jnp.dot(earlier, onehot.astype(jnp.bfloat16), preferred_element_type=jnp.float32)
-    slot = jnp.sum(before * onehot, axis=1).astype(jnp.int32)
-    position = flat_routes * capacity + slot
-
-    slot_ids = jnp.arange(slots, dtype=jnp.int32)
-    pick_route = position[None, :] == slot_ids[:, None]
-    pick_token = pick_route.reshape(slots, tok_rows, route_count).any(axis=2)
-    sent_rows = jnp.dot(
-        pick_token.astype(out_grad.dtype), out_grad, preferred_element_type=jnp.float32
-    ).astype(out_grad.dtype)
-    pieces = weight_pieces(combine_weight.reshape(-1))
-    pieces = jnp.pad(pieces, ((0, 0), (0, lanes - pieces.shape[1])))
-    sent_pieces = jnp.dot(
-        pick_route.astype(jnp.bfloat16), pieces, preferred_element_type=jnp.float32
-    ).astype(jnp.bfloat16)
-    packed = jnp.concatenate([sent_rows, sent_pieces], axis=1)
+    packed, position = pack_slots(routes.T, combine_weight.T, out_grad, experts, capacity)
     arrived = lax.all_to_all(
         packed.reshape(experts, capacity, feature_count + lanes),
         "expert",
@@ -120,7 +163,7 @@
     returned = lax.all_to_all(
         slot_grad.reshape(experts, capacity), "expert", split_axis=0, concat_axis=0, tiled=True
     )
-    grad_combine = returned.reshape(-1)[position].reshape(tok_rows, route_count)
+    grad_combine = returned.reshape(-1)[position].T
     return (
         grad_weight[None],
         grad_gate.reshape(saved_gate.shape),

time: 92.7 us -> 92.4 us (level)
  Pallas kernels: 5.63 us -> 8.78 us
  matrix products: 6.85 us -> 4.86 us
  local copies, waits for them, and re-layouts: 6.32 us -> 4.43 us
    pallas_call x0 -> x1, Pallas kernels: none -> 3.14 us  [pack_slots(): pl.pallas_call(functools.partial(front_kernel, experts=experts, capacity=...]
    dot_general x3 -> x0, matrix products: 2 us -> none  [the longest x1 1.6 us: local(): jnp.dot(pick_token.astype(out_grad.dtype), out_grad, preferred_element_ty...]
    unnamed x5 -> x4, local copies, waits for them, and re-layouts: 2.37 us -> 0.66 us
where the time goes in v11:
time: 92.4 us; the launch traced here: 92 us
  blocking collectives  26.9 us (29%)
  waiting for transfers between devices  26 us (28%)
  between operations  14.1 us (15%)
  Pallas kernels  8.78 us (10%)
  matrix products  4.86 us (5%)
  local copies, waits for them, and re-layouts  4.43 us (5%)
  other arithmetic  3.79 us (4%)
  starting transfers between devices  3.26 us (4%)
    all_to_all x1, blocking collectives, local(): lax.all_to_all(packed.reshape(experts, capacity, feature_count + lanes),...  26.9 us
    reduce_scatter x1, waiting for transfers between devices, local(): lax.psum_scatter(partial_grad, 'dp', scatter_dimension=0, tiled=True)  21.4 us
    pallas_call x1, Pallas kernels, weighted_partial(): pl.pallas_call(partial_kernel, out_shape=(jax.ShapeDtypeStruct((hidden_co...  5.63 us
    dot_general x1, matrix products, local(): lax.dot_general(rows, matrix, (((1,), (1,)), ((), ())), preferred_element...  4.86 us
    all_to_all x1, waiting for transfers between devices, local(): lax.all_to_all(slot_grad.reshape(experts, capacity), 'expert', split_axis...  4.52 us
    all_to_all x1, starting transfers between devices, local(): lax.all_to_all(slot_grad.reshape(experts, capacity), 'expert', split_axis...  3.22 us
    pallas_call x1, Pallas kernels, pack_slots(): pl.pallas_call(functools.partial(front_kernel, experts=experts, capacity=...  3.14 us
    gather x1, local copies, waits for them, and re-layouts, local(): grad_combine = returned.reshape(-1)[position].T  2.5 us
  transfers between devices with their start and end apart: 2, of which 2 were waited for; matrix products, arithmetic and copies ran while one was open for 11% of the time, Pallas kernels for 0%

profile of v11, /device:TPU:0, one launch (start us, length us, event | category | flops | bytes accessed | tf_op | source)
XLA Modules:
  0.0 92.0 jit_solution(14761812086809545533)
XLA Ops:
  7.2 0.0 copy-start
  7.2 0.0 reduce-scatter.2.cloned.1.call-start
  7.2 3.1 %shard_map.93 = (bf16[384,2176]{1,0:T(8,128)(2,1)}, s32[2,128]{1,0:T(2,128)}) custom-call(s32[2,128]{1,0:T(2,128)} %bitcast.31, f32[2,128]{1,0:T(2,128)} %bitcast.32, bf16[128,2048]{1,0:T(8,128)(2,1)} %rows_ref.1), custom_call_target="tpu_custom_call" | custom-call | flops 201326592 | bytes 2097152 | tf_op jit(solution)/shard_map/pallas_call | solution.py:71
  10.4 26.9 %all_to_all.14 = bf16[4,96,2176]{2,1,0:T(8,128)(2,1)} all-to-all(bf16[4,96,2176]{2,1,0:T(8,128)(2,1)} %bitcast.27), channel_id=1, replica_groups=mesh['expert'=4,'dp'=8] {'expert'}, dimensions={0} | all-to-all | bytes 3342336 | tf_op jit(solution)/shard_map/all_to_all | solution.py:133
  37.2 5.6 %shard_map.94 = (bf16[768,2048]{1,0:T(8,128)(2,1)}, bf16[384,768]{1,0:T(8,128)(2,1)}) custom-call(bf16[384,2176]{1,0:T(8,128)(2,1)} %bitcast.24, bf16[384,768]{1,0:T(8,128)(2,1)} %bitcast.29, bf16[384,768]{1,0:T(8,128)(2,1)} %bitcast.30), custom_call_target="tpu_custom_call" | custom-call | flops 1207959552 | bytes 6586368 | tf_op jit(solution)/shard_map/pallas_call | solution.py:109
  42.9 0.0 copy-start.1
  42.9 0.0 reduce-scatter.2.cloned.1.call-update
  42.9 0.7 copy-done.1
  43.5 0.9 slice_convert_fusion
  44.5 0.3 fusion.11
  44.7 0.0 copy-done
  44.7 4.9 %fusion.10 = (bf16[384,768]{1,0:T(8,128)(2,1)}, bf16[384,768]{1,0:T(8,128)(2,1)}, f32[384]{0:T(512)S(1)}) fusion(f32[384]{0:T(512)S(1)} %fusion.11, bf16[1,1,4,96,768]{4,3,2,1,0:T(8,128)(2,1)} %param.9, bf16[1,1,4,96,768]{4,3,2,1,0:T(8,128)(2,1)} %param.10, bf16[384,768]{1,0:T(8,128)(2,1)} %get-tuple-element.10, bf16[1,768,2048]{2,1,0:T(8,128)(2,1)S(1)} %copy-done, ...), kind=kOutput, calls=%fused_computation.14 | convolution fusion | flops 1213562496 | bytes 7670784 | tf_op jit(solution)/shard_map/dot_general | solution.py:154
  49.6 0.7 all_to_all.10
  50.3 3.2 %all-to-all-start.1 = ((f32[4,1,96]{2,1,0:T(1,128)}), f32[4,1,96]{2,1,0:T(1,128)S(1)}, u32[]{:S(2)}, u32[]{:S(2)}) async-start(f32[4,1,96]{2,1,0:T(1,128)} %all_to_all.10), calls=%async_computation.2 | async-start | bytes 4096 | tf_op jit(solution)/shard_map/all_to_all | solution.py:163
  53.5 4.5 %all-to-all-done.1 = f32[4,1,96]{2,1,0:T(1,128)S(1)} async-done(((f32[4,1,96]{2,1,0:T(1,128)}), f32[4,1,96]{2,1,0:T(1,128)S(1)}, u32[]{:S(2)}, u32[]{:S(2)}) %all-to-all-start.1) | async-done | bytes 1568 | tf_op jit(solution)/shard_map/all_to_all | solution.py:163
  58.0 0.5 broadcast.14
  58.5 0.7 reduce.5
  59.2 0.1 reshape.40
  59.3 2.5 %gather_fusion = f32[256]{0:T(256)} fusion(f32[384]{0:T(512)S(1)} %reshape.40, s32[1024]{0:T(1024)S(1)} %pad_clamp_fusion), kind=kCustom, calls=%fused_computation | custom fusion | bytes 3072 | tf_op jit(solution)/shard_map/gather | solution.py:166
  61.8 21.4 %reduce-scatter.2.cloned.1.call-done = bf16[96,2048]{1,0:T(8,128)(2,1)} async-done(((bf16[768,2048]{1,0:T(8,128)(2,1)}), bf16[96,2048]{1,0:T(8,128)(2,1)}) %reduce-scatter.2.cloned.1.call-update) | async-done | bytes 393232 | tf_op jit(solution)/shard_map/reduce_scatter | solution.py:147
  83.2 1.9 %bitcast_convert_fusion = f32[1,96,2048]{2,1,0:T(8,128)} fusion(bf16[96,2048]{1,0:T(8,128)(2,1)} %reduce-scatter.2.cloned.1.call-done), kind=kLoop, calls=%fused_computation.16 | loop fusion | flops 196608 | bytes 1179648 | tf_op jit(solution)/shard_map/broadcast_in_dim | solution.py:168
  (2 shorter events, 0.0 us)
Async XLA Ops:
  7.2 37.6 %copy-start = (bf16[1,768,2048]{2,1,0:T(8,128)(2,1)S(1)}, bf16[1,768,2048]{2,1,0:T(8,128)(2,1)}, u32[]{:S(2)}) copy-start(bf16[1,768,2048]{2,1,0:T(8,128)(2,1)} %param.11) | copy-start | bytes 9437188
  7.2 76.0 %reduce-scatter.2.cloned.1.call-start = ((), (), s32[]{:S(2)}) async-start(), calls=%async_computation.3 | async-start | bytes 3538944 | tf_op jit(solution)/shard_map/reduce_scatter | solution.py:147
  42.9 0.7 copy-start.1
  50.3 7.8 %all-to-all-start.1 = ((f32[4,1,96]{2,1,0:T(1,128)}), f32[4,1,96]{2,1,0:T(1,128)S(1)}, u32[]{:S(2)}, u32[]{:S(2)}) async-start(f32[4,1,96]{2,1,0:T(1,128)} %all_to_all.10), calls=%async_computation.2 | async-start | bytes 4096 | tf_op jit(solution)/shard_map/all_to_all | solution.py:163
Sparse Core Ops, SparseCore 0:
  43.0 40.1 reduce-scatter.1

commit v12 on v11

--- a/solution.py
+++ b/solution.py
@@ -83,37 +83,81 @@
     )(routes_t, weights_t, rows)
 
 
-def partial_kernel(arrived_ref, gate_ref, up_ref, partial_ref, hidden_ref):
-    features = partial_ref.shape[1]
-    gate = gate_ref[...].astype(jnp.float32)
+def partial_kernel(arrived_hbm, gate_hbm, up_hbm, partial_hbm, hidden_hbm,
+                   tiles_v, pieces_v, gate_v, up_v, hidden_v, out_v, in_sems, out_sems, *, tile):
+    count = tiles_v.shape[0]
+    features = count * tile
+    lanes = pieces_v.shape[1]
+    loads = [
+        pltpu.make_async_copy(gate_hbm, gate_v, in_sems.at[0]),
+        pltpu.make_async_copy(up_hbm, up_v, in_sems.at[1]),
+        pltpu.make_async_copy(
+            arrived_hbm.at[:, pl.ds(features, lanes)], pieces_v, in_sems.at[2]
+        ),
+    ]
+    tiles = [
+        pltpu.make_async_copy(
+            arrived_hbm.at[:, pl.ds(part * tile, tile)], tiles_v.at[part], in_sems.at[3 + part]
+        )
+        for part in range(count)
+    ]
+    for copy in loads + tiles:
+        copy.start()
+    loads[0].wait()
+    loads[1].wait()
+    gate = gate_v[...].astype(jnp.float32)
     sigmoid_gate = 1.0 / (1.0 + jnp.exp(-gate))
-    hidden = (gate * sigmoid_gate * up_ref[...].astype(jnp.float32)).astype(jnp.bfloat16)
-    hidden_ref[...] = hidden
+    hidden = (gate * sigmoid_gate * up_v[...].astype(jnp.float32)).astype(jnp.bfloat16)
+    hidden_v[...] = hidden
+    store_hidden = pltpu.make_async_copy(hidden_v, hidden_hbm, out_sems.at[count])
+    store_hidden.start()
     hidden_t = jnp.transpose(hidden.astype(jnp.float32)).astype(jnp.bfloat16)
-    got = arrived_ref[:, features:features + 128].astype(jnp.float32)
+    loads[2].wait()
+    got = pieces_v[...].astype(jnp.float32)
     weights = (got[:, 0:1] + got[:, 1:2]) + got[:, 2:3]
-    tile = 512 if features % 512 == 0 else features
-    for start in range(0, features, tile):
-        rows = arrived_ref[:, start:start + tile].astype(jnp.float32)
-        weighted = (weights * rows).astype(jnp.bfloat16)
-        partial_ref[:, start:start + tile] = jnp.dot(
-            hidden_t, weighted, preferred_element_type=jnp.float32
-        ).astype(jnp.bfloat16)
+    stores = []
+    for part in range(count):
+        tiles[part].wait()
+        weighted = (weights * tiles_v[part].astype(jnp.float32)).astype(jnp.bfloat16)
+        out_v[part] = jnp.dot(hidden_t, weighted, preferred_element_type=jnp.float32).astype(
+            jnp.bfloat16
+        )
+        store = pltpu.make_async_copy(
+            out_v.at[part], partial_hbm.at[:, pl.ds(part * tile, tile)], out_sems.at[part]
+        )
+        store.start()
+        stores.append(store)
+    for store in stores:
+        store.wait()
+    store_hidden.wait()
 
 
 def weighted_partial(arrived, gate, up, features):
     slots, hidden_count = gate.shape
-    vmem = pl.BlockSpec(memory_space=pltpu.VMEM)
+    lanes = arrived.shape[1] - features
+    tile = 512 if features % 512 == 0 else features
+    count = features // tile
     flops = 2 * slots * hidden_count * features
     moved = 2 * (arrived.size + 2 * gate.size + hidden_count * features + gate.size)
+    anywhere = pl.BlockSpec(memory_space=pl.ANY)
     return pl.pallas_call(
-        partial_kernel,
+        functools.partial(partial_kernel, tile=tile),
         out_shape=(
             jax.ShapeDtypeStruct((hidden_count, features), jnp.bfloat16),
             jax.ShapeDtypeStruct((slots, hidden_count), jnp.bfloat16),
         ),
-        in_specs=[vmem, vmem, vmem],
-        out_specs=(vmem, vmem),
+        in_specs=[anywhere, anywhere, anywhere],
+        out_specs=(anywhere, anywhere),
+        scratch_shapes=[
+            pltpu.VMEM((count, slots, tile), jnp.bfloat16),
+            pltpu.VMEM((slots, lanes), jnp.bfloat16),
+            pltpu.VMEM((slots, hidden_count), jnp.bfloat16),
+            pltpu.VMEM((slots, hidden_count), jnp.bfloat16),
+            pltpu.VMEM((slots, hidden_count), jnp.bfloat16),
+            pltpu.VMEM((count, hidden_count, tile), jnp.bfloat16),
+            pltpu.SemaphoreType.DMA((3 + count,)),
+            pltpu.SemaphoreType.DMA((count + 1,)),
+        ],
         cost_estimate=pl.CostEstimate(
             flops=flops, bytes_accessed=moved, transcendentals=gate.size
         ),

time: 92.4 us -> 92.1 us (level)
  no operation moved by 1% of the time
where the time goes in v12:
time: 92.1 us; the launch traced here: 91.7 us
  blocking collectives  26.9 us (29%)
  waiting for transfers between devices  26 us (28%)
  between operations  14.1 us (15%)
  Pallas kernels  8.5 us (9%)
  matrix products  4.86 us (5%)
  local copies, waits for them, and re-layouts  4.42 us (5%)
  other arithmetic  3.79 us (4%)
  starting transfers between devices  3.26 us (4%)
    all_to_all x1, blocking collectives, local(): lax.all_to_all(packed.reshape(experts, capacity, feature_count + lanes),...  26.9 us
    reduce_scatter x1, waiting for transfers between devices, local(): lax.psum_scatter(partial_grad, 'dp', scatter_dimension=0, tiled=True)  21.4 us
    pallas_call x1, Pallas kernels, weighted_partial(): pl.pallas_call(functools.partial(partial_kernel, tile=tile), out_shape=(j...  5.35 us
    dot_general x1, matrix products, local(): lax.dot_general(rows, matrix, (((1,), (1,)), ((), ())), preferred_element...  4.86 us
    all_to_all x1, waiting for transfers between devices, local(): lax.all_to_all(slot_grad.reshape(experts, capacity), 'expert', split_axis...  4.52 us
    all_to_all x1, starting transfers between devices, local(): lax.all_to_all(slot_grad.reshape(experts, capacity), 'expert', split_axis...  3.22 us
    pallas_call x1, Pallas kernels, pack_slots(): pl.pallas_call(functools.partial(front_kernel, experts=experts, capacity=...  3.14 us
    gather x1, local copies, waits for them, and re-layouts, local(): grad_combine = returned.reshape(-1)[position].T  2.5 us
  transfers between devices with their start and end apart: 2, of which 2 were waited for; matrix products, arithmetic and copies ran while one was open for 11% of the time, Pallas kernels for 0%

profile of v12, /device:TPU:0, one launch (start us, length us, event | category | flops | bytes accessed | tf_op | source)
XLA Modules:
  0.0 91.7 jit_solution(3786651060959874051)
XLA Ops:
  7.2 0.0 copy-start
  7.2 0.0 reduce-scatter.2.cloned.1.call-start
  7.2 3.1 %shard_map.93 = (bf16[384,2176]{1,0:T(8,128)(2,1)}, s32[2,128]{1,0:T(2,128)}) custom-call(s32[2,128]{1,0:T(2,128)} %bitcast.31, f32[2,128]{1,0:T(2,128)} %bitcast.32, bf16[128,2048]{1,0:T(8,128)(2,1)} %rows_ref.1), custom_call_target="tpu_custom_call" | custom-call | flops 201326592 | bytes 2097152 | tf_op jit(solution)/shard_map/pallas_call | solution.py:71
  10.4 26.9 %all_to_all.14 = bf16[4,96,2176]{2,1,0:T(8,128)(2,1)} all-to-all(bf16[4,96,2176]{2,1,0:T(8,128)(2,1)} %bitcast.27), channel_id=1, replica_groups=mesh['expert'=4,'dp'=8] {'expert'}, dimensions={0} | all-to-all | bytes 3342336 | tf_op jit(solution)/shard_map/all_to_all | solution.py:177
  37.2 5.4 %shard_map.94 = (bf16[768,2048]{1,0:T(8,128)(2,1)}, bf16[384,768]{1,0:T(8,128)(2,1)}) custom-call(bf16[384,2176]{1,0:T(8,128)(2,1)} %bitcast.24, bf16[384,768]{1,0:T(8,128)(2,1)} %bitcast.29, bf16[384,768]{1,0:T(8,128)(2,1)} %bitcast.30), custom_call_target="tpu_custom_call" | custom-call | flops 1207959552 | bytes 6586368 | tf_op jit(solution)/shard_map/pallas_call | solution.py:143
  42.6 0.0 copy-start.1
  42.6 0.0 reduce-scatter.2.cloned.1.call-update
  42.6 0.6 copy-done.1
  43.3 0.9 slice_convert_fusion
  44.2 0.3 fusion.11
  44.5 0.0 copy-done
  44.5 4.9 %fusion.10 = (bf16[384,768]{1,0:T(8,128)(2,1)}, bf16[384,768]{1,0:T(8,128)(2,1)}, f32[384]{0:T(512)S(1)}) fusion(f32[384]{0:T(512)S(1)} %fusion.11, bf16[1,1,4,96,768]{4,3,2,1,0:T(8,128)(2,1)} %param.9, bf16[1,1,4,96,768]{4,3,2,1,0:T(8,128)(2,1)} %param.10, bf16[384,768]{1,0:T(8,128)(2,1)} %get-tuple-element.10, bf16[1,768,2048]{2,1,0:T(8,128)(2,1)S(1)} %copy-done, ...), kind=kOutput, calls=%fused_computation.14 | convolution fusion | flops 1213562496 | bytes 7670784 | tf_op jit(solution)/shard_map/dot_general | solution.py:198
  49.3 0.7 all_to_all.10
  50.0 3.2 %all-to-all-start.1 = ((f32[4,1,96]{2,1,0:T(1,128)}), f32[4,1,96]{2,1,0:T(1,128)S(1)}, u32[]{:S(2)}, u32[]{:S(2)}) async-start(f32[4,1,96]{2,1,0:T(1,128)} %all_to_all.10), calls=%async_computation.2 | async-start | bytes 4096 | tf_op jit(solution)/shard_map/all_to_all | solution.py:207
  53.2 4.5 %all-to-all-done.1 = f32[4,1,96]{2,1,0:T(1,128)S(1)} async-done(((f32[4,1,96]{2,1,0:T(1,128)}), f32[4,1,96]{2,1,0:T(1,128)S(1)}, u32[]{:S(2)}, u32[]{:S(2)}) %all-to-all-start.1) | async-done | bytes 1568 | tf_op jit(solution)/shard_map/all_to_all | solution.py:207
  57.8 0.5 broadcast.14
  58.3 0.7 reduce.5
  58.9 0.1 reshape.40
  59.0 2.5 %gather_fusion = f32[256]{0:T(256)} fusion(f32[384]{0:T(512)S(1)} %reshape.40, s32[1024]{0:T(1024)S(1)} %pad_clamp_fusion), kind=kCustom, calls=%fused_computation | custom fusion | bytes 3072 | tf_op jit(solution)/shard_map/gather | solution.py:210
  61.5 21.4 %reduce-scatter.2.cloned.1.call-done = bf16[96,2048]{1,0:T(8,128)(2,1)} async-done(((bf16[768,2048]{1,0:T(8,128)(2,1)}), bf16[96,2048]{1,0:T(8,128)(2,1)}) %reduce-scatter.2.cloned.1.call-update) | async-done | bytes 393232 | tf_op jit(solution)/shard_map/reduce_scatter | solution.py:191
  83.0 1.9 %bitcast_convert_fusion = f32[1,96,2048]{2,1,0:T(8,128)} fusion(bf16[96,2048]{1,0:T(8,128)(2,1)} %reduce-scatter.2.cloned.1.call-done), kind=kLoop, calls=%fused_computation.16 | loop fusion | flops 196608 | bytes 1179648 | tf_op jit(solution)/shard_map/broadcast_in_dim | solution.py:212
  (2 shorter events, 0.0 us)
Async XLA Ops:
  7.2 37.3 %copy-start = (bf16[1,768,2048]{2,1,0:T(8,128)(2,1)S(1)}, bf16[1,768,2048]{2,1,0:T(8,128)(2,1)}, u32[]{:S(2)}) copy-start(bf16[1,768,2048]{2,1,0:T(8,128)(2,1)} %param.11) | copy-start | bytes 9437188
  7.2 75.8 %reduce-scatter.2.cloned.1.call-start = ((), (), s32[]{:S(2)}) async-start(), calls=%async_computation.3 | async-start | bytes 3538944 | tf_op jit(solution)/shard_map/reduce_scatter | solution.py:191
  42.6 0.7 copy-start.1
  50.0 7.8 %all-to-all-start.1 = ((f32[4,1,96]{2,1,0:T(1,128)}), f32[4,1,96]{2,1,0:T(1,128)S(1)}, u32[]{:S(2)}, u32[]{:S(2)}) async-start(f32[4,1,96]{2,1,0:T(1,128)} %all_to_all.10), calls=%async_computation.2 | async-start | bytes 4096 | tf_op jit(solution)/shard_map/all_to_all | solution.py:207
Sparse Core Ops, SparseCore 0:
  42.8 40.1 reduce-scatter.1

commit v13 on v12

--- a/solution.py
+++ b/solution.py
@@ -83,45 +83,61 @@
     )(routes_t, weights_t, rows)
 
 
-def partial_kernel(arrived_hbm, gate_hbm, up_hbm, partial_hbm, hidden_hbm,
-                   tiles_v, pieces_v, gate_v, up_v, hidden_v, out_v, in_sems, out_sems, *, tile):
+def hidden_kernel(gate_ref, up_ref, hidden_ref, hidden_t_ref):
+    gate = gate_ref[...].astype(jnp.float32)
+    sigmoid_gate = 1.0 / (1.0 + jnp.exp(-gate))
+    hidden = (gate * sigmoid_gate * up_ref[...].astype(jnp.float32)).astype(jnp.bfloat16)
+    hidden_ref[...] = hidden
+    hidden_t_ref[...] = jnp.transpose(hidden.astype(jnp.float32)).astype(jnp.bfloat16)
+
+
+def hidden_pair(gate, up):
+    slots, hidden_count = gate.shape
+    vmem = pl.BlockSpec(memory_space=pltpu.VMEM)
+    return pl.pallas_call(
+        hidden_kernel,
+        out_shape=(
+            jax.ShapeDtypeStruct((slots, hidden_count), jnp.bfloat16),
+            jax.ShapeDtypeStruct((hidden_count, slots), jnp.bfloat16),
+        ),
+        in_specs=[vmem, vmem],
+        out_specs=(vmem, vmem),
+        cost_estimate=pl.CostEstimate(
+            flops=8 * gate.size, bytes_accessed=8 * gate.size, transcendentals=gate.size
+        ),
+    )(gate, up)
+
+
+def partial_kernel(arrived_hbm, hidden_t_hbm, partial_hbm, tiles_v, pieces_v, hidden_t_v,
+                   out_v, in_sems, out_sems, *, tile):
     count = tiles_v.shape[0]
     features = count * tile
     lanes = pieces_v.shape[1]
     loads = [
-        pltpu.make_async_copy(gate_hbm, gate_v, in_sems.at[0]),
-        pltpu.make_async_copy(up_hbm, up_v, in_sems.at[1]),
+        pltpu.make_async_copy(hidden_t_hbm, hidden_t_v, in_sems.at[0]),
         pltpu.make_async_copy(
-            arrived_hbm.at[:, pl.ds(features, lanes)], pieces_v, in_sems.at[2]
+            arrived_hbm.at[:, pl.ds(features, lanes)], pieces_v, in_sems.at[1]
         ),
     ]
     tiles = [
         pltpu.make_async_copy(
-            arrived_hbm.at[:, pl.ds(part * tile, tile)], tiles_v.at[part], in_sems.at[3 + part]
+            arrived_hbm.at[:, pl.ds(part * tile, tile)], tiles_v.at[part], in_sems.at[2 + part]
         )
         for part in range(count)
     ]
     for copy in loads + tiles:
         copy.start()
-    loads[0].wait()
     loads[1].wait()
-    gate = gate_v[...].astype(jnp.float32)
-    sigmoid_gate = 1.0 / (1.0 + jnp.exp(-gate))
-    hidden = (gate * sigmoid_gate * up_v[...].astype(jnp.float32)).astype(jnp.bfloat16)
-    hidden_v[...] = hidden
-    store_hidden = pltpu.make_async_copy(hidden_v, hidden_hbm, out_sems.at[count])
-    store_hidden.start()
-    hidden_t = jnp.transpose(hidden.astype(jnp.float32)).astype(jnp.bfloat16)
-    loads[2].wait()
     got = pieces_v[...].astype(jnp.float32)
     weights = (got[:, 0:1] + got[:, 1:2]) + got[:, 2:3]
+    loads[0].wait()
     stores = []
     for part in range(count):
         tiles[part].wait()
         weighted = (weights * tiles_v[part].astype(jnp.float32)).astype(jnp.bfloat16)
-        out_v[part] = jnp.dot(hidden_t, weighted, preferred_element_type=jnp.float32).astype(
-            jnp.bfloat16
-        )
+        out_v[part] = jnp.dot(
+            hidden_t_v[...], weighted, preferred_element_type=jnp.float32
+        ).astype(jnp.bfloat16)
         store = pltpu.make_async_copy(
             out_v.at[part], partial_hbm.at[:, pl.ds(part * tile, tile)], out_sems.at[part]
         )
@@ -129,39 +145,31 @@
         stores.append(store)
     for store in stores:
         store.wait()
-    store_hidden.wait()
-
-
-def weighted_partial(arrived, gate, up, features):
-    slots, hidden_count = gate.shape
+
+
+def weighted_partial(arrived, hidden_t, features):
+    hidden_count, slots = hidden_t.shape
     lanes = arrived.shape[1] - features
     tile = 512 if features % 512 == 0 else features
     count = features // tile
     flops = 2 * slots * hidden_count * features
-    moved = 2 * (arrived.size + 2 * gate.size + hidden_count * features + gate.size)
+    moved = 2 * (arrived.size + hidden_t.size + hidden_count * features)
     anywhere = pl.BlockSpec(memory_space=pl.ANY)
     return pl.pallas_call(
         functools.partial(partial_kernel, tile=tile),
-        out_shape=(
-            jax.ShapeDtypeStruct((hidden_count, features), jnp.bfloat16),
-            jax.ShapeDtypeStruct((slots, hidden_count), jnp.bfloat16),
-        ),
-        in_specs=[anywhere, anywhere, anywhere],
-        out_specs=(anywhere, anywhere),
+        out_shape=jax.ShapeDtypeStruct((hidden_count, features), jnp.bfloat16),
+        in_specs=[anywhere, anywhere],
+        out_specs=anywhere,
         scratch_shapes=[
             pltpu.VMEM((count, slots, tile), jnp.bfloat16),
             pltpu.VMEM((slots, lanes), jnp.bfloat16),
-            pltpu.VMEM((slots, hidden_count), jnp.bfloat16),
-            pltpu.VMEM((slots, hidden_count), jnp.bfloat16),
-            pltpu.VMEM((slots, hidden_count), jnp.bfloat16),
+            pltpu.VMEM((hidden_count, slots), jnp.bfloat16),
             pltpu.VMEM((count, hidden_count, tile), jnp.bfloat16),
-            pltpu.SemaphoreType.DMA((3 + count,)),
-            pltpu.SemaphoreType.DMA((count + 1,)),
+            pltpu.SemaphoreType.DMA((2 + count,)),
+            pltpu.SemaphoreType.DMA((count,)),
         ],
-        cost_estimate=pl.CostEstimate(
-            flops=flops, bytes_accessed=moved, transcendentals=gate.size
-        ),
-    )(arrived, gate, up)
+        cost_estimate=pl.CostEstimate(flops=flops, bytes_accessed=moved, transcendentals=0),
+    )(arrived, hidden_t)
 
 
 def local(out_grad, combine_weight, routes, saved_gate, saved_up, w_down):
@@ -187,7 +195,8 @@
 
     gate_bf = saved_gate.reshape(-1, hidden_count)
     up_bf = saved_up.reshape(-1, hidden_count)
-    partial_grad, hidden = weighted_partial(arrived, gate_bf, up_bf, feature_count)
+    hidden, hidden_t = hidden_pair(gate_bf, up_bf)
+    partial_grad = weighted_partial(arrived, hidden_t, feature_count)
     summed = lax.psum_scatter(partial_grad, "dp", scatter_dimension=0, tiled=True)
     gate_pre = gate_bf.astype(jnp.float32)
     up_pre = up_bf.astype(jnp.float32)

time: 92.1 us -> 91.4 us (level)
  blocking collectives: 26.9 us -> 0 us
  waiting for transfers between devices: 26 us -> 45 us
  starting transfers between devices: 3.26 us -> 8.39 us
  Pallas kernels: 8.5 us -> 10.5 us
    all_to_all x1 -> x0, blocking collectives: 26.9 us -> none  [local(): lax.all_to_all(packed.reshape(experts, capacity, feature_count + lanes),...]
    all_to_all x0 -> x1, waiting for transfers between devices: none -> 18.3 us  [local(): lax.all_to_all(packed.reshape(experts, capacity, feature_count + lanes),...]
    all_to_all x0 -> x1, starting transfers between devices: none -> 5.16 us  [local(): lax.all_to_all(packed.reshape(experts, capacity, feature_count + lanes),...]
    pallas_call x1 -> x2, Pallas kernels: 5.35 us -> 7.34 us  [the longest x1 4.6 us: weighted_partial(): pl.pallas_call(functools.partial(partial_kernel, tile=tile), out_shape=ja...]
  transfers between devices with their start and end apart: 2 -> 3, of which waited for: 2 -> 3; matrix products, arithmetic and copies ran while one was open for 11% -> 11% of each run, Pallas kernels for 0% -> 3%
where the time goes in v13:
time: 91.4 us; the launch traced here: 91 us
  waiting for transfers between devices  45 us (49%)
  between operations  14.1 us (15%)
  Pallas kernels  10.5 us (11%)
  starting transfers between devices  8.39 us (9%)
  matrix products  4.86 us (5%)
  local copies, waits for them, and re-layouts  4.42 us (5%)
  other arithmetic  3.79 us (4%)
    reduce_scatter x1, waiting for transfers between devices, local(): lax.psum_scatter(partial_grad, 'dp', scatter_dimension=0, tiled=True)  22.1 us
    all_to_all x1, waiting for transfers between devices, local(): lax.all_to_all(packed.reshape(experts, capacity, feature_count + lanes),...  18.3 us
    all_to_all x1, starting transfers between devices, local(): lax.all_to_all(packed.reshape(experts, capacity, feature_count + lanes),...  5.16 us
    dot_general x1, matrix products, local(): lax.dot_general(rows, matrix, (((1,), (1,)), ((), ())), preferred_element...  4.86 us
    pallas_call x1, Pallas kernels, weighted_partial(): pl.pallas_call(functools.partial(partial_kernel, tile=tile), out_shape=ja...  4.6 us
    all_to_all x1, waiting for transfers between devices, local(): lax.all_to_all(slot_grad.reshape(experts, capacity), 'expert', split_axis...  4.52 us
    all_to_all x1, starting transfers between devices, local(): lax.all_to_all(slot_grad.reshape(experts, capacity), 'expert', split_axis...  3.22 us
    pallas_call x1, Pallas kernels, pack_slots(): pl.pallas_call(functools.partial(front_kernel, experts=experts, capacity=...  3.14 us
  transfers between devices with their start and end apart: 3, of which 3 were waited for; matrix products, arithmetic and copies ran while one was open for 11% of the time, Pallas kernels for 3%

profile of v13, /device:TPU:0, one launch (start us, length us, event | category | flops | bytes accessed | tf_op | source)
XLA Modules:
  0.0 91.0 jit_solution(3190055617996060875)
XLA Ops:
  7.2 0.0 copy-start
  7.2 3.1 %shard_map.93 = (bf16[384,2176]{1,0:T(8,128)(2,1)}, s32[2,128]{1,0:T(2,128)}) custom-call(s32[2,128]{1,0:T(2,128)} %bitcast.28, f32[2,128]{1,0:T(2,128)} %bitcast.29, bf16[128,2048]{1,0:T(8,128)(2,1)} %rows_ref.1), custom_call_target="tpu_custom_call" | custom-call | flops 201326592 | bytes 2097152 | tf_op jit(solution)/shard_map/pallas_call | solution.py:71
  10.3 5.2 %all-to-all-start = ((bf16[4,96,2176]{2,1,0:T(8,128)(2,1)}), bf16[4,96,2176]{2,1,0:T(8,128)(2,1)}, u32[]{:S(2)}, u32[]{:S(2)}) async-start(bf16[4,96,2176]{2,1,0:T(8,128)(2,1)} %bitcast.24), calls=%async_computation | async-start | bytes 3342336 | tf_op jit(solution)/shard_map/all_to_all | solution.py:185
  15.5 0.0 reduce-scatter.2.cloned.1.call-start
  15.5 2.7 %shard_map.94 = (bf16[384,768]{1,0:T(8,128)(2,1)}, bf16[768,384]{1,0:T(8,128)(2,1)}) custom-call(bf16[384,768]{1,0:T(8,128)(2,1)} %bitcast.25, bf16[384,768]{1,0:T(8,128)(2,1)} %bitcast.26), custom_call_target="tpu_custom_call" | custom-call | flops 2359296 | bytes 2359296 | tf_op jit(solution)/shard_map/pallas_call | solution.py:97
  18.2 18.3 %all-to-all-done = bf16[4,96,2176]{2,1,0:T(8,128)(2,1)} async-done(((bf16[4,96,2176]{2,1,0:T(8,128)(2,1)}), bf16[4,96,2176]{2,1,0:T(8,128)(2,1)}, u32[]{:S(2)}, u32[]{:S(2)}) %all-to-all-start) | async-done | bytes 1671200 | tf_op jit(solution)/shard_map/all_to_all | solution.py:185
  36.6 4.6 %shard_map.95 = bf16[768,2048]{1,0:T(8,128)(2,1)} custom-call(bf16[384,2176]{1,0:T(8,128)(2,1)} %bitcast.3.arrived_hbm, bf16[768,384]{1,0:T(8,128)(2,1)} %get-tuple-element.9.hidden_t_hbm), custom_call_target="tpu_custom_call" | custom-call | flops 1207959552 | bytes 5406720 | tf_op jit(solution)/shard_map/pallas_call | solution.py:158
  41.2 0.0 copy-start.1
  41.2 0.0 reduce-scatter.2.cloned.1.call-update
  41.2 0.6 copy-done.1
  41.8 0.9 slice_convert_fusion
  42.8 0.3 fusion.11
  43.0 0.0 copy-done
  43.0 4.9 %fusion.10 = (bf16[384,768]{1,0:T(8,128)(2,1)}, bf16[384,768]{1,0:T(8,128)(2,1)}, f32[384]{0:T(512)S(1)}) fusion(f32[384]{0:T(512)S(1)} %fusion.11, bf16[1,1,4,96,768]{4,3,2,1,0:T(8,128)(2,1)} %param.9, bf16[1,1,4,96,768]{4,3,2,1,0:T(8,128)(2,1)} %param.10, bf16[384,768]{1,0:T(8,128)(2,1)} %get-tuple-element.10, bf16[1,768,2048]{2,1,0:T(8,128)(2,1)S(1)} %copy-done, ...), kind=kOutput, calls=%fused_computation.14 | convolution fusion | flops 1213562496 | bytes 7670784 | tf_op jit(solution)/shard_map/dot_general | solution.py:207
  47.9 0.7 all_to_all.10
  48.5 3.2 %all-to-all-start.1 = ((f32[4,1,96]{2,1,0:T(1,128)}), f32[4,1,96]{2,1,0:T(1,128)S(1)}, u32[]{:S(2)}, u32[]{:S(2)}) async-start(f32[4,1,96]{2,1,0:T(1,128)} %all_to_all.10), calls=%async_computation.2 | async-start | bytes 4096 | tf_op jit(solution)/shard_map/all_to_all | solution.py:216
  51.8 4.5 %all-to-all-done.1 = f32[4,1,96]{2,1,0:T(1,128)S(1)} async-done(((f32[4,1,96]{2,1,0:T(1,128)}), f32[4,1,96]{2,1,0:T(1,128)S(1)}, u32[]{:S(2)}, u32[]{:S(2)}) %all-to-all-start.1) | async-done | bytes 1568 | tf_op jit(solution)/shard_map/all_to_all | solution.py:216
  56.3 0.5 broadcast.14
  56.8 0.7 reduce.5
  57.5 0.1 reshape.40
  57.6 2.5 %gather_fusion = f32[256]{0:T(256)} fusion(f32[384]{0:T(512)S(1)} %reshape.40, s32[1024]{0:T(1024)S(1)} %pad_clamp_fusion), kind=kCustom, calls=%fused_computation | custom fusion | bytes 3072 | tf_op jit(solution)/shard_map/gather | solution.py:219
  60.1 22.1 %reduce-scatter.2.cloned.1.call-done = bf16[96,2048]{1,0:T(8,128)(2,1)} async-done(((bf16[768,2048]{1,0:T(8,128)(2,1)}), bf16[96,2048]{1,0:T(8,128)(2,1)}) %reduce-scatter.2.cloned.1.call-update) | async-done | bytes 393232 | tf_op jit(solution)/shard_map/reduce_scatter | solution.py:200
  82.2 1.9 %bitcast_convert_fusion = f32[1,96,2048]{2,1,0:T(8,128)} fusion(bf16[96,2048]{1,0:T(8,128)(2,1)} %reduce-scatter.2.cloned.1.call-done), kind=kLoop, calls=%fused_computation.16 | loop fusion | flops 196608 | bytes 1179648 | tf_op jit(solution)/shard_map/broadcast_in_dim | solution.py:221
  (2 shorter events, 0.0 us)
Async XLA Ops:
  7.2 35.9 %copy-start = (bf16[1,768,2048]{2,1,0:T(8,128)(2,1)S(1)}, bf16[1,768,2048]{2,1,0:T(8,128)(2,1)}, u32[]{:S(2)}) copy-start(bf16[1,768,2048]{2,1,0:T(8,128)(2,1)} %param.11) | copy-start | bytes 9437188
  10.3 26.2 %all-to-all-start = ((bf16[4,96,2176]{2,1,0:T(8,128)(2,1)}), bf16[4,96,2176]{2,1,0:T(8,128)(2,1)}, u32[]{:S(2)}, u32[]{:S(2)}) async-start(bf16[4,96,2176]{2,1,0:T(8,128)(2,1)} %bitcast.24), calls=%async_computation | async-start | bytes 3342336 | tf_op jit(solution)/shard_map/all_to_all | solution.py:185
  15.5 66.7 %reduce-scatter.2.cloned.1.call-start = ((), (), s32[]{:S(2)}) async-start(), calls=%async_computation.3 | async-start | bytes 3538944 | tf_op jit(solution)/shard_map/reduce_scatter | solution.py:200
  41.2 0.7 copy-start.1
  48.5 7.8 %all-to-all-start.1 = ((f32[4,1,96]{2,1,0:T(1,128)}), f32[4,1,96]{2,1,0:T(1,128)S(1)}, u32[]{:S(2)}, u32[]{:S(2)}) async-start(f32[4,1,96]{2,1,0:T(1,128)} %all_to_all.10), calls=%async_computation.2 | async-start | bytes 4096 | tf_op jit(solution)/shard_map/all_to_all | solution.py:216
Sparse Core Ops, SparseCore 0:
  41.3 40.8 reduce-scatter.1

commit v14 on v13

--- a/solution.py
+++ b/solution.py
@@ -128,15 +128,15 @@
     for copy in loads + tiles:
         copy.start()
     loads[1].wait()
-    got = pieces_v[...].astype(jnp.float32)
-    weights = (got[:, 0:1] + got[:, 1:2]) + got[:, 2:3]
+    got = jnp.transpose(pieces_v[...].astype(jnp.float32))
+    weights = (got[0:1, :] + got[1:2, :]) + got[2:3, :]
     loads[0].wait()
+    scaled = (hidden_t_v[...].astype(jnp.float32) * weights).astype(jnp.bfloat16)
     stores = []
     for part in range(count):
         tiles[part].wait()
-        weighted = (weights * tiles_v[part].astype(jnp.float32)).astype(jnp.bfloat16)
         out_v[part] = jnp.dot(
-            hidden_t_v[...], weighted, preferred_element_type=jnp.float32
+            scaled, tiles_v[part], preferred_element_type=jnp.float32
         ).astype(jnp.bfloat16)
         store = pltpu.make_async_copy(
             out_v.at[part], partial_hbm.at[:, pl.ds(part * tile, tile)], out_sems.at[part]

time: 91.4 us -> 91.4 us (level)
  no operation moved by 1% of the time
where the time goes in v14:
time: 91.4 us; the launch traced here: 91 us
  waiting for transfers between devices  45 us (49%)
  between operations  14.1 us (15%)
  Pallas kernels  10.5 us (11%)
  starting transfers between devices  8.39 us (9%)
  matrix products  4.85 us (5%)
  local copies, waits for them, and re-layouts  4.42 us (5%)
  other arithmetic  3.79 us (4%)
    reduce_scatter x1, waiting for transfers between devices, local(): lax.psum_scatter(partial_grad, 'dp', scatter_dimension=0, tiled=True)  22.1 us
    all_to_all x1, waiting for transfers between devices, local(): lax.all_to_all(packed.reshape(experts, capacity, feature_count + lanes),...  18.3 us
    all_to_all x1, starting transfers between devices, local(): lax.all_to_all(packed.reshape(experts, capacity, feature_count + lanes),...  5.16 us
    dot_general x1, matrix products, local(): lax.dot_general(rows, matrix, (((1,), (1,)), ((), ())), preferred_element...  4.85 us
    pallas_call x1, Pallas kernels, weighted_partial(): pl.pallas_call(functools.partial(partial_kernel, tile=tile), out_shape=ja...  4.61 us
    all_to_all x1, waiting for transfers between devices, local(): lax.all_to_all(slot_grad.reshape(experts, capacity), 'expert', split_axis...  4.52 us
    all_to_all x1, starting transfers between devices, local(): lax.all_to_all(slot_grad.reshape(experts, capacity), 'expert', split_axis...  3.22 us
    pallas_call x1, Pallas kernels, pack_slots(): pl.pallas_call(functools.partial(front_kernel, experts=experts, capacity=...  3.14 us
  transfers between devices with their start and end apart: 3, of which 3 were waited for; matrix products, arithmetic and copies ran while one was open for 11% of the time, Pallas kernels for 3%

profile of v14, /device:TPU:0, one launch (start us, length us, event | category | flops | bytes accessed | tf_op | source)
XLA Modules:
  0.0 91.0 jit_solution(2170137954539826761)
XLA Ops:
  7.2 0.0 copy-start
  7.2 3.1 %shard_map.93 = (bf16[384,2176]{1,0:T(8,128)(2,1)}, s32[2,128]{1,0:T(2,128)}) custom-call(s32[2,128]{1,0:T(2,128)} %bitcast.28, f32[2,128]{1,0:T(2,128)} %bitcast.29, bf16[128,2048]{1,0:T(8,128)(2,1)} %rows_ref.1), custom_call_target="tpu_custom_call" | custom-call | flops 201326592 | bytes 2097152 | tf_op jit(solution)/shard_map/pallas_call | solution.py:71
  10.3 5.2 %all-to-all-start = ((bf16[4,96,2176]{2,1,0:T(8,128)(2,1)}), bf16[4,96,2176]{2,1,0:T(8,128)(2,1)}, u32[]{:S(2)}, u32[]{:S(2)}) async-start(bf16[4,96,2176]{2,1,0:T(8,128)(2,1)} %bitcast.24), calls=%async_computation | async-start | bytes 3342336 | tf_op jit(solution)/shard_map/all_to_all | solution.py:185
  15.5 0.0 reduce-scatter.2.cloned.1.call-start
  15.5 2.7 %shard_map.94 = (bf16[384,768]{1,0:T(8,128)(2,1)}, bf16[768,384]{1,0:T(8,128)(2,1)}) custom-call(bf16[384,768]{1,0:T(8,128)(2,1)} %bitcast.25, bf16[384,768]{1,0:T(8,128)(2,1)} %bitcast.26), custom_call_target="tpu_custom_call" | custom-call | flops 2359296 | bytes 2359296 | tf_op jit(solution)/shard_map/pallas_call | solution.py:97
  18.2 18.3 %all-to-all-done = bf16[4,96,2176]{2,1,0:T(8,128)(2,1)} async-done(((bf16[4,96,2176]{2,1,0:T(8,128)(2,1)}), bf16[4,96,2176]{2,1,0:T(8,128)(2,1)}, u32[]{:S(2)}, u32[]{:S(2)}) %all-to-all-start) | async-done | bytes 1671200 | tf_op jit(solution)/shard_map/all_to_all | solution.py:185
  36.6 4.6 %shard_map.95 = bf16[768,2048]{1,0:T(8,128)(2,1)} custom-call(bf16[384,2176]{1,0:T(8,128)(2,1)} %bitcast.3.arrived_hbm, bf16[768,384]{1,0:T(8,128)(2,1)} %get-tuple-element.9.hidden_t_hbm), custom_call_target="tpu_custom_call" | custom-call | flops 1207959552 | bytes 5406720 | tf_op jit(solution)/shard_map/pallas_call | solution.py:158
  41.2 0.0 copy-start.1
  41.2 0.0 reduce-scatter.2.cloned.1.call-update
  41.2 0.6 copy-done.1
  41.9 0.9 slice_convert_fusion
  42.8 0.3 fusion.11
  43.0 0.0 copy-done
  43.0 4.9 %fusion.10 = (bf16[384,768]{1,0:T(8,128)(2,1)}, bf16[384,768]{1,0:T(8,128)(2,1)}, f32[384]{0:T(512)S(1)}) fusion(f32[384]{0:T(512)S(1)} %fusion.11, bf16[1,1,4,96,768]{4,3,2,1,0:T(8,128)(2,1)} %param.9, bf16[1,1,4,96,768]{4,3,2,1,0:T(8,128)(2,1)} %param.10, bf16[384,768]{1,0:T(8,128)(2,1)} %get-tuple-element.10, bf16[1,768,2048]{2,1,0:T(8,128)(2,1)S(1)} %copy-done, ...), kind=kOutput, calls=%fused_computation.14 | convolution fusion | flops 1213562496 | bytes 7670784 | tf_op jit(solution)/shard_map/dot_general | solution.py:207
  47.9 0.7 all_to_all.10
  48.6 3.2 %all-to-all-start.1 = ((f32[4,1,96]{2,1,0:T(1,128)}), f32[4,1,96]{2,1,0:T(1,128)S(1)}, u32[]{:S(2)}, u32[]{:S(2)}) async-start(f32[4,1,96]{2,1,0:T(1,128)} %all_to_all.10), calls=%async_computation.2 | async-start | bytes 4096 | tf_op jit(solution)/shard_map/all_to_all | solution.py:216
  51.8 4.5 %all-to-all-done.1 = f32[4,1,96]{2,1,0:T(1,128)S(1)} async-done(((f32[4,1,96]{2,1,0:T(1,128)}), f32[4,1,96]{2,1,0:T(1,128)S(1)}, u32[]{:S(2)}, u32[]{:S(2)}) %all-to-all-start.1) | async-done | bytes 1568 | tf_op jit(solution)/shard_map/all_to_all | solution.py:216
  56.3 0.5 broadcast.14
  56.8 0.7 reduce.5
  57.5 0.1 reshape.40
  57.6 2.5 %gather_fusion = f32[256]{0:T(256)} fusion(f32[384]{0:T(512)S(1)} %reshape.40, s32[1024]{0:T(1024)S(1)} %pad_clamp_fusion), kind=kCustom, calls=%fused_computation | custom fusion | bytes 3072 | tf_op jit(solution)/shard_map/gather | solution.py:219
  60.1 22.1 %reduce-scatter.2.cloned.1.call-done = bf16[96,2048]{1,0:T(8,128)(2,1)} async-done(((bf16[768,2048]{1,0:T(8,128)(2,1)}), bf16[96,2048]{1,0:T(8,128)(2,1)}) %reduce-scatter.2.cloned.1.call-update) | async-done | bytes 393232 | tf_op jit(solution)/shard_map/reduce_scatter | solution.py:200
  82.2 1.9 %bitcast_convert_fusion = f32[1,96,2048]{2,1,0:T(8,128)} fusion(bf16[96,2048]{1,0:T(8,128)(2,1)} %reduce-scatter.2.cloned.1.call-done), kind=kLoop, calls=%fused_computation.16 | loop fusion | flops 196608 | bytes 1179648 | tf_op jit(solution)/shard_map/broadcast_in_dim | solution.py:221
  (2 shorter events, 0.0 us)
Async XLA Ops:
  7.2 35.9 %copy-start = (bf16[1,768,2048]{2,1,0:T(8,128)(2,1)S(1)}, bf16[1,768,2048]{2,1,0:T(8,128)(2,1)}, u32[]{:S(2)}) copy-start(bf16[1,768,2048]{2,1,0:T(8,128)(2,1)} %param.11) | copy-start | bytes 9437188
  10.3 26.2 %all-to-all-start = ((bf16[4,96,2176]{2,1,0:T(8,128)(2,1)}), bf16[4,96,2176]{2,1,0:T(8,128)(2,1)}, u32[]{:S(2)}, u32[]{:S(2)}) async-start(bf16[4,96,2176]{2,1,0:T(8,128)(2,1)} %bitcast.24), calls=%async_computation | async-start | bytes 3342336 | tf_op jit(solution)/shard_map/all_to_all | solution.py:185
  15.5 66.7 %reduce-scatter.2.cloned.1.call-start = ((), (), s32[]{:S(2)}) async-start(), calls=%async_computation.3 | async-start | bytes 3538944 | tf_op jit(solution)/shard_map/reduce_scatter | solution.py:200
  41.2 0.7 copy-start.1
  48.6 7.8 %all-to-all-start.1 = ((f32[4,1,96]{2,1,0:T(1,128)}), f32[4,1,96]{2,1,0:T(1,128)S(1)}, u32[]{:S(2)}, u32[]{:S(2)}) async-start(f32[4,1,96]{2,1,0:T(1,128)} %all_to_all.10), calls=%async_computation.2 | async-start | bytes 4096 | tf_op jit(solution)/shard_map/all_to_all | solution.py:216
Sparse Core Ops, SparseCore 0:
  41.3 40.8 reduce-scatter.1

commit v15 on v13

--- a/solution.py
+++ b/solution.py
@@ -20,9 +20,10 @@
     return jnp.stack([high, middle, low], axis=-1).astype(jnp.bfloat16)
 
 
-def front_kernel(routes_ref, weights_ref, rows_ref, packed_ref, position_ref, *, experts, capacity):
+def front_kernel(routes_ref, weights_ref, rows_ref, packed_hbm, position_ref, packed_v, sems, *,
+                 experts, capacity):
     route_count, tokens = routes_ref.shape
-    slots, width = packed_ref.shape
+    slots, width = packed_v.shape
     features = rows_ref.shape[1]
     padded = -(-experts // 8) * 8
     routes = routes_ref[...]
@@ -50,17 +51,33 @@
         )
     pick = pick.astype(jnp.bfloat16)
     tile = 512 if features % 512 == 0 else features
-    for start in range(0, features, tile):
-        packed_ref[:, start:start + tile] = jnp.dot(
+    stores = []
+    for part, start in enumerate(range(0, features, tile)):
+        packed_v[:, start:start + tile] = jnp.dot(
             pick, rows_ref[:, start:start + tile], preferred_element_type=jnp.float32
         ).astype(jnp.bfloat16)
+        store = pltpu.make_async_copy(
+            packed_v.at[:, pl.ds(start, tile)], packed_hbm.at[:, pl.ds(start, tile)],
+            sems.at[part],
+        )
+        store.start()
+        stores.append(store)
     high = weight.astype(jnp.bfloat16).astype(jnp.float32)
     rest = weight - high
     middle = rest.astype(jnp.bfloat16).astype(jnp.float32)
     low = rest - middle
     column = lax.broadcasted_iota(jnp.int32, (slots, width - features), 1)
     pieces = jnp.where(column == 0, high, jnp.where(column == 1, middle, jnp.where(column == 2, low, 0.0)))
-    packed_ref[:, features:] = pieces.astype(jnp.bfloat16)
+    packed_v[:, features:] = pieces.astype(jnp.bfloat16)
+    store = pltpu.make_async_copy(
+        packed_v.at[:, pl.ds(features, width - features)],
+        packed_hbm.at[:, pl.ds(features, width - features)],
+        sems.at[len(stores)],
+    )
+    store.start()
+    stores.append(store)
+    for store in stores:
+        store.wait()
 
 
 def pack_slots(routes_t, weights_t, rows, experts, capacity):
@@ -75,7 +92,11 @@
             jax.ShapeDtypeStruct((route_count, tokens), jnp.int32),
         ),
         in_specs=[vmem, vmem, vmem],
-        out_specs=(vmem, vmem),
+        out_specs=(pl.BlockSpec(memory_space=pl.ANY), vmem),
+        scratch_shapes=[
+            pltpu.VMEM((slots, features + 128), jnp.bfloat16),
+            pltpu.SemaphoreType.DMA((features // (512 if features % 512 == 0 else features) + 1,)),
+        ],
         cost_estimate=pl.CostEstimate(
             flops=2 * slots * tokens * features, bytes_accessed=2 * (rows.size + slots * features),
             transcendentals=0,

time: 91.4 us -> 91.7 us (level)
  no operation moved by 1% of the time
where the time goes in v15:
time: 91.7 us; the launch traced here: 91.3 us
  waiting for transfers between devices  45 us (49%)
  between operations  14.1 us (15%)
  Pallas kernels  10.8 us (12%)
  starting transfers between devices  8.4 us (9%)
  matrix products  4.87 us (5%)
  local copies, waits for them, and re-layouts  4.42 us (5%)
  other arithmetic  3.79 us (4%)
    reduce_scatter x1, waiting for transfers between devices, local(): lax.psum_scatter(partial_grad, 'dp', scatter_dimension=0, tiled=True)  22.1 us
    all_to_all x1, waiting for transfers between devices, local(): lax.all_to_all(packed.reshape(experts, capacity, feature_count + lanes),...  18.3 us
    all_to_all x1, starting transfers between devices, local(): lax.all_to_all(packed.reshape(experts, capacity, feature_count + lanes),...  5.17 us
    dot_general x1, matrix products, local(): lax.dot_general(rows, matrix, (((1,), (1,)), ((), ())), preferred_element...  4.87 us
    pallas_call x1, Pallas kernels, weighted_partial(): pl.pallas_call(functools.partial(partial_kernel, tile=tile), out_shape=ja...  4.6 us
    all_to_all x1, waiting for transfers between devices, local(): lax.all_to_all(slot_grad.reshape(experts, capacity), 'expert', split_axis...  4.52 us
    pallas_call x1, Pallas kernels, pack_slots(): pl.pallas_call(functools.partial(front_kernel, experts=experts, capacity=...  3.44 us
    all_to_all x1, starting transfers between devices, local(): lax.all_to_all(slot_grad.reshape(experts, capacity), 'expert', split_axis...  3.22 us
  transfers between devices with their start and end apart: 3, of which 3 were waited for; matrix products, arithmetic and copies ran while one was open for 11% of the time, Pallas kernels for 3%

profile of v15, /device:TPU:0, one launch (start us, length us, event | category | flops | bytes accessed | tf_op | source)
XLA Modules:
  0.0 91.3 jit_solution(14245303476084587089)
XLA Ops:
  7.2 0.0 copy-start
  7.2 3.4 %shard_map.93 = (bf16[384,2176]{1,0:T(8,128)(2,1)}, s32[2,128]{1,0:T(2,128)}) custom-call(s32[2,128]{1,0:T(2,128)} %bitcast.28, f32[2,128]{1,0:T(2,128)} %bitcast.29, bf16[128,2048]{1,0:T(8,128)(2,1)} %rows_ref.1), custom_call_target="tpu_custom_call" | custom-call | flops 201326592 | bytes 2097152 | tf_op jit(solution)/shard_map/pallas_call | solution.py:88
  10.6 5.2 %all-to-all-start = ((bf16[4,96,2176]{2,1,0:T(8,128)(2,1)}), bf16[4,96,2176]{2,1,0:T(8,128)(2,1)}, u32[]{:S(2)}, u32[]{:S(2)}) async-start(bf16[4,96,2176]{2,1,0:T(8,128)(2,1)} %bitcast.24), calls=%async_computation | async-start | bytes 3342336 | tf_op jit(solution)/shard_map/all_to_all | solution.py:206
  15.8 0.0 reduce-scatter.2.cloned.1.call-start
  15.8 2.7 %shard_map.94 = (bf16[384,768]{1,0:T(8,128)(2,1)}, bf16[768,384]{1,0:T(8,128)(2,1)}) custom-call(bf16[384,768]{1,0:T(8,128)(2,1)} %bitcast.25, bf16[384,768]{1,0:T(8,128)(2,1)} %bitcast.26), custom_call_target="tpu_custom_call" | custom-call | flops 2359296 | bytes 2359296 | tf_op jit(solution)/shard_map/pallas_call | solution.py:118
  18.5 18.3 %all-to-all-done = bf16[4,96,2176]{2,1,0:T(8,128)(2,1)} async-done(((bf16[4,96,2176]{2,1,0:T(8,128)(2,1)}), bf16[4,96,2176]{2,1,0:T(8,128)(2,1)}, u32[]{:S(2)}, u32[]{:S(2)}) %all-to-all-start) | async-done | bytes 1671200 | tf_op jit(solution)/shard_map/all_to_all | solution.py:206
  36.9 4.6 %shard_map.95 = bf16[768,2048]{1,0:T(8,128)(2,1)} custom-call(bf16[384,2176]{1,0:T(8,128)(2,1)} %bitcast.3.arrived_hbm, bf16[768,384]{1,0:T(8,128)(2,1)} %get-tuple-element.9.hidden_t_hbm), custom_call_target="tpu_custom_call" | custom-call | flops 1207959552 | bytes 5406720 | tf_op jit(solution)/shard_map/pallas_call | solution.py:179
  41.5 0.0 copy-start.1
  41.5 0.0 reduce-scatter.2.cloned.1.call-update
  41.5 0.6 copy-done.1
  42.2 0.9 slice_convert_fusion
  43.1 0.3 fusion.11
  43.3 0.0 copy-done
  43.3 4.9 %fusion.10 = (bf16[384,768]{1,0:T(8,128)(2,1)}, bf16[384,768]{1,0:T(8,128)(2,1)}, f32[384]{0:T(512)S(1)}) fusion(f32[384]{0:T(512)S(1)} %fusion.11, bf16[1,1,4,96,768]{4,3,2,1,0:T(8,128)(2,1)} %param.9, bf16[1,1,4,96,768]{4,3,2,1,0:T(8,128)(2,1)} %param.10, bf16[384,768]{1,0:T(8,128)(2,1)} %get-tuple-element.10, bf16[1,768,2048]{2,1,0:T(8,128)(2,1)S(1)} %copy-done, ...), kind=kOutput, calls=%fused_computation.14 | convolution fusion | flops 1213562496 | bytes 7670784 | tf_op jit(solution)/shard_map/dot_general | solution.py:228
  48.2 0.7 all_to_all.10
  48.9 3.2 %all-to-all-start.1 = ((f32[4,1,96]{2,1,0:T(1,128)}), f32[4,1,96]{2,1,0:T(1,128)S(1)}, u32[]{:S(2)}, u32[]{:S(2)}) async-start(f32[4,1,96]{2,1,0:T(1,128)} %all_to_all.10), calls=%async_computation.2 | async-start | bytes 4096 | tf_op jit(solution)/shard_map/all_to_all | solution.py:237
  52.1 4.5 %all-to-all-done.1 = f32[4,1,96]{2,1,0:T(1,128)S(1)} async-done(((f32[4,1,96]{2,1,0:T(1,128)}), f32[4,1,96]{2,1,0:T(1,128)S(1)}, u32[]{:S(2)}, u32[]{:S(2)}) %all-to-all-start.1) | async-done | bytes 1568 | tf_op jit(solution)/shard_map/all_to_all | solution.py:237
  56.6 0.5 broadcast.14
  57.2 0.7 reduce.5
  57.8 0.1 reshape.40
  57.9 2.5 %gather_fusion = f32[256]{0:T(256)} fusion(f32[384]{0:T(512)S(1)} %reshape.40, s32[1024]{0:T(1024)S(1)} %pad_clamp_fusion), kind=kCustom, calls=%fused_computation | custom fusion | bytes 3072 | tf_op jit(solution)/shard_map/gather | solution.py:240
  60.4 22.1 %reduce-scatter.2.cloned.1.call-done = bf16[96,2048]{1,0:T(8,128)(2,1)} async-done(((bf16[768,2048]{1,0:T(8,128)(2,1)}), bf16[96,2048]{1,0:T(8,128)(2,1)}) %reduce-scatter.2.cloned.1.call-update) | async-done | bytes 393232 | tf_op jit(solution)/shard_map/reduce_scatter | solution.py:221
  82.5 1.9 %bitcast_convert_fusion = f32[1,96,2048]{2,1,0:T(8,128)} fusion(bf16[96,2048]{1,0:T(8,128)(2,1)} %reduce-scatter.2.cloned.1.call-done), kind=kLoop, calls=%fused_computation.16 | loop fusion | flops 196608 | bytes 1179648 | tf_op jit(solution)/shard_map/broadcast_in_dim | solution.py:242
  (2 shorter events, 0.0 us)
Async XLA Ops:
  7.2 36.2 %copy-start = (bf16[1,768,2048]{2,1,0:T(8,128)(2,1)S(1)}, bf16[1,768,2048]{2,1,0:T(8,128)(2,1)}, u32[]{:S(2)}) copy-start(bf16[1,768,2048]{2,1,0:T(8,128)(2,1)} %param.11) | copy-start | bytes 9437188
  10.6 26.2 %all-to-all-start = ((bf16[4,96,2176]{2,1,0:T(8,128)(2,1)}), bf16[4,96,2176]{2,1,0:T(8,128)(2,1)}, u32[]{:S(2)}, u32[]{:S(2)}) async-start(bf16[4,96,2176]{2,1,0:T(8,128)(2,1)} %bitcast.24), calls=%async_computation | async-start | bytes 3342336 | tf_op jit(solution)/shard_map/all_to_all | solution.py:206
  15.8 66.7 %reduce-scatter.2.cloned.1.call-start = ((), (), s32[]{:S(2)}) async-start(), calls=%async_computation.3 | async-start | bytes 3538944 | tf_op jit(solution)/shard_map/reduce_scatter | solution.py:221
  41.5 0.7 copy-start.1
  48.9 7.8 %all-to-all-start.1 = ((f32[4,1,96]{2,1,0:T(1,128)}), f32[4,1,96]{2,1,0:T(1,128)S(1)}, u32[]{:S(2)}, u32[]{:S(2)}) async-start(f32[4,1,96]{2,1,0:T(1,128)} %all_to_all.10), calls=%async_computation.2 | async-start | bytes 4096 | tf_op jit(solution)/shard_map/all_to_all | solution.py:237
Sparse Core Ops, SparseCore 0:
  41.6 40.8 reduce-scatter.1

commit v16 on v13

--- a/solution.py
+++ b/solution.py
@@ -150,7 +150,7 @@
 def weighted_partial(arrived, hidden_t, features):
     hidden_count, slots = hidden_t.shape
     lanes = arrived.shape[1] - features
-    tile = 512 if features % 512 == 0 else features
+    tile = 1024 if features % 1024 == 0 else features
     count = features // tile
     flops = 2 * slots * hidden_count * features
     moved = 2 * (arrived.size + hidden_t.size + hidden_count * features)

time: 91.4 us -> 91.4 us (level)
  no operation moved by 1% of the time
where the time goes in v16:
time: 91.4 us; the launch traced here: 91 us
  waiting for transfers between devices  45 us (49%)
  between operations  14.1 us (15%)
  Pallas kernels  10.5 us (11%)
  starting transfers between devices  8.39 us (9%)
  matrix products  4.87 us (5%)
  local copies, waits for them, and re-layouts  4.42 us (5%)
  other arithmetic  3.79 us (4%)
    reduce_scatter x1, waiting for transfers between devices, local(): lax.psum_scatter(partial_grad, 'dp', scatter_dimension=0, tiled=True)  22.1 us
    all_to_all x1, waiting for transfers between devices, local(): lax.all_to_all(packed.reshape(experts, capacity, feature_count + lanes),...  18.3 us
    all_to_all x1, starting transfers between devices, local(): lax.all_to_all(packed.reshape(experts, capacity, feature_count + lanes),...  5.16 us
    dot_general x1, matrix products, local(): lax.dot_general(rows, matrix, (((1,), (1,)), ((), ())), preferred_element...  4.87 us
    pallas_call x1, Pallas kernels, weighted_partial(): pl.pallas_call(functools.partial(partial_kernel, tile=tile), out_shape=ja...  4.62 us
    all_to_all x1, waiting for transfers between devices, local(): lax.all_to_all(slot_grad.reshape(experts, capacity), 'expert', split_axis...  4.52 us
    all_to_all x1, starting transfers between devices, local(): lax.all_to_all(slot_grad.reshape(experts, capacity), 'expert', split_axis...  3.22 us
    pallas_call x1, Pallas kernels, pack_slots(): pl.pallas_call(functools.partial(front_kernel, experts=experts, capacity=...  3.14 us
  transfers between devices with their start and end apart: 3, of which 3 were waited for; matrix products, arithmetic and copies ran while one was open for 11% of the time, Pallas kernels for 3%

profile of v16, /device:TPU:0, one launch (start us, length us, event | category | flops | bytes accessed | tf_op | source)
XLA Modules:
  0.0 91.0 jit_solution(5020573526807374798)
XLA Ops:
  7.2 0.0 copy-start
  7.2 3.1 %shard_map.93 = (bf16[384,2176]{1,0:T(8,128)(2,1)}, s32[2,128]{1,0:T(2,128)}) custom-call(s32[2,128]{1,0:T(2,128)} %bitcast.28, f32[2,128]{1,0:T(2,128)} %bitcast.29, bf16[128,2048]{1,0:T(8,128)(2,1)} %rows_ref.1), custom_call_target="tpu_custom_call" | custom-call | flops 201326592 | bytes 2097152 | tf_op jit(solution)/shard_map/pallas_call | solution.py:71
  10.3 5.2 %all-to-all-start = ((bf16[4,96,2176]{2,1,0:T(8,128)(2,1)}), bf16[4,96,2176]{2,1,0:T(8,128)(2,1)}, u32[]{:S(2)}, u32[]{:S(2)}) async-start(bf16[4,96,2176]{2,1,0:T(8,128)(2,1)} %bitcast.24), calls=%async_computation | async-start | bytes 3342336 | tf_op jit(solution)/shard_map/all_to_all | solution.py:185
  15.5 0.0 reduce-scatter.2.cloned.1.call-start
  15.5 2.7 %shard_map.94 = (bf16[384,768]{1,0:T(8,128)(2,1)}, bf16[768,384]{1,0:T(8,128)(2,1)}) custom-call(bf16[384,768]{1,0:T(8,128)(2,1)} %bitcast.25, bf16[384,768]{1,0:T(8,128)(2,1)} %bitcast.26), custom_call_target="tpu_custom_call" | custom-call | flops 2359296 | bytes 2359296 | tf_op jit(solution)/shard_map/pallas_call | solution.py:97
  18.2 18.3 %all-to-all-done = bf16[4,96,2176]{2,1,0:T(8,128)(2,1)} async-done(((bf16[4,96,2176]{2,1,0:T(8,128)(2,1)}), bf16[4,96,2176]{2,1,0:T(8,128)(2,1)}, u32[]{:S(2)}, u32[]{:S(2)}) %all-to-all-start) | async-done | bytes 1671200 | tf_op jit(solution)/shard_map/all_to_all | solution.py:185
  36.6 4.6 %shard_map.95 = bf16[768,2048]{1,0:T(8,128)(2,1)} custom-call(bf16[384,2176]{1,0:T(8,128)(2,1)} %bitcast.3.arrived_hbm, bf16[768,384]{1,0:T(8,128)(2,1)} %get-tuple-element.9.hidden_t_hbm), custom_call_target="tpu_custom_call" | custom-call | flops 1207959552 | bytes 5406720 | tf_op jit(solution)/shard_map/pallas_call | solution.py:158
  41.2 0.0 copy-start.1
  41.2 0.0 reduce-scatter.2.cloned.1.call-update
  41.2 0.6 copy-done.1
  41.9 0.9 slice_convert_fusion
  42.8 0.3 fusion.11
  43.0 0.0 copy-done
  43.0 4.9 %fusion.10 = (bf16[384,768]{1,0:T(8,128)(2,1)}, bf16[384,768]{1,0:T(8,128)(2,1)}, f32[384]{0:T(512)S(1)}) fusion(f32[384]{0:T(512)S(1)} %fusion.11, bf16[1,1,4,96,768]{4,3,2,1,0:T(8,128)(2,1)} %param.9, bf16[1,1,4,96,768]{4,3,2,1,0:T(8,128)(2,1)} %param.10, bf16[384,768]{1,0:T(8,128)(2,1)} %get-tuple-element.10, bf16[1,768,2048]{2,1,0:T(8,128)(2,1)S(1)} %copy-done, ...), kind=kOutput, calls=%fused_computation.14 | convolution fusion | flops 1213562496 | bytes 7670784 | tf_op jit(solution)/shard_map/dot_general | solution.py:207
  47.9 0.7 all_to_all.10
  48.6 3.2 %all-to-all-start.1 = ((f32[4,1,96]{2,1,0:T(1,128)}), f32[4,1,96]{2,1,0:T(1,128)S(1)}, u32[]{:S(2)}, u32[]{:S(2)}) async-start(f32[4,1,96]{2,1,0:T(1,128)} %all_to_all.10), calls=%async_computation.2 | async-start | bytes 4096 | tf_op jit(solution)/shard_map/all_to_all | solution.py:216
  51.8 4.5 %all-to-all-done.1 = f32[4,1,96]{2,1,0:T(1,128)S(1)} async-done(((f32[4,1,96]{2,1,0:T(1,128)}), f32[4,1,96]{2,1,0:T(1,128)S(1)}, u32[]{:S(2)}, u32[]{:S(2)}) %all-to-all-start.1) | async-done | bytes 1568 | tf_op jit(solution)/shard_map/all_to_all | solution.py:216
  56.3 0.5 broadcast.14
  56.9 0.7 reduce.5
  57.5 0.1 reshape.40
  57.6 2.5 %gather_fusion = f32[256]{0:T(256)} fusion(f32[384]{0:T(512)S(1)} %reshape.40, s32[1024]{0:T(1024)S(1)} %pad_clamp_fusion), kind=kCustom, calls=%fused_computation | custom fusion | bytes 3072 | tf_op jit(solution)/shard_map/gather | solution.py:219
  60.1 22.1 %reduce-scatter.2.cloned.1.call-done = bf16[96,2048]{1,0:T(8,128)(2,1)} async-done(((bf16[768,2048]{1,0:T(8,128)(2,1)}), bf16[96,2048]{1,0:T(8,128)(2,1)}) %reduce-scatter.2.cloned.1.call-update) | async-done | bytes 393232 | tf_op jit(solution)/shard_map/reduce_scatter | solution.py:200
  82.2 1.9 %bitcast_convert_fusion = f32[1,96,2048]{2,1,0:T(8,128)} fusion(bf16[96,2048]{1,0:T(8,128)(2,1)} %reduce-scatter.2.cloned.1.call-done), kind=kLoop, calls=%fused_computation.16 | loop fusion | flops 196608 | bytes 1179648 | tf_op jit(solution)/shard_map/broadcast_in_dim | solution.py:221
  (2 shorter events, 0.0 us)
Async XLA Ops:
  7.2 35.9 %copy-start = (bf16[1,768,2048]{2,1,0:T(8,128)(2,1)S(1)}, bf16[1,768,2048]{2,1,0:T(8,128)(2,1)}, u32[]{:S(2)}) copy-start(bf16[1,768,2048]{2,1,0:T(8,128)(2,1)} %param.11) | copy-start | bytes 9437188
  10.3 26.2 %all-to-all-start = ((bf16[4,96,2176]{2,1,0:T(8,128)(2,1)}), bf16[4,96,2176]{2,1,0:T(8,128)(2,1)}, u32[]{:S(2)}, u32[]{:S(2)}) async-start(bf16[4,96,2176]{2,1,0:T(8,128)(2,1)} %bitcast.24), calls=%async_computation | async-start | bytes 3342336 | tf_op jit(solution)/shard_map/all_to_all | solution.py:185
  15.5 66.8 %reduce-scatter.2.cloned.1.call-start = ((), (), s32[]{:S(2)}) async-start(), calls=%async_computation.3 | async-start | bytes 3538944 | tf_op jit(solution)/shard_map/reduce_scatter | solution.py:200
  41.2 0.7 copy-start.1
  48.6 7.8 %all-to-all-start.1 = ((f32[4,1,96]{2,1,0:T(1,128)}), f32[4,1,96]{2,1,0:T(1,128)S(1)}, u32[]{:S(2)}, u32[]{:S(2)}) async-start(f32[4,1,96]{2,1,0:T(1,128)} %all_to_all.10), calls=%async_computation.2 | async-start | bytes 4096 | tf_op jit(solution)/shard_map/all_to_all | solution.py:216
Sparse Core Ops, SparseCore 0:
  41.3 40.8 reduce-scatter.1

commit v17 on v13

--- a/solution.py
+++ b/solution.py
@@ -172,6 +172,23 @@
     )(arrived, hidden_t)
 
 
+def widen_kernel(narrow_ref, wide_ref):
+    wide_ref[...] = narrow_ref[...].astype(jnp.float32)
+
+
+def widen(narrow):
+    vmem = pl.BlockSpec(memory_space=pltpu.VMEM)
+    return pl.pallas_call(
+        widen_kernel,
+        out_shape=jax.ShapeDtypeStruct(narrow.shape, jnp.float32),
+        in_specs=[vmem],
+        out_specs=vmem,
+        cost_estimate=pl.CostEstimate(
+            flops=narrow.size, bytes_accessed=6 * narrow.size, transcendentals=0
+        ),
+    )(narrow)
+
+
 def local(out_grad, combine_weight, routes, saved_gate, saved_up, w_down):
     experts = lax.axis_size("expert")
     tok_rows, route_count = routes.shape
@@ -201,7 +218,7 @@
     gate_pre = gate_bf.astype(jnp.float32)
     up_pre = up_bf.astype(jnp.float32)
     sigmoid_gate = jax.nn.sigmoid(gate_pre)
-    grad_weight = summed.astype(jnp.float32)
+    grad_weight = widen(summed)
 
     matrix = w_down[0]
     back = lax.dot_general(

time: 91.4 us -> 91.4 us (level)
  other arithmetic: 3.79 us -> 1.84 us
  Pallas kernels: 10.5 us -> 12.4 us
    broadcast_in_dim x1 -> x0, other arithmetic: 1.94 us -> none  [local(): grad_weight[None]]
    pallas_call x0 -> x1, Pallas kernels: none -> 1.93 us  [widen(): pl.pallas_call(widen_kernel, out_shape=jax.ShapeDtypeStruct(narrow.shape,...]
where the time goes in v17:
time: 91.4 us; the launch traced here: 91 us
  waiting for transfers between devices  45 us (49%)
  between operations  14.1 us (15%)
  Pallas kernels  12.4 us (14%)
  starting transfers between devices  8.39 us (9%)
  matrix products  4.86 us (5%)
  local copies, waits for them, and re-layouts  4.42 us (5%)
  other arithmetic  1.84 us (2%)
    reduce_scatter x1, waiting for transfers between devices, local(): lax.psum_scatter(partial_grad, 'dp', scatter_dimension=0, tiled=True)  22.1 us
    all_to_all x1, waiting for transfers between devices, local(): lax.all_to_all(packed.reshape(experts, capacity, feature_count + lanes),...  18.3 us
    all_to_all x1, starting transfers between devices, local(): lax.all_to_all(packed.reshape(experts, capacity, feature_count + lanes),...  5.16 us
    dot_general x1, matrix products, local(): lax.dot_general(rows, matrix, (((1,), (1,)), ((), ())), preferred_element...  4.86 us
    pallas_call x1, Pallas kernels, weighted_partial(): pl.pallas_call(functools.partial(partial_kernel, tile=tile), out_shape=ja...  4.6 us
    all_to_all x1, waiting for transfers between devices, local(): lax.all_to_all(slot_grad.reshape(experts, capacity), 'expert', split_axis...  4.52 us
    all_to_all x1, starting transfers between devices, local(): lax.all_to_all(slot_grad.reshape(experts, capacity), 'expert', split_axis...  3.22 us
    pallas_call x1, Pallas kernels, pack_slots(): pl.pallas_call(functools.partial(front_kernel, experts=experts, capacity=...  3.14 us
  transfers between devices with their start and end apart: 3, of which 3 were waited for; matrix products, arithmetic and copies ran while one was open for 11% of the time, Pallas kernels for 3%

profile of v17, /device:TPU:0, one launch (start us, length us, event | category | flops | bytes accessed | tf_op | source)
XLA Modules:
  0.0 91.0 jit_solution(13282426257092719376)
XLA Ops:
  7.2 0.0 copy-start
  7.2 3.1 %shard_map.93 = (bf16[384,2176]{1,0:T(8,128)(2,1)}, s32[2,128]{1,0:T(2,128)}) custom-call(s32[2,128]{1,0:T(2,128)} %bitcast.27, f32[2,128]{1,0:T(2,128)} %bitcast.28, bf16[128,2048]{1,0:T(8,128)(2,1)} %rows_ref.1), custom_call_target="tpu_custom_call" | custom-call | flops 201326592 | bytes 2097152 | tf_op jit(solution)/shard_map/pallas_call | solution.py:71
  10.3 5.2 %all-to-all-start = ((bf16[4,96,2176]{2,1,0:T(8,128)(2,1)}), bf16[4,96,2176]{2,1,0:T(8,128)(2,1)}, u32[]{:S(2)}, u32[]{:S(2)}) async-start(bf16[4,96,2176]{2,1,0:T(8,128)(2,1)} %bitcast.22), calls=%async_computation | async-start | bytes 3342336 | tf_op jit(solution)/shard_map/all_to_all | solution.py:202
  15.5 0.0 reduce-scatter.2.cloned.1.call-start
  15.5 2.7 %shard_map.94 = (bf16[384,768]{1,0:T(8,128)(2,1)}, bf16[768,384]{1,0:T(8,128)(2,1)}) custom-call(bf16[384,768]{1,0:T(8,128)(2,1)} %bitcast.24, bf16[384,768]{1,0:T(8,128)(2,1)} %bitcast.25), custom_call_target="tpu_custom_call" | custom-call | flops 2359296 | bytes 2359296 | tf_op jit(solution)/shard_map/pallas_call | solution.py:97
  18.2 18.3 %all-to-all-done = bf16[4,96,2176]{2,1,0:T(8,128)(2,1)} async-done(((bf16[4,96,2176]{2,1,0:T(8,128)(2,1)}), bf16[4,96,2176]{2,1,0:T(8,128)(2,1)}, u32[]{:S(2)}, u32[]{:S(2)}) %all-to-all-start) | async-done | bytes 1671200 | tf_op jit(solution)/shard_map/all_to_all | solution.py:202
  36.6 4.6 %shard_map.95 = bf16[768,2048]{1,0:T(8,128)(2,1)} custom-call(bf16[384,2176]{1,0:T(8,128)(2,1)} %bitcast.3.arrived_hbm, bf16[768,384]{1,0:T(8,128)(2,1)} %get-tuple-element.9.hidden_t_hbm), custom_call_target="tpu_custom_call" | custom-call | flops 1207959552 | bytes 5406720 | tf_op jit(solution)/shard_map/pallas_call | solution.py:158
  41.2 0.0 copy-start.1
  41.2 0.0 reduce-scatter.2.cloned.1.call-update
  41.2 0.6 copy-done.1
  41.8 0.9 slice_convert_fusion
  42.8 0.3 fusion.11
  43.0 0.0 copy-done
  43.0 4.9 %fusion.10 = (bf16[384,768]{1,0:T(8,128)(2,1)}, bf16[384,768]{1,0:T(8,128)(2,1)}, f32[384]{0:T(512)S(1)}) fusion(f32[384]{0:T(512)S(1)} %fusion.11, bf16[1,1,4,96,768]{4,3,2,1,0:T(8,128)(2,1)} %param.9, bf16[1,1,4,96,768]{4,3,2,1,0:T(8,128)(2,1)} %param.10, bf16[384,768]{1,0:T(8,128)(2,1)} %get-tuple-element.10, bf16[1,768,2048]{2,1,0:T(8,128)(2,1)S(1)} %copy-done, ...), kind=kOutput, calls=%fused_computation.14 | convolution fusion | flops 1213562496 | bytes 7670784 | tf_op jit(solution)/shard_map/dot_general | solution.py:224
  47.9 0.7 all_to_all.10
  48.5 3.2 %all-to-all-start.1 = ((f32[4,1,96]{2,1,0:T(1,128)}), f32[4,1,96]{2,1,0:T(1,128)S(1)}, u32[]{:S(2)}, u32[]{:S(2)}) async-start(f32[4,1,96]{2,1,0:T(1,128)} %all_to_all.10), calls=%async_computation.2 | async-start | bytes 4096 | tf_op jit(solution)/shard_map/all_to_all | solution.py:233
  51.8 4.5 %all-to-all-done.1 = f32[4,1,96]{2,1,0:T(1,128)S(1)} async-done(((f32[4,1,96]{2,1,0:T(1,128)}), f32[4,1,96]{2,1,0:T(1,128)S(1)}, u32[]{:S(2)}, u32[]{:S(2)}) %all-to-all-start.1) | async-done | bytes 1568 | tf_op jit(solution)/shard_map/all_to_all | solution.py:233
  56.3 0.5 broadcast.14
  56.8 0.7 reduce.5
  57.5 0.1 reshape.40
  57.6 2.5 %gather_fusion = f32[256]{0:T(256)} fusion(f32[384]{0:T(512)S(1)} %reshape.40, s32[1024]{0:T(1024)S(1)} %pad_clamp_fusion), kind=kCustom, calls=%fused_computation | custom fusion | bytes 3072 | tf_op jit(solution)/shard_map/gather | solution.py:236
  60.1 22.1 %reduce-scatter.2.cloned.1.call-done.narrow_ref = bf16[96,2048]{1,0:T(8,128)(2,1)} async-done(((bf16[768,2048]{1,0:T(8,128)(2,1)}), bf16[96,2048]{1,0:T(8,128)(2,1)}) %reduce-scatter.2.cloned.1.call-update) | async-done | bytes 393232 | tf_op jit(solution)/shard_map/reduce_scatter | solution.py:217
  82.2 1.9 %shard_map.96 = f32[96,2048]{1,0:T(8,128)} custom-call(bf16[96,2048]{1,0:T(8,128)(2,1)} %reduce-scatter.2.cloned.1.call-done.narrow_ref), custom_call_target="tpu_custom_call" | custom-call | flops 196608 | bytes 1179648 | tf_op jit(solution)/shard_map/pallas_call | solution.py:181
  (2 shorter events, 0.0 us)
Async XLA Ops:
  7.2 35.9 %copy-start = (bf16[1,768,2048]{2,1,0:T(8,128)(2,1)S(1)}, bf16[1,768,2048]{2,1,0:T(8,128)(2,1)}, u32[]{:S(2)}) copy-start(bf16[1,768,2048]{2,1,0:T(8,128)(2,1)} %param.11) | copy-start | bytes 9437188
  10.3 26.2 %all-to-all-start = ((bf16[4,96,2176]{2,1,0:T(8,128)(2,1)}), bf16[4,96,2176]{2,1,0:T(8,128)(2,1)}, u32[]{:S(2)}, u32[]{:S(2)}) async-start(bf16[4,96,2176]{2,1,0:T(8,128)(2,1)} %bitcast.22), calls=%async_computation | async-start | bytes 3342336 | tf_op jit(solution)/shard_map/all_to_all | solution.py:202
  15.5 66.7 %reduce-scatter.2.cloned.1.call-start = ((), (), s32[]{:S(2)}) async-start(), calls=%async_computation.3 | async-start | bytes 3538944 | tf_op jit(solution)/shard_map/reduce_scatter | solution.py:217
  41.2 0.7 copy-start.1
  48.5 7.8 %all-to-all-start.1 = ((f32[4,1,96]{2,1,0:T(1,128)}), f32[4,1,96]{2,1,0:T(1,128)S(1)}, u32[]{:S(2)}, u32[]{:S(2)}) async-start(f32[4,1,96]{2,1,0:T(1,128)} %all_to_all.10), calls=%async_computation.2 | async-start | bytes 4096 | tf_op jit(solution)/shard_map/all_to_all | solution.py:233
Sparse Core Ops, SparseCore 0:
  41.3 40.8 reduce-scatter.1
